TPU v7x, 32 devices: a whole 2x2x4 slice. The times are simulated.
32 devices in a mesh: group: 1, ctx: 16 (over z, y, x), head: 2 (over core).
Axes of the slice: x: 2, y: 2, z: 4, core: 2. Of those that a mesh axis runs over, the one named last changes fastest.
Arguments:
- pair_raw: bfloat16 [4096, 2, 1024], P(('group', 'ctx'), None, 'head'), may hold values from -6 to 6
- value_raw: bfloat16 [4096, 2048], P(('group', 'ctx'), 'head'), may hold values from -6 to 6
- gate_raw: bfloat16 [4096, 2048], P(('group', 'ctx'), 'head'), may hold values from -6 to 6
- write_strength: float32 [4096, 16], P(('group', 'ctx'), 'head'), may hold values from 0.05 to 0.95
- log_decay: float32 [4096, 16], P(('group', 'ctx'), 'head'), may hold values from -2.6 to 0
- segment_ids: int32 [4096], P('group'), may hold values from 0 to 1, never falling along the last dimension, each value on 1 to 3968 neighbouring positions
- pair_filter: float32 [4, 2, 1024], P(None, None, 'head'), may hold values from -3 to 3
- value_filter: float32 [4, 2048], P(None, 'head'), may hold values from -3 to 3
- norm_gain: float32 [128], replicated, may hold values from 0.1 to 1.9
- out_weight: bfloat16 [2048, 2048], P('head'), may hold values from -0.125 to 0.125
- residual: bfloat16 [4096, 2048], P(('group', 'ctx', 'head')), may hold values from -27 to 27
- post_gain: float32 [2048], replicated, may hold values from 0.1 to 1.9
- routes: int32 [4096, 10], P(('group', 'ctx', 'head')), may hold values from 0 to 31, all different within a row; in each aligned block of 128 rows (0 to 127, 128 to 255, ...) at most 50 rows name the same one
- route_weights: float32 [4096, 10], P(('group', 'ctx', 'head')), may hold values from 0.05 to 0.3
- expert_up: bfloat16 [32, 2048, 1024], P(('ctx', 'head')), may hold values from -0.125 to 0.125
- expert_down: bfloat16 [32, 512, 2048], P(('ctx', 'head')), may hold values from -0.25 to 0.25
Outputs:
- layer_out: bfloat16 [4096, 2048], P(('group', 'ctx', 'head'))
Inputs may be any that keep to these rules, and one draw needn't show every extreme that they name: `routes`: in each aligned block of 128 rows (the rows of one device) no expert is named by more than 50 rows; a row names 10 different experts. `segment_ids`: rollout numbers never fall along the slab; a rollout holds 1 to 3968 tokens of the slab.
All inputs are finite; a program needn't handle non-finite values.
Results may differ from a plain program's by a relative error of at most 0.012.
Values may be sent and summed in bfloat16 or wider, within the bound.
No kernel may reach another device: no remote copies, remote signals or barrier semaphores. Data moves between devices by JAX's collectives and lax.ppermute only.
A program may use at most 128 MiB of HBM per device.

v0:
```python
import jax
import jax.numpy as jnp
from jax import lax
from jax.sharding import Mesh, PartitionSpec as P

D = 2048
DK = 128
DV = 128
BLOCK = 64
CTX = ("ctx_hi", "ctx_lo")


HIGHEST = lax.Precision.HIGHEST


def passed_along(block, axis, distance):
    devices = range(lax.axis_size(axis))
    route = [(i - distance, i) for i in devices if i - distance in devices]
    return lax.ppermute(block, axis, route)


def scanned_entry(whole_map, whole_shift, axis):
    peers, position = (lax.axis_size(axis), lax.axis_index(axis))
    distance = 1
    while distance < peers:
        last = 2 * distance >= peers
        reached = position >= distance
        if last:
            shift_in = passed_along(whole_shift.astype(jnp.bfloat16), axis, distance)
            shift_in = shift_in.astype(jnp.float32)
        else:
            both = jnp.stack([whole_map, whole_shift]).astype(jnp.bfloat16)
            both_in = passed_along(both, axis, distance).astype(jnp.float32)
            map_in, shift_in = (both_in[0], both_in[1])
        new_shift = batched(whole_map, shift_in) + whole_shift
        if not last:
            whole_map = jnp.where(reached, batched(whole_map, map_in), whole_map)
        whole_shift = jnp.where(reached, new_shift, whole_shift)
        distance *= 2
    return passed_along(whole_shift.astype(jnp.bfloat16), axis, 1).astype(jnp.float32)


def precise_dot(left, right):
    return jnp.dot(left, right, precision=HIGHEST, preferred_element_type=jnp.float32)


def causal_filter(padded_raw, filter_taps, padded_ids, kernel):
    length = padded_raw.shape[0] - (kernel - 1)
    source = padded_raw.astype(jnp.float32)
    current_ids = padded_ids[kernel - 1 :]
    summed = jnp.zeros((length, padded_raw.shape[1]), jnp.float32)
    for lag_step in range(kernel):
        offset_start = kernel - 1 - lag_step
        shifted = source[offset_start : offset_start + length]
        matching = (padded_ids[offset_start : offset_start + length] == current_ids).astype(
            jnp.float32
        )
        summed = summed + filter_taps[lag_step] * shifted * matching[:, None]
    return jax.nn.silu(summed)


def unit_rows(values_in):
    return values_in / jnp.sqrt(jnp.sum(values_in * values_in, axis=-1, keepdims=True) + 1e-06)


def mixer_inputs(pair_padded, value_padded, pair_filter, value_filter, padded_ids, kernel):
    pair_act = causal_filter(pair_padded, pair_filter.reshape(kernel, -1), padded_ids, kernel)
    length = pair_act.shape[0]
    pair_heads = pair_act.reshape(length, 2, -1, DK)
    queries = unit_rows(pair_heads[:, 0]) * DK ** (-0.5)
    key_rows = unit_rows(pair_heads[:, 1])
    value_rows = causal_filter(value_padded, value_filter, padded_ids, kernel).reshape(
        length, -1, DV
    )
    repeat_factor = value_rows.shape[1] // key_rows.shape[1]
    return (
        jnp.repeat(queries, repeat_factor, axis=1),
        jnp.repeat(key_rows, repeat_factor, axis=1),
        value_rows,
    )


def unit_lower_inverse(system):
    size = system.shape[-1]
    row_index = lax.broadcasted_iota(jnp.int32, (size, size), 0)
    col_index = lax.broadcasted_iota(jnp.int32, (size, size), 1)
    inverse = jnp.broadcast_to(jnp.eye(size, dtype=system.dtype), system.shape)
    width = 1
    while width < size:
        linking = (
            (row_index // (2 * width) == col_index // (2 * width))
            & ((row_index // width) % 2 == 1)
            & ((col_index // width) % 2 == 0)
        )
        lower_left = jnp.where(linking, system, 0.0)
        inverse = inverse - precise_dot(inverse, precise_dot(lower_left, inverse))
        width *= 2
    return inverse


def block_setup(queries, key_rows, value_rows, strength, decay_rows, segment_here, prior_id):
    cumulative = jnp.cumsum(decay_rows)
    row_index = lax.broadcasted_iota(jnp.int32, (BLOCK, BLOCK), 0)
    col_index = lax.broadcasted_iota(jnp.int32, (BLOCK, BLOCK), 1)
    same_segment = segment_here[:, None] == segment_here[None, :]
    causal = (row_index >= col_index) & same_segment
    strictly = (row_index > col_index) & same_segment
    decay_matrix = jnp.where(
        causal, jnp.exp(jnp.where(causal, cumulative[:, None] - cumulative[None, :], 0.0)), 0.0
    )
    carried_in = (segment_here == prior_id).astype(jnp.float32)
    keyed_beta = key_rows * strength[:, None]
    coupling = jnp.where(strictly, precise_dot(keyed_beta, key_rows.T) * decay_matrix, 0.0)
    system = jnp.eye(BLOCK, dtype=jnp.float32) + coupling
    stacked = jnp.concatenate(
        [value_rows * strength[:, None], keyed_beta * (jnp.exp(cumulative) * carried_in)[:, None]],
        axis=1,
    )
    solved = precise_dot(unit_lower_inverse(system), stacked)
    targets = solved[:, :DV]
    corrector = solved[:, DV:]
    within = jnp.where(causal, precise_dot(queries, key_rows.T) * decay_matrix, 0.0)
    query_decayed = queries * (jnp.exp(cumulative) * carried_in)[:, None]
    final_log = cumulative[BLOCK - 1]
    weighting = (segment_here == segment_here[BLOCK - 1]).astype(jnp.float32) * jnp.exp(
        final_log - cumulative
    )
    keys_weighted = key_rows * weighting[:, None]
    transition = jnp.exp(final_log) * carried_in[BLOCK - 1] * jnp.eye(
        DK, dtype=jnp.float32
    ) - precise_dot(keys_weighted.T, corrector)
    increment = precise_dot(keys_weighted.T, targets)
    return (within, query_decayed, targets, corrector, transition, increment)


def head_major(array_in, block_count):
    moved = jnp.moveaxis(array_in, 1, 0)
    return moved.reshape((array_in.shape[1], block_count, BLOCK) + array_in.shape[2:])


def block_tables(queries, key_rows, value_rows, strength, decay_rows, padded_ids, kernel):
    length = queries.shape[0]
    block_count = length // BLOCK
    current_ids = padded_ids[kernel - 1 :].reshape(block_count, BLOCK)
    prior_ids = padded_ids[kernel - 2 : kernel - 2 + length : BLOCK]
    per_block = jax.vmap(block_setup, in_axes=(0, 0, 0, 0, 0, 0, 0))
    per_head = jax.vmap(per_block, in_axes=(0, 0, 0, 0, 0, None, None))
    return per_head(
        head_major(queries, block_count),
        head_major(key_rows, block_count),
        head_major(value_rows, block_count),
        head_major(strength, block_count),
        head_major(decay_rows, block_count),
        current_ids,
        prior_ids,
    )


def blockwise(left, right):
    return jnp.einsum("hbij,hbjk->hbik", left, right, precision=HIGHEST)


def batched(left, right):
    return jnp.einsum("hij,hjk->hik", left, right, precision=HIGHEST)


def sweep_blocks(block_terms, start_state):
    blocks_first = tuple((jnp.swapaxes(member, 0, 1) for member in block_terms))

    def advance(carry_state, pieces):
        within, query_decayed, targets, corrector, transition, increment = pieces
        fresh_values = targets - batched(corrector, carry_state)
        emitted = batched(query_decayed, carry_state) + batched(within, fresh_values)
        updated = batched(transition, carry_state) + increment
        return (updated, emitted)

    final_state, emitted = lax.scan(advance, start_state, blocks_first)
    return emitted


def tokens_first(emitted):
    heads_count = emitted.shape[1]
    return jnp.transpose(emitted, (0, 2, 1, 3)).reshape(-1, heads_count, emitted.shape[3])


def gate_output(mixed_heads, gate_raw, norm_gain):
    square_mean = jnp.mean(mixed_heads * mixed_heads, axis=-1, keepdims=True)
    gate_values = jax.nn.silu(gate_raw.reshape(mixed_heads.shape).astype(jnp.float32))
    normed = mixed_heads / jnp.sqrt(square_mean + 1e-06) * norm_gain * gate_values
    return normed.astype(jnp.bfloat16).reshape(mixed_heads.shape[0], -1)


def post_norm(hidden, post_gain):
    hidden_full = hidden.astype(jnp.float32)
    square_mean = jnp.mean(hidden_full * hidden_full, axis=-1, keepdims=True)
    return (hidden_full / jnp.sqrt(square_mean + 1e-06) * post_gain).astype(jnp.bfloat16)


def expert_apply_rows(rows_in, up_matrix, down_matrix):
    hidden_units = down_matrix.shape[0]
    gate_up = jnp.dot(rows_in, up_matrix, preferred_element_type=jnp.float32)
    activated = (jax.nn.silu(gate_up[:, :hidden_units]) * gate_up[:, hidden_units:]).astype(
        jnp.bfloat16
    )
    return jnp.dot(activated, down_matrix, preferred_element_type=jnp.float32).astype(jnp.bfloat16)


def expert_apply(arrived, expert_up, expert_down):
    member_rows = arrived[:, 0]
    flattened = member_rows.reshape(-1, member_rows.shape[-1])
    result = expert_apply_rows(flattened, expert_up[0], expert_down[0])
    outputs = [result.reshape(member_rows.shape)]
    return jnp.stack(outputs, axis=1)


def route_slots(routes, experts_all, capacity):
    assigned = routes.reshape(-1)
    expert_ids = jnp.arange(experts_all, dtype=jnp.int32)
    onehot = (assigned[:, None] == expert_ids[None, :]).astype(jnp.int32)
    slot_rank = jnp.sum((jnp.cumsum(onehot, axis=0) - 1) * onehot, axis=1)
    return assigned * capacity + slot_rank


def per_device(
    pair_raw,
    value_raw,
    gate_raw,
    write_strength,
    log_decay,
    segment_ids,
    pair_filter,
    value_filter,
    norm_gain,
    out_weight,
    residual,
    post_gain,
    routes,
    route_weights,
    expert_up,
    expert_down,
):
    local_tokens = pair_raw.shape[0]
    kernel = value_filter.shape[0]
    pair_flat = pair_raw.reshape(local_tokens, -1)
    pair_width = pair_flat.shape[1]
    rim_rows = jnp.concatenate(
        [pair_flat[local_tokens - (kernel - 1) :], value_raw[local_tokens - (kernel - 1) :]], axis=1
    )
    before = passed_along(rim_rows, CTX, 1)
    first_token = lax.axis_index(CTX) * local_tokens
    padded_ids = jnp.concatenate([jnp.full((kernel - 1,), -1, jnp.int32), segment_ids])
    window_ids = lax.dynamic_slice_in_dim(padded_ids, first_token, local_tokens + kernel - 1)
    pair_padded = jnp.concatenate([before[:, :pair_width], pair_flat])
    value_padded = jnp.concatenate([before[:, pair_width:], value_raw])
    queries, key_rows, value_rows = mixer_inputs(
        pair_padded, value_padded, pair_filter, value_filter, window_ids, kernel
    )
    block_terms = block_tables(
        queries, key_rows, value_rows, write_strength, log_decay, window_ids, kernel
    )
    within, query_decayed, targets, corrector, transition, increment = block_terms
    heads_here, block_count = transition.shape[:2]
    prefix_map = jnp.broadcast_to(jnp.eye(DK, dtype=jnp.float32), (heads_here, DK, DK))
    prefix_shift = jnp.zeros((heads_here, DK, DV), jnp.float32)
    prefix_maps, prefix_shifts = ([], [])
    for block in range(block_count):
        prefix_maps.append(prefix_map)
        prefix_shifts.append(prefix_shift)
        prefix_map = batched(transition[:, block], prefix_map)
        prefix_shift = batched(transition[:, block], prefix_shift) + increment[:, block]
    stacked_maps = jnp.stack(prefix_maps, axis=1)
    stacked_shifts = jnp.stack(prefix_shifts, axis=1)
    query_effective = query_decayed - blockwise(within, corrector)
    through_entry = blockwise(query_effective, stacked_maps)
    fixed_part = blockwise(query_effective, stacked_shifts) + blockwise(within, targets)
    entering = scanned_entry(prefix_map, prefix_shift, CTX)
    emitted = (
        jnp.einsum("hbtk,hkv->hbtv", through_entry, entering, precision=HIGHEST) + fixed_part
    )
    mixed_heads = jnp.transpose(emitted, (1, 2, 0, 3)).reshape(-1, heads_here, DV)
    gated_out = gate_output(mixed_heads, gate_raw, norm_gain)
    partial_out = jnp.dot(gated_out, out_weight, preferred_element_type=jnp.float32)
    pairs = lax.axis_size("head")
    if pairs == 2:
        side = lax.axis_index("head")
        halves = partial_out.reshape(2, -1, partial_out.shape[1])
        kept = lax.dynamic_index_in_dim(halves, side, keepdims=False)
        given = lax.dynamic_index_in_dim(halves, 1 - side, keepdims=False)
        attention = kept + lax.ppermute(
            given.astype(jnp.bfloat16), "head", [(0, 1), (1, 0)]
        ).astype(jnp.float32)
    else:
        attention = lax.psum_scatter(
            partial_out.astype(jnp.bfloat16), "head", scatter_dimension=0, tiled=True
        ).astype(jnp.float32)
    hidden = (residual.astype(jnp.float32) + attention).astype(jnp.bfloat16)
    expert_in = post_norm(hidden, post_gain)
    levels = lax.axis_size("ctx_hi")
    level = lax.axis_index("ctx_hi")
    local_experts = expert_up.shape[0]
    per_level = lax.axis_size("ctx_lo") * lax.axis_size("head") * local_experts
    experts_all = levels * per_level
    local_rows = routes.shape[0]
    top_count = routes.shape[1]
    capacity = local_rows * top_count * 5 // (4 * experts_all)
    own_high = route_weights.astype(jnp.bfloat16)
    own_low = (route_weights - own_high.astype(jnp.float32)).astype(jnp.bfloat16)
    spare = -(-(3 * top_count) // 128) * 128 - 3 * top_count
    packed = jnp.concatenate(
        [
            expert_in,
            routes.astype(jnp.bfloat16),
            own_high,
            own_low,
            jnp.zeros((local_rows, spare), jnp.bfloat16),
        ],
        axis=1,
    )
    expert_ids = jnp.arange(experts_all, dtype=jnp.int32)
    earlier_rows = (
        lax.broadcasted_iota(jnp.int32, (local_rows, local_rows), 0)
        > lax.broadcasted_iota(jnp.int32, (local_rows, local_rows), 1)
    ).astype(jnp.bfloat16)
    slots_total = per_level * capacity
    slot_ids = jnp.arange(slots_total, dtype=jnp.int32)
    level_axes = ("ctx_lo", "head")
    routed = None
    for turn in range(levels):
        if turn == 0:
            chunk = packed
        else:
            chunk = lax.ppermute(
                packed, "ctx_hi", [(i, (i - turn) % levels) for i in range(levels)]
            )
        chunk_in = chunk[:, :D]
        chunk_routes = chunk[:, D : D + top_count].astype(jnp.int32)
        chunk_high = chunk[:, D + top_count : D + 2 * top_count]
        chunk_low = chunk[:, D + 2 * top_count : D + 3 * top_count]
        route_hot = chunk_routes[:, :, None] == expert_ids[None, None, :]
        row_hot = jnp.any(route_hot, axis=1).astype(jnp.bfloat16)
        earlier = jnp.dot(earlier_rows, row_hot, preferred_element_type=jnp.float32)
        slot_rank = jnp.sum(jnp.where(route_hot, earlier[:, None, :], 0.0), axis=2).astype(
            jnp.int32
        )
        slot_index = jnp.where(
            chunk_routes // per_level == level,
            (chunk_routes % per_level) * capacity + slot_rank,
            -1,
        )
        hits = slot_index[:, :, None] == slot_ids[None, None, :]
        picker = jnp.any(hits, axis=1).astype(jnp.bfloat16)
        outgoing = lax.dot_general(
            picker, chunk_in, (((0,), (0,)), ((), ())), preferred_element_type=jnp.float32
        ).astype(jnp.bfloat16)
        outgoing = outgoing.reshape(per_level // local_experts, local_experts * capacity, D)
        arrived = lax.all_to_all(outgoing, level_axes, split_axis=0, concat_axis=0, tiled=True)
        arrived = arrived.reshape(per_level // local_experts, local_experts, capacity, D)
        answered = jnp.stack(
            [
                expert_apply_rows(
                    arrived[:, member].reshape(-1, D), expert_up[member], expert_down[member]
                ).reshape(arrived.shape[0], capacity, D)
                for member in range(local_experts)
            ],
            axis=1,
        ).reshape(per_level // local_experts, local_experts * capacity, D)
        returned = lax.all_to_all(answered, level_axes, split_axis=0, concat_axis=0, tiled=True)
        result_rows = returned.reshape(slots_total, D)
        weight_high = jnp.sum(jnp.where(hits, chunk_high[:, :, None], 0.0), axis=1).astype(
            jnp.bfloat16
        )
        weight_low = jnp.sum(jnp.where(hits, chunk_low[:, :, None], 0.0), axis=1).astype(
            jnp.bfloat16
        )
        partial = jnp.dot(weight_high, result_rows, preferred_element_type=jnp.float32) + jnp.dot(
            weight_low, result_rows, preferred_element_type=jnp.float32
        )
        if turn == 0:
            routed = partial
        else:
            routed = routed + lax.ppermute(
                partial.astype(jnp.bfloat16),
                "ctx_hi",
                [(i, (i + turn) % levels) for i in range(levels)],
            ).astype(jnp.float32)
    combined = hidden.astype(jnp.float32) + routed
    return combined.astype(jnp.bfloat16)


def split_mesh(mesh):
    groups, peers, pairs = (mesh.shape["group"], mesh.shape["ctx"], mesh.shape["head"])
    low = 4 if peers % 4 == 0 else 1
    devices = mesh.devices.reshape(groups, peers // low, low, pairs)
    return Mesh(devices, ("group", "ctx_hi", "ctx_lo", "head"))


def solution(mesh):
    return jax.shard_map(
        per_device,
        mesh=split_mesh(mesh),
        in_specs=(
            P(("group", "ctx_hi", "ctx_lo"), None, "head"),
            P(("group", "ctx_hi", "ctx_lo"), "head"),
            P(("group", "ctx_hi", "ctx_lo"), "head"),
            P(("group", "ctx_hi", "ctx_lo"), "head"),
            P(("group", "ctx_hi", "ctx_lo"), "head"),
            P("group"),
            P(None, None, "head"),
            P(None, "head"),
            P(),
            P("head", None),
            P(("group", "ctx_hi", "ctx_lo", "head"), None),
            P(),
            P(("group", "ctx_hi", "ctx_lo", "head"), None),
            P(("group", "ctx_hi", "ctx_lo", "head"), None),
            P(("ctx_hi", "ctx_lo", "head"), None, None),
            P(("ctx_hi", "ctx_lo", "head"), None, None),
        ),
        out_specs=P(("group", "ctx_hi", "ctx_lo", "head"), None),
        check_vma=False,
    )
```

profile of v0, /device:TPU:0, one launch (start us, length us, event | category | flops | bytes accessed | tf_op | source)
XLA Modules:
  0.0 393.9 jit_solution(4042023442825659182)
XLA Ops:
  1.6 4.8 %collective-permute-start = (bf16[3,2048]{1,0:T(4,128)(2,1)S(1)}, bf16[3,2048]{1,0:T(4,128)(2,1)S(1)}, u32[]{:S(2)}, u32[]{:S(2)}) collective-permute-start(bf16[3,2048]{1,0:T(4,128)(2,1)S(1)} %pad_maximum_fusion.5), channel_id=1, source_target_pairs={{0,2},{2,4},{4,6},{6,8},{8,10},{10,12},{12,14},{14,16},{16,18},{18... | collective-permute-start | bytes 36872 | tf_op jit(solution)/shard_map/ppermute | solution.py:19
  14.5 2.9 multiply_bitcast_fusion
  40.6 3.5 fusion.82
  44.2 3.7 multiply_subtract_fusion
  55.1 4.2 %collective-permute-start.1 = (bf16[2,8,128,128]{3,2,1,0:T(8,128)(2,1)}, bf16[2,8,128,128]{3,2,1,0:T(8,128)(2,1)}, u32[]{:S(2)}, u32[]{:S(2)}) collective-permute-start(bf16[2,8,128,128]{3,2,1,0:T(8,128)(2,1)} %pad_maximum_fusion.2), channel_id=1, source_target_pairs={{0,2},{2,4},{4,6},{6,8},{8,10},{10,12},{12,14},{14,16},{16,18},{18... | collective-permute-start | bytes 1572872 | tf_op jit(solution)/shard_map/ppermute | solution.py:19
  59.5 10.3 %collective-permute-done.1 = bf16[2,8,128,128]{3,2,1,0:T(8,128)(2,1)} collective-permute-done((bf16[2,8,128,128]{3,2,1,0:T(8,128)(2,1)}, bf16[2,8,128,128]{3,2,1,0:T(8,128)(2,1)}, u32[]{:S(2)}, u32[]{:S(2)}) %collective-permute-start.1) | collective-permute-done | bytes 524320 | tf_op jit(solution)/shard_map/ppermute | solution.py:19
  73.0 5.3 %collective-permute-start.2 = (bf16[2,8,128,128]{3,2,1,0:T(8,128)(2,1)S(1)}, bf16[2,8,128,128]{3,2,1,0:T(8,128)(2,1)S(1)}, u32[]{:S(2)}, u32[]{:S(2)}) collective-permute-start(bf16[2,8,128,128]{3,2,1,0:T(8,128)(2,1)S(1)} %pad_maximum_fusion.3), channel_id=1, source_target_pairs={{0,4},{2,6},{4,8},{6,10},{8,12},{10,14},{12,16},{14,18},{16,20},{1... | collective-permute-start | bytes 1572872 | tf_op jit(solution)/shard_map/ppermute | solution.py:19
  80.3 7.9 %collective-permute-done.2 = bf16[2,8,128,128]{3,2,1,0:T(8,128)(2,1)S(1)} collective-permute-done((bf16[2,8,128,128]{3,2,1,0:T(8,128)(2,1)S(1)}, bf16[2,8,128,128]{3,2,1,0:T(8,128)(2,1)S(1)}, u32[]{:S(2)}, u32[]{:S(2)}) %collective-permute-start.2) | collective-permute-done | bytes 524320 | tf_op jit(solution)/shard_map/ppermute | solution.py:19
  89.2 6.4 %collective-permute-start.3 = (bf16[2,8,128,128]{3,2,1,0:T(8,128)(2,1)S(1)}, bf16[2,8,128,128]{3,2,1,0:T(8,128)(2,1)S(1)}, u32[]{:S(2)}, u32[]{:S(2)}) collective-permute-start(bf16[2,8,128,128]{3,2,1,0:T(8,128)(2,1)S(1)} %pad_maximum_fusion.4), channel_id=1, source_target_pairs={{0,8},{2,10},{4,12},{6,14},{8,16},{10,18},{12,20},{14,22},{16,24},... | collective-permute-start | bytes 1572872 | tf_op jit(solution)/shard_map/ppermute | solution.py:19
  98.2 6.4 %collective-permute-done.3 = bf16[2,8,128,128]{3,2,1,0:T(8,128)(2,1)S(1)} collective-permute-done((bf16[2,8,128,128]{3,2,1,0:T(8,128)(2,1)S(1)}, bf16[2,8,128,128]{3,2,1,0:T(8,128)(2,1)S(1)}, u32[]{:S(2)}, u32[]{:S(2)}) %collective-permute-start.3) | collective-permute-done | bytes 524320 | tf_op jit(solution)/shard_map/ppermute | solution.py:19
  105.0 5.6 %collective-permute-start.4 = (bf16[8,128,128]{2,1,0:T(8,128)(2,1)S(1)}, bf16[8,128,128]{2,1,0:T(8,128)(2,1)S(1)}, u32[]{:S(2)}, u32[]{:S(2)}) collective-permute-start(bf16[8,128,128]{2,1,0:T(8,128)(2,1)S(1)} %get-tuple-element.62), channel_id=1, source_target_pairs={{0,16},{2,18},{4,20},{6,22},{8,24},{10,26},{12,28},{14,30},{1,17},... | collective-permute-start | bytes 786440 | tf_op jit(solution)/shard_map/ppermute | solution.py:19
  116.4 2.1 fusion.23
  131.8 10.7 %collective-permute-start.11 = (bf16[128,2176]{1,0:T(8,128)(2,1)}, bf16[128,2176]{1,0:T(8,128)(2,1)}, u32[]{:S(2)}, u32[]{:S(2)}) collective-permute-start(bf16[128,2176]{1,0:T(8,128)(2,1)} %concatenate.23), channel_id=1, source_target_pairs={{0,8},{8,16},{16,24},{24,0},{1,9},{9,17},{17,25},{25,1},{2,10},{10... | collective-permute-start | bytes 1671176 | tf_op jit(solution)/shard_map/ppermute | solution.py:332
  144.8 2.6 reshape.262
  147.4 4.7 %all-to-all-start = ((bf16[8,50,2048]{2,1,0:T(8,128)(2,1)}), bf16[8,50,2048]{2,1,0:T(8,128)(2,1)}, u32[]{:S(2)}, u32[]{:S(2)}) async-start(bf16[8,50,2048]{2,1,0:T(8,128)(2,1)} %reshape.262), calls=%async_computation | async-start | bytes 3670016 | tf_op jit(solution)/shard_map/all_to_all | solution.py:356
  152.1 3.4 collective-permute-start.9
  155.5 3.7 collective-permute-done.11
  161.8 2.8 convolution_convert_fusion.4
  164.6 2.6 reshape.268
  167.2 8.7 %all-to-all-done = bf16[8,50,2048]{2,1,0:T(8,128)(2,1)} async-done(((bf16[8,50,2048]{2,1,0:T(8,128)(2,1)}), bf16[8,50,2048]{2,1,0:T(8,128)(2,1)}, u32[]{:S(2)}, u32[]{:S(2)}) %all-to-all-start) | async-done | bytes 1638432 | tf_op jit(solution)/shard_map/all_to_all | solution.py:356
  175.9 4.3 %all-to-all-start.6 = ((bf16[8,50,2048]{2,1,0:T(8,128)(2,1)}), bf16[8,50,2048]{2,1,0:T(8,128)(2,1)}, u32[]{:S(2)}, u32[]{:S(2)}) async-start(bf16[8,50,2048]{2,1,0:T(8,128)(2,1)} %reshape.268), calls=%async_computation.6 | async-start | bytes 3670016 | tf_op jit(solution)/shard_map/all_to_all | solution.py:356
  180.3 2.9 collective-permute-start.7
  185.9 2.6 reshape.266
  188.6 15.5 %all-to-all-done.6 = bf16[8,50,2048]{2,1,0:T(8,128)(2,1)} async-done(((bf16[8,50,2048]{2,1,0:T(8,128)(2,1)}), bf16[8,50,2048]{2,1,0:T(8,128)(2,1)}, u32[]{:S(2)}, u32[]{:S(2)}) %all-to-all-start.6) | async-done | bytes 1638432 | tf_op jit(solution)/shard_map/all_to_all | solution.py:356
  204.1 4.3 %all-to-all-start.4 = ((bf16[8,50,2048]{2,1,0:T(8,128)(2,1)}), bf16[8,50,2048]{2,1,0:T(8,128)(2,1)}, u32[]{:S(2)}, u32[]{:S(2)}) async-start(bf16[8,50,2048]{2,1,0:T(8,128)(2,1)} %reshape.266), calls=%async_computation.4 | async-start | bytes 3670016 | tf_op jit(solution)/shard_map/all_to_all | solution.py:356
  211.2 2.9 convolution_convert_fusion.6
  214.0 2.6 reshape.264
  216.6 15.7 %all-to-all-done.4 = bf16[8,50,2048]{2,1,0:T(8,128)(2,1)} async-done(((bf16[8,50,2048]{2,1,0:T(8,128)(2,1)}), bf16[8,50,2048]{2,1,0:T(8,128)(2,1)}, u32[]{:S(2)}, u32[]{:S(2)}) %all-to-all-start.4) | async-done | bytes 1638432 | tf_op jit(solution)/shard_map/all_to_all | solution.py:356
  232.3 4.3 %all-to-all-start.2 = ((bf16[8,50,2048]{2,1,0:T(8,128)(2,1)}), bf16[8,50,2048]{2,1,0:T(8,128)(2,1)}, u32[]{:S(2)}, u32[]{:S(2)}) async-start(bf16[8,50,2048]{2,1,0:T(8,128)(2,1)} %reshape.264), calls=%async_computation.2 | async-start | bytes 3670016 | tf_op jit(solution)/shard_map/all_to_all | solution.py:356
  236.6 2.7 reshape_squeeze_reshape.15
  239.3 4.5 %fusion = f32[400,1024]{1,0:T(8,128)S(1)} fusion(bf16[400,2048]{1,0:T(8,128)(2,1)} %reshape_squeeze_reshape.15, bf16[1,2048,1024]{2,1,0:T(8,128)(2,1)} %param.30), kind=kOutput, calls=%fused_computation | convolution fusion | flops 1677721600 | bytes 7471104 | tf_op jit(solution)/shard_map/dot_general | solution.py:201
  243.9 2.2 convolution_convert_fusion
  246.1 2.7 reshape_stack_reshape.15
  248.8 11.7 %all-to-all-done.2 = bf16[8,50,2048]{2,1,0:T(8,128)(2,1)} async-done(((bf16[8,50,2048]{2,1,0:T(8,128)(2,1)}), bf16[8,50,2048]{2,1,0:T(8,128)(2,1)}, u32[]{:S(2)}, u32[]{:S(2)}) %all-to-all-start.2) | async-done | bytes 1638432 | tf_op jit(solution)/shard_map/all_to_all | solution.py:356
  260.5 4.3 %all-to-all-start.7 = ((bf16[8,50,2048]{2,1,0:T(8,128)(2,1)}), bf16[8,50,2048]{2,1,0:T(8,128)(2,1)}, u32[]{:S(2)}, u32[]{:S(2)}) async-start(bf16[8,50,2048]{2,1,0:T(8,128)(2,1)} %reshape_stack_reshape.15), calls=%async_computation.7 | async-start | bytes 3670016 | tf_op jit(solution)/shard_map/all_to_all | solution.py:367
  265.0 2.7 reshape_squeeze_reshape.14
  267.6 4.5 %fusion.2 = f32[400,1024]{1,0:T(8,128)S(1)} fusion(bf16[400,2048]{1,0:T(8,128)(2,1)} %reshape_squeeze_reshape.14, bf16[1,2048,1024]{2,1,0:T(8,128)(2,1)} %param.30), kind=kOutput, calls=%fused_computation.2 | convolution fusion | flops 1677721600 | bytes 7471104 | tf_op jit(solution)/shard_map/dot_general | solution.py:201
  272.2 2.2 convolution_convert_fusion.1
  274.4 2.6 reshape_stack_reshape.14
  277.0 11.7 %all-to-all-done.7 = bf16[8,50,2048]{2,1,0:T(8,128)(2,1)} async-done(((bf16[8,50,2048]{2,1,0:T(8,128)(2,1)}), bf16[8,50,2048]{2,1,0:T(8,128)(2,1)}, u32[]{:S(2)}, u32[]{:S(2)}) %all-to-all-start.7) | async-done | bytes 1638432 | tf_op jit(solution)/shard_map/all_to_all | solution.py:367
  288.7 4.5 %all-to-all-start.5 = ((bf16[8,50,2048]{2,1,0:T(8,128)(2,1)}), bf16[8,50,2048]{2,1,0:T(8,128)(2,1)}, u32[]{:S(2)}, u32[]{:S(2)}) async-start(bf16[8,50,2048]{2,1,0:T(8,128)(2,1)} %reshape_stack_reshape.14), calls=%async_computation.5 | async-start | bytes 3670016 | tf_op jit(solution)/shard_map/all_to_all | solution.py:367
  294.8 2.6 reshape_squeeze_reshape.12
  297.4 2.6 reshape_squeeze_reshape.13
  300.0 4.5 %fusion.4 = f32[400,1024]{1,0:T(8,128)S(1)} fusion(bf16[400,2048]{1,0:T(8,128)(2,1)} %reshape_squeeze_reshape.13, bf16[1,2048,1024]{2,1,0:T(8,128)(2,1)} %param.30), kind=kOutput, calls=%fused_computation.4 | convolution fusion | flops 1677721600 | bytes 7471104 | tf_op jit(solution)/shard_map/dot_general | solution.py:201
  304.6 2.2 convolution_convert_fusion.2
  306.8 2.7 reshape_stack_reshape.13
  309.5 7.6 %all-to-all-done.5 = bf16[8,50,2048]{2,1,0:T(8,128)(2,1)} async-done(((bf16[8,50,2048]{2,1,0:T(8,128)(2,1)}), bf16[8,50,2048]{2,1,0:T(8,128)(2,1)}, u32[]{:S(2)}, u32[]{:S(2)}) %all-to-all-start.5) | async-done | bytes 1638432 | tf_op jit(solution)/shard_map/all_to_all | solution.py:367
  317.0 4.3 %all-to-all-start.3 = ((bf16[8,50,2048]{2,1,0:T(8,128)(2,1)}), bf16[8,50,2048]{2,1,0:T(8,128)(2,1)}, u32[]{:S(2)}, u32[]{:S(2)}) async-start(bf16[8,50,2048]{2,1,0:T(8,128)(2,1)} %reshape_stack_reshape.13), calls=%async_computation.3 | async-start | bytes 3670016 | tf_op jit(solution)/shard_map/all_to_all | solution.py:367
  321.4 4.5 %fusion.6 = f32[400,1024]{1,0:T(8,128)S(1)} fusion(bf16[400,2048]{1,0:T(8,128)(2,1)} %reshape_squeeze_reshape.12, bf16[1,2048,1024]{2,1,0:T(8,128)(2,1)} %param.30), kind=kOutput, calls=%fused_computation.6 | convolution fusion | flops 1677721600 | bytes 7471104 | tf_op jit(solution)/shard_map/dot_general | solution.py:201
  325.9 2.2 convolution_convert_fusion.3
  328.2 2.6 reshape_stack_reshape.12
  330.8 2.6 reshape.269
  336.7 2.8 collective-permute-start.12
  339.5 2.6 reshape.267
  342.1 3.1 all-to-all-done.3
  345.2 4.3 %all-to-all-start.1 = ((bf16[8,50,2048]{2,1,0:T(8,128)(2,1)}), bf16[8,50,2048]{2,1,0:T(8,128)(2,1)}, u32[]{:S(2)}, u32[]{:S(2)}) async-start(bf16[8,50,2048]{2,1,0:T(8,128)(2,1)} %reshape_stack_reshape.12), calls=%async_computation.1 | async-start | bytes 3670016 | tf_op jit(solution)/shard_map/all_to_all | solution.py:367
  349.6 2.0 fusion.247
  352.9 3.4 collective-permute-start.10
  356.3 2.6 reshape.265
  358.9 2.0 fusion.246
  362.7 10.7 %all-to-all-done.1 = bf16[8,50,2048]{2,1,0:T(8,128)(2,1)} async-done(((bf16[8,50,2048]{2,1,0:T(8,128)(2,1)}), bf16[8,50,2048]{2,1,0:T(8,128)(2,1)}, u32[]{:S(2)}, u32[]{:S(2)}) %all-to-all-start.1) | async-done | bytes 1638432 | tf_op jit(solution)/shard_map/all_to_all | solution.py:367
  373.4 2.6 reshape.263
  378.1 12.9 %collective-permute-done.10 = bf16[128,2048]{1,0:T(8,128)(2,1)} collective-permute-done((bf16[128,2048]{1,0:T(8,128)(2,1)}, bf16[128,2048]{1,0:T(8,128)(2,1)}, u32[]{:S(2)}, u32[]{:S(2)}) %collective-permute-start.10) | collective-permute-done | bytes 524320 | tf_op jit(solution)/shard_map/ppermute | solution.py:381
  391.0 2.7 fusion.66
  (265 shorter events, 87.7 us)
Async XLA Ops:
  0.0 243.8 %copy-start = (bf16[1,512,2048]{2,1,0:T(8,128)(2,1)S(1)}, bf16[1,512,2048]{2,1,0:T(8,128)(2,1)}, u32[]{:S(2)}) copy-start(bf16[1,512,2048]{2,1,0:T(8,128)(2,1)} %param.31) | copy-start | bytes 6291460
  0.0 14.2 %copy-start.26 = (bf16[256,1024]{1,0:T(8,128)(2,1)S(1)}, bf16[256,1024]{1,0:T(8,128)(2,1)}, u32[]{:S(2)}) copy-start(bf16[256,1024]{1,0:T(8,128)(2,1)} %param.17) | copy-start | bytes 1572868
  1.6 12.6 %collective-permute-start = (bf16[3,2048]{1,0:T(4,128)(2,1)S(1)}, bf16[3,2048]{1,0:T(4,128)(2,1)S(1)}, u32[]{:S(2)}, u32[]{:S(2)}) collective-permute-start(bf16[3,2048]{1,0:T(4,128)(2,1)S(1)} %pad_maximum_fusion.5), channel_id=1, source_target_pairs={{0,2},{2,4},{4,6},{6,8},{8,10},{10,12},{12,14},{14,16},{16,18},{18... | collective-permute-start | bytes 36872 | tf_op jit(solution)/shard_map/ppermute | solution.py:19
  36.4 1.2 copy-start.17
  40.6 3.5 copy-start.1
  48.5 1.9 copy-start.23
  49.1 1.4 copy-start.10
  49.8 2.2 copy-start.12
  50.5 2.2 copy-start.14
  51.3 2.1 copy-start.19
  52.0 1.4 copy-start.21
  52.7 2.4 copy-start.16
  52.7 6.6 %copy-start.36 = (s32[128,10]{0,1:T(8,128)S(1)}, s32[128,10]{0,1:T(8,128)}, u32[]{:S(2)}) copy-start(s32[128,10]{0,1:T(8,128)} %param.28) | copy-start | bytes 15364
  53.4 0.8 copy-start.7
  55.1 14.6 %collective-permute-start.1 = (bf16[2,8,128,128]{3,2,1,0:T(8,128)(2,1)}, bf16[2,8,128,128]{3,2,1,0:T(8,128)(2,1)}, u32[]{:S(2)}, u32[]{:S(2)}) collective-permute-start(bf16[2,8,128,128]{3,2,1,0:T(8,128)(2,1)} %pad_maximum_fusion.2), channel_id=1, source_target_pairs={{0,2},{2,4},{4,6},{6,8},{8,10},{10,12},{12,14},{14,16},{16,18},{18... | collective-permute-start | bytes 1572872 | tf_op jit(solution)/shard_map/ppermute | solution.py:19
  59.4 12.0 %copy-start.8 = (f32[8,128,128]{2,1,0:T(8,128)S(1)}, f32[8,128,128]{2,1,0:T(8,128)}, u32[]{:S(2)}) copy-start(f32[8,128,128]{2,1,0:T(8,128)} %copy-done.7) | copy-start | bytes 1572868
  71.4 6.9 %copy-start.38 = (f32[128]{0:T(128)S(1)}, f32[128]{0:T(128)}, u32[]{:S(2)}) copy-start(f32[128]{0:T(128)} %param.24) | copy-start | bytes 1540
  71.4 6.9 %copy-start.25 = (f32[256,4,128]{2,1,0:T(4,128)S(1)}, f32[256,4,128]{2,1,0:T(4,128)}, u32[]{:S(2)}) copy-start(f32[256,4,128]{2,1,0:T(4,128)} %get-tuple-element.24) | copy-start | bytes 1572868
  73.0 15.3 %collective-permute-start.2 = (bf16[2,8,128,128]{3,2,1,0:T(8,128)(2,1)S(1)}, bf16[2,8,128,128]{3,2,1,0:T(8,128)(2,1)S(1)}, u32[]{:S(2)}, u32[]{:S(2)}) collective-permute-start(bf16[2,8,128,128]{3,2,1,0:T(8,128)(2,1)S(1)} %pad_maximum_fusion.3), channel_id=1, source_target_pairs={{0,4},{2,6},{4,8},{6,10},{8,12},{10,14},{12,16},{14,18},{16,20},{1... | collective-permute-start | bytes 1572872 | tf_op jit(solution)/shard_map/ppermute | solution.py:19
  88.6 7.0 %copy-start.2 = (f32[8,4,64,256]{3,2,1,0:T(8,128)S(1)}, f32[8,4,64,256]{3,2,1,0:T(8,128)}, u32[]{:S(2)}) copy-start(f32[8,4,64,256]{3,2,1,0:T(8,128)} %copy-done.1) | copy-start | bytes 6291460
  89.2 15.4 %collective-permute-start.3 = (bf16[2,8,128,128]{3,2,1,0:T(8,128)(2,1)S(1)}, bf16[2,8,128,128]{3,2,1,0:T(8,128)(2,1)S(1)}, u32[]{:S(2)}, u32[]{:S(2)}) collective-permute-start(bf16[2,8,128,128]{3,2,1,0:T(8,128)(2,1)S(1)} %pad_maximum_fusion.4), channel_id=1, source_target_pairs={{0,8},{2,10},{4,12},{6,14},{8,16},{10,18},{12,20},{14,22},{16,24},... | collective-permute-start | bytes 1572872 | tf_op jit(solution)/shard_map/ppermute | solution.py:19
  98.1 12.5 %copy-start.11 = (f32[8,128,128]{2,1,0:T(8,128)S(1)}, f32[8,128,128]{2,1,0:T(8,128)}, u32[]{:S(2)}) copy-start(f32[8,128,128]{2,1,0:T(8,128)} %copy-done.10) | copy-start | bytes 1572868
  98.1 12.5 %copy-start.13 = (f32[8,128,128]{2,1,0:T(8,128)S(1)}, f32[8,128,128]{2,1,0:T(8,128)}, u32[]{:S(2)}) copy-start(f32[8,128,128]{2,1,0:T(8,128)} %copy-done.12) | copy-start | bytes 1572868
  98.2 12.5 %copy-start.15 = (f32[8,128,128]{2,1,0:T(8,128)S(1)}, f32[8,128,128]{2,1,0:T(8,128)}, u32[]{:S(2)}) copy-start(f32[8,128,128]{2,1,0:T(8,128)} %copy-done.14) | copy-start | bytes 1572868
  105.0 9.3 %collective-permute-start.4 = (bf16[8,128,128]{2,1,0:T(8,128)(2,1)S(1)}, bf16[8,128,128]{2,1,0:T(8,128)(2,1)S(1)}, u32[]{:S(2)}, u32[]{:S(2)}) collective-permute-start(bf16[8,128,128]{2,1,0:T(8,128)(2,1)S(1)} %get-tuple-element.62), channel_id=1, source_target_pairs={{0,16},{2,18},{4,20},{6,22},{8,24},{10,26},{12,28},{14,30},{1,17},... | collective-permute-start | bytes 786440 | tf_op jit(solution)/shard_map/ppermute | solution.py:19
  112.6 3.8 copy-start.20
  112.6 3.8 copy-start.22
  112.7 3.8 copy-start.24
  114.8 5.5 %collective-permute-start.5 = (bf16[8,128,128]{2,1,0:T(8,128)(2,1)S(1)}, bf16[8,128,128]{2,1,0:T(8,128)(2,1)S(1)}, u32[]{:S(2)}, u32[]{:S(2)}) collective-permute-start(bf16[8,128,128]{2,1,0:T(8,128)(2,1)S(1)} %fusion.58), channel_id=1, source_target_pairs={{0,2},{2,4},{4,6},{6,8},{8,10},{10,12},{12,14},{14,16},{16,18},{18... | collective-permute-start | bytes 786440 | tf_op jit(solution)/shard_map/ppermute | solution.py:19
  121.2 1.0 copy-start.28
  121.9 2.2 copy-start.18
  124.1 2.8 copy-start.37
  124.1 4.8 %copy-start.27 = (bf16[128,2048]{1,0:T(8,128)(2,1)S(1)}, bf16[128,2048]{1,0:T(8,128)(2,1)}, u32[]{:S(2)}) copy-start(bf16[128,2048]{1,0:T(8,128)(2,1)} %param.26) | copy-start | bytes 1572868
  125.4 1.3 copy-start.9
  126.7 3.9 copy-start.35
  126.8 2.1 collective-permute-start.6
  126.9 0.6 copy-start.33
  126.9 0.7 copy-start.31
  131.8 27.4 %collective-permute-start.11 = (bf16[128,2176]{1,0:T(8,128)(2,1)}, bf16[128,2176]{1,0:T(8,128)(2,1)}, u32[]{:S(2)}, u32[]{:S(2)}) collective-permute-start(bf16[128,2176]{1,0:T(8,128)(2,1)} %concatenate.23), channel_id=1, source_target_pairs={{0,8},{8,16},{16,24},{24,0},{1,9},{9,17},{17,25},{25,1},{2,10},{10... | collective-permute-start | bytes 1671176 | tf_op jit(solution)/shard_map/ppermute | solution.py:332
  142.7 4.7 %copy-start.29 = (s32[128,10]{0,1:T(8,128)}, s32[128,10]{0,1:T(8,128)S(1)}, u32[]{:S(2)}) copy-start(s32[128,10]{0,1:T(8,128)S(1)} %copy.171) | copy-start | bytes 15364
  147.4 28.6 %all-to-all-start = ((bf16[8,50,2048]{2,1,0:T(8,128)(2,1)}), bf16[8,50,2048]{2,1,0:T(8,128)(2,1)}, u32[]{:S(2)}, u32[]{:S(2)}) async-start(bf16[8,50,2048]{2,1,0:T(8,128)(2,1)} %reshape.262), calls=%async_computation | async-start | bytes 3670016 | tf_op jit(solution)/shard_map/all_to_all | solution.py:356
  152.1 31.1 %collective-permute-start.9 = (bf16[128,2176]{1,0:T(8,128)(2,1)}, bf16[128,2176]{1,0:T(8,128)(2,1)S(1)}, u32[]{:S(2)}, u32[]{:S(2)}) collective-permute-start(bf16[128,2176]{1,0:T(8,128)(2,1)} %concatenate.23), channel_id=1, source_target_pairs={{0,16},{8,24},{16,0},{24,8},{1,17},{9,25},{17,1},{25,9},{2,18},{10... | collective-permute-start | bytes 1671176 | tf_op jit(solution)/shard_map/ppermute | solution.py:332
  175.9 28.2 %all-to-all-start.6 = ((bf16[8,50,2048]{2,1,0:T(8,128)(2,1)}), bf16[8,50,2048]{2,1,0:T(8,128)(2,1)}, u32[]{:S(2)}, u32[]{:S(2)}) async-start(bf16[8,50,2048]{2,1,0:T(8,128)(2,1)} %reshape.268), calls=%async_computation.6 | async-start | bytes 3670016 | tf_op jit(solution)/shard_map/all_to_all | solution.py:356
  180.3 28.2 %collective-permute-start.7 = (bf16[128,2176]{1,0:T(8,128)(2,1)}, bf16[128,2176]{1,0:T(8,128)(2,1)}, u32[]{:S(2)}, u32[]{:S(2)}) collective-permute-start(bf16[128,2176]{1,0:T(8,128)(2,1)} %concatenate.23), channel_id=1, source_target_pairs={{0,24},{8,0},{16,8},{24,16},{1,25},{9,1},{17,9},{25,17},{2,26},{10... | collective-permute-start | bytes 1671176 | tf_op jit(solution)/shard_map/ppermute | solution.py:332
  204.1 28.2 %all-to-all-start.4 = ((bf16[8,50,2048]{2,1,0:T(8,128)(2,1)}), bf16[8,50,2048]{2,1,0:T(8,128)(2,1)}, u32[]{:S(2)}, u32[]{:S(2)}) async-start(bf16[8,50,2048]{2,1,0:T(8,128)(2,1)} %reshape.266), calls=%async_computation.4 | async-start | bytes 3670016 | tf_op jit(solution)/shard_map/all_to_all | solution.py:356
  232.3 28.2 %all-to-all-start.2 = ((bf16[8,50,2048]{2,1,0:T(8,128)(2,1)}), bf16[8,50,2048]{2,1,0:T(8,128)(2,1)}, u32[]{:S(2)}, u32[]{:S(2)}) async-start(bf16[8,50,2048]{2,1,0:T(8,128)(2,1)} %reshape.264), calls=%async_computation.2 | async-start | bytes 3670016 | tf_op jit(solution)/shard_map/all_to_all | solution.py:356
  260.5 28.2 %all-to-all-start.7 = ((bf16[8,50,2048]{2,1,0:T(8,128)(2,1)}), bf16[8,50,2048]{2,1,0:T(8,128)(2,1)}, u32[]{:S(2)}, u32[]{:S(2)}) async-start(bf16[8,50,2048]{2,1,0:T(8,128)(2,1)} %reshape_stack_reshape.15), calls=%async_computation.7 | async-start | bytes 3670016 | tf_op jit(solution)/shard_map/all_to_all | solution.py:367
  288.7 28.4 %all-to-all-start.5 = ((bf16[8,50,2048]{2,1,0:T(8,128)(2,1)}), bf16[8,50,2048]{2,1,0:T(8,128)(2,1)}, u32[]{:S(2)}, u32[]{:S(2)}) async-start(bf16[8,50,2048]{2,1,0:T(8,128)(2,1)} %reshape_stack_reshape.14), calls=%async_computation.5 | async-start | bytes 3670016 | tf_op jit(solution)/shard_map/all_to_all | solution.py:367
  317.0 28.2 %all-to-all-start.3 = ((bf16[8,50,2048]{2,1,0:T(8,128)(2,1)}), bf16[8,50,2048]{2,1,0:T(8,128)(2,1)}, u32[]{:S(2)}, u32[]{:S(2)}) async-start(bf16[8,50,2048]{2,1,0:T(8,128)(2,1)} %reshape_stack_reshape.13), calls=%async_computation.3 | async-start | bytes 3670016 | tf_op jit(solution)/shard_map/all_to_all | solution.py:367
  333.4 2.0 copy-start.5
  336.7 41.3 %collective-permute-start.12 = (bf16[128,2048]{1,0:T(8,128)(2,1)}, bf16[128,2048]{1,0:T(8,128)(2,1)S(1)}, u32[]{:S(2)}, u32[]{:S(2)}) collective-permute-start(bf16[128,2048]{1,0:T(8,128)(2,1)} %fusion.12), channel_id=1, source_target_pairs={{0,24},{8,0},{16,8},{24,16},{1,25},{9,1},{17,9},{25,17},{2,26},{10... | collective-permute-start | bytes 1572872 | tf_op jit(solution)/shard_map/ppermute | solution.py:381
  345.2 28.2 %all-to-all-start.1 = ((bf16[8,50,2048]{2,1,0:T(8,128)(2,1)}), bf16[8,50,2048]{2,1,0:T(8,128)(2,1)}, u32[]{:S(2)}, u32[]{:S(2)}) async-start(bf16[8,50,2048]{2,1,0:T(8,128)(2,1)} %reshape_stack_reshape.12), calls=%async_computation.1 | async-start | bytes 3670016 | tf_op jit(solution)/shard_map/all_to_all | solution.py:367
  349.6 2.0 copy-start.4
  352.9 38.0 %collective-permute-start.10 = (bf16[128,2048]{1,0:T(8,128)(2,1)}, bf16[128,2048]{1,0:T(8,128)(2,1)}, u32[]{:S(2)}, u32[]{:S(2)}) collective-permute-start(bf16[128,2048]{1,0:T(8,128)(2,1)} %fusion.11), channel_id=1, source_target_pairs={{0,16},{8,24},{16,0},{24,8},{1,17},{9,25},{17,1},{25,9},{2,18},{10... | collective-permute-start | bytes 1572872 | tf_op jit(solution)/shard_map/ppermute | solution.py:381
  358.9 2.1 copy-start.6
  360.9 1.3 copy-start.30
  360.9 1.3 copy-start.32
  361.0 1.3 copy-start.34
  362.2 28.7 %collective-permute-start.8 = (bf16[128,2048]{1,0:T(8,128)(2,1)}, bf16[128,2048]{1,0:T(8,128)(2,1)}, u32[]{:S(2)}, u32[]{:S(2)}) collective-permute-start(bf16[128,2048]{1,0:T(8,128)(2,1)} %fusion.10), channel_id=1, source_target_pairs={{0,8},{8,16},{16,24},{24,0},{1,9},{9,17},{17,25},{25,1},{2,10},{10... | collective-permute-start | bytes 1572872 | tf_op jit(solution)/shard_map/ppermute | solution.py:381
  376.0 14.9 %copy-start.3 = (bf16[400,2048]{1,0:T(8,128)(2,1)S(1)}, bf16[400,2048]{1,0:T(8,128)(2,1)}, u32[]{:S(2)}) copy-start(bf16[400,2048]{1,0:T(8,128)(2,1)} %reshape.263) | copy-start | bytes 4915204
where the time goes:
time: 400 us; the launch traced here: 394 us
  waiting for transfers between devices  130 us (32%)
  matrix products  97.6 us (24%)
  starting transfers between devices  86.5 us (22%)
  local copies, waits for them, and re-layouts  59.4 us (15%)
  other arithmetic  19 us (5%)
    all_to_all x4, waiting for transfers between devices, per_device(): lax.all_to_all(outgoing, level_axes, split_axis=0, concat_axis=0, tiled=T...  51.6 us
    all_to_all x4, waiting for transfers between devices, per_device(): lax.all_to_all(answered, level_axes, split_axis=0, concat_axis=0, tiled=T...  33 us
    ppermute x6, starting transfers between devices, passed_along(): return lax.ppermute(block, axis, route)  28 us
    ppermute x6, waiting for transfers between devices, passed_along(): return lax.ppermute(block, axis, route)  27.6 us
    dot_general x17, matrix products, precise_dot(): jnp.dot(left, right, precision=HIGHEST, preferred_element_type=jnp.float32)  27 us
    dot_general x4, matrix products, expert_apply_rows(): gate_up = jnp.dot(rows_in, up_matrix, preferred_element_type=jnp.float32)  18.1 us
    all_to_all x4, starting transfers between devices, per_device(): lax.all_to_all(outgoing, level_axes, split_axis=0, concat_axis=0, tiled=T...  17.7 us
    all_to_all x4, starting transfers between devices, per_device(): lax.all_to_all(answered, level_axes, split_axis=0, concat_axis=0, tiled=T...  17.5 us
  transfers between devices with their start and end apart: 21, of which 16 were waited for; matrix products, arithmetic and copies ran while one was open for 30% of the time, Pallas kernels for 0%

commit v1 on v0

--- a/solution.py
+++ b/solution.py
@@ -324,48 +324,57 @@
     slots_total = per_level * capacity
     slot_ids = jnp.arange(slots_total, dtype=jnp.int32)
     level_axes = ("ctx_lo", "head")
+    received = [packed] + [
+        lax.ppermute(packed, "ctx_hi", [(i, (i - turn) % levels) for i in range(levels)])
+        for turn in range(1, levels)
+    ]
+    turn_groups = [[0]] + ([list(range(1, levels))] if levels > 1 else [])
     routed = None
-    for turn in range(levels):
-        if turn == 0:
-            chunk = packed
-        else:
-            chunk = lax.ppermute(
-                packed, "ctx_hi", [(i, (i - turn) % levels) for i in range(levels)]
-            )
+    for group_turns in turn_groups:
+        members = len(group_turns)
+        chunk = jnp.concatenate([received[turn] for turn in group_turns], axis=0)
         chunk_in = chunk[:, :D]
         chunk_routes = chunk[:, D : D + top_count].astype(jnp.int32)
         chunk_high = chunk[:, D + top_count : D + 2 * top_count]
         chunk_low = chunk[:, D + 2 * top_count : D + 3 * top_count]
         route_hot = chunk_routes[:, :, None] == expert_ids[None, None, :]
         row_hot = jnp.any(route_hot, axis=1).astype(jnp.bfloat16)
-        earlier = jnp.dot(earlier_rows, row_hot, preferred_element_type=jnp.float32)
+        earlier = jnp.einsum(
+            "ij,sje->sie",
+            earlier_rows,
+            row_hot.reshape(members, local_rows, experts_all),
+            preferred_element_type=jnp.float32,
+        ).reshape(members * local_rows, experts_all)
         slot_rank = jnp.sum(jnp.where(route_hot, earlier[:, None, :], 0.0), axis=2).astype(
             jnp.int32
         )
+        member_of = lax.broadcasted_iota(jnp.int32, chunk_routes.shape, 0) // local_rows
+        group_capacity = members * capacity
         slot_index = jnp.where(
             chunk_routes // per_level == level,
-            (chunk_routes % per_level) * capacity + slot_rank,
+            (chunk_routes % per_level) * group_capacity + member_of * capacity + slot_rank,
             -1,
         )
+        slot_ids = jnp.arange(per_level * group_capacity, dtype=jnp.int32)
         hits = slot_index[:, :, None] == slot_ids[None, None, :]
         picker = jnp.any(hits, axis=1).astype(jnp.bfloat16)
         outgoing = lax.dot_general(
             picker, chunk_in, (((0,), (0,)), ((), ())), preferred_element_type=jnp.float32
         ).astype(jnp.bfloat16)
-        outgoing = outgoing.reshape(per_level // local_experts, local_experts * capacity, D)
+        outgoing = outgoing.reshape(per_level // local_experts, local_experts * group_capacity, D)
         arrived = lax.all_to_all(outgoing, level_axes, split_axis=0, concat_axis=0, tiled=True)
-        arrived = arrived.reshape(per_level // local_experts, local_experts, capacity, D)
+        arrived = arrived.reshape(per_level // local_experts, local_experts, group_capacity, D)
         answered = jnp.stack(
             [
                 expert_apply_rows(
                     arrived[:, member].reshape(-1, D), expert_up[member], expert_down[member]
-                ).reshape(arrived.shape[0], capacity, D)
+                ).reshape(arrived.shape[0], group_capacity, D)
                 for member in range(local_experts)
             ],
             axis=1,
-        ).reshape(per_level // local_experts, local_experts * capacity, D)
+        ).reshape(per_level // local_experts, local_experts * group_capacity, D)
         returned = lax.all_to_all(answered, level_axes, split_axis=0, concat_axis=0, tiled=True)
-        result_rows = returned.reshape(slots_total, D)
+        result_rows = returned.reshape(per_level * group_capacity, D)
         weight_high = jnp.sum(jnp.where(hits, chunk_high[:, :, None], 0.0), axis=1).astype(
             jnp.bfloat16
         )
@@ -375,14 +384,16 @@
         partial = jnp.dot(weight_high, result_rows, preferred_element_type=jnp.float32) + jnp.dot(
             weight_low, result_rows, preferred_element_type=jnp.float32
         )
-        if turn == 0:
-            routed = partial
-        else:
-            routed = routed + lax.ppermute(
-                partial.astype(jnp.bfloat16),
-                "ctx_hi",
-                [(i, (i + turn) % levels) for i in range(levels)],
-            ).astype(jnp.float32)
+        for index, turn in enumerate(group_turns):
+            piece = partial[index * local_rows : (index + 1) * local_rows]
+            if turn == 0:
+                routed = piece
+            else:
+                routed = routed + lax.ppermute(
+                    piece.astype(jnp.bfloat16),
+                    "ctx_hi",
+                    [(i, (i + turn) % levels) for i in range(levels)],
+                ).astype(jnp.float32)
     combined = hidden.astype(jnp.float32) + routed
     return combined.astype(jnp.bfloat16)
 

time: 400 us -> 439 us (1.097)
  the two profiles are of different devices: /device:TPU:0 before, /device:TPU:11 now
where the time goes in v1:
time: 439 us; the launch traced here: 434 us
  waiting for transfers between devices  212 us (48%)
  matrix products  85.8 us (20%)
  starting transfers between devices  58.9 us (13%)
  local copies, waits for them, and re-layouts  51.1 us (12%)
  other arithmetic  25 us (6%)
    all_to_all x2, waiting for transfers between devices, per_device(): lax.all_to_all(outgoing, level_axes, split_axis=0, concat_axis=0, tiled=T...  50.9 us
    ppermute x3, waiting for transfers between devices, per_device(): lax.ppermute(packed, 'ctx_hi', [(i, (i - turn) % levels) for i in range(l...  45.3 us
    all_to_all x2, waiting for transfers between devices, per_device(): lax.all_to_all(answered, level_axes, split_axis=0, concat_axis=0, tiled=T...  42 us
    ppermute x6, waiting for transfers between devices, passed_along(): return lax.ppermute(block, axis, route)  38.2 us
    ppermute x3, waiting for transfers between devices, per_device(): lax.ppermute(piece.astype(jnp.bfloat16), 'ctx_hi', [(i, (i + turn) % leve...  35.1 us
    dot_general x17, matrix products, precise_dot(): jnp.dot(left, right, precision=HIGHEST, preferred_element_type=jnp.float32)  27 us
    ppermute x6, starting transfers between devices, passed_along(): return lax.ppermute(block, axis, route)  20.2 us
    all_to_all x2, starting transfers between devices, per_device(): lax.all_to_all(outgoing, level_axes, split_axis=0, concat_axis=0, tiled=T...  14.7 us
  transfers between devices with their start and end apart: 17, of which 15 were waited for; matrix products, arithmetic and copies ran while one was open for 19% of the time, Pallas kernels for 0%

profile of v1, /device:TPU:11, one launch (start us, length us, event | category | flops | bytes accessed | tf_op | source)
XLA Modules:
  0.0 433.9 jit_solution(15124624269432420446)
XLA Ops:
  1.6 3.1 collective-permute-start
  12.8 2.9 multiply_bitcast_fusion
  15.7 1.7 reshape.237
  18.1 1.6 fusion.113
  19.8 2.0 fusion.39
  31.8 1.6 convolution_subtract_fusion.1
  36.9 1.9 fusion.12
  38.9 3.5 fusion.73
  42.4 3.7 multiply_subtract_fusion
  54.2 3.1 collective-permute-start.1
  57.4 11.5 %collective-permute-done.1 = bf16[2,8,128,128]{3,2,1,0:T(8,128)(2,1)} collective-permute-done((bf16[2,8,128,128]{3,2,1,0:T(8,128)(2,1)}, bf16[2,8,128,128]{3,2,1,0:T(8,128)(2,1)}, u32[]{:S(2)}, u32[]{:S(2)}) %collective-permute-start.1) | collective-permute-done | bytes 524320 | tf_op jit(solution)/shard_map/ppermute | solution.py:19
  68.9 1.7 convolution_select_fusion.2
  70.6 1.4 fusion.46
  72.1 3.1 collective-permute-start.2
  75.4 1.8 fusion.35
  77.3 9.2 %collective-permute-done.2 = bf16[2,8,128,128]{3,2,1,0:T(8,128)(2,1)S(1)} collective-permute-done((bf16[2,8,128,128]{3,2,1,0:T(8,128)(2,1)S(1)}, bf16[2,8,128,128]{3,2,1,0:T(8,128)(2,1)S(1)}, u32[]{:S(2)}, u32[]{:S(2)}) %collective-permute-start.2) | collective-permute-done | bytes 524320 | tf_op jit(solution)/shard_map/ppermute | solution.py:19
  87.4 3.3 collective-permute-start.3
  91.9 1.3 convolution_subtract_fusion.5
  93.3 6.8 %collective-permute-done.3 = bf16[2,8,128,128]{3,2,1,0:T(8,128)(2,1)S(1)} collective-permute-done((bf16[2,8,128,128]{3,2,1,0:T(8,128)(2,1)S(1)}, bf16[2,8,128,128]{3,2,1,0:T(8,128)(2,1)S(1)}, u32[]{:S(2)}, u32[]{:S(2)}) %collective-permute-start.3) | collective-permute-done | bytes 524320 | tf_op jit(solution)/shard_map/ppermute | solution.py:19
  100.5 4.4 %collective-permute-start.4 = (bf16[8,128,128]{2,1,0:T(8,128)(2,1)S(1)}, bf16[8,128,128]{2,1,0:T(8,128)(2,1)S(1)}, u32[]{:S(2)}, u32[]{:S(2)}) collective-permute-start(bf16[8,128,128]{2,1,0:T(8,128)(2,1)S(1)} %get-tuple-element.55), channel_id=1, source_target_pairs={{0,16},{2,18},{4,20},{6,22},{8,24},{10,26},{12,28},{14,30},{1,17},... | collective-permute-start | bytes 786440 | tf_op jit(solution)/shard_map/ppermute | solution.py:19
  104.9 1.9 fusion.31
  107.3 7.4 %collective-permute-done.4 = bf16[8,128,128]{2,1,0:T(8,128)(2,1)S(1)} collective-permute-done((bf16[8,128,128]{2,1,0:T(8,128)(2,1)S(1)}, bf16[8,128,128]{2,1,0:T(8,128)(2,1)S(1)}, u32[]{:S(2)}, u32[]{:S(2)}) %collective-permute-start.4) | collective-permute-done | bytes 262176 | tf_op jit(solution)/shard_map/ppermute | solution.py:19
  115.1 3.1 collective-permute-start.5
  118.4 2.1 fusion.20
  120.5 3.3 collective-permute-done.5
  127.7 1.3 fusion.9
  128.9 1.3 copy-done.7
  130.4 2.6 collective-permute-start.6
  135.3 1.7 fusion.54
  138.3 3.1 collective-permute-start.8
  141.4 2.8 collective-permute-start.9
  144.2 8.5 %collective-permute-done.7 = bf16[128,2176]{1,0:T(8,128)(2,1)S(1)} collective-permute-done((bf16[128,2176]{1,0:T(8,128)(2,1)}, bf16[128,2176]{1,0:T(8,128)(2,1)S(1)}, u32[]{:S(2)}, u32[]{:S(2)}) %collective-permute-start.7) | collective-permute-done | bytes 557088 | tf_op jit(solution)/shard_map/ppermute | solution.py:328
  152.8 24.9 %collective-permute-done.8 = bf16[128,2176]{1,0:T(8,128)(2,1)S(1)} collective-permute-done((bf16[128,2176]{1,0:T(8,128)(2,1)}, bf16[128,2176]{1,0:T(8,128)(2,1)S(1)}, u32[]{:S(2)}, u32[]{:S(2)}) %collective-permute-start.8) | collective-permute-done | bytes 557088 | tf_op jit(solution)/shard_map/ppermute | solution.py:328
  177.7 11.9 %collective-permute-done.9 = bf16[128,2176]{1,0:T(8,128)(2,1)S(1)} collective-permute-done((bf16[128,2176]{1,0:T(8,128)(2,1)}, bf16[128,2176]{1,0:T(8,128)(2,1)S(1)}, u32[]{:S(2)}, u32[]{:S(2)}) %collective-permute-start.9) | collective-permute-done | bytes 557088 | tf_op jit(solution)/shard_map/ppermute | solution.py:328
  193.5 3.6 fusion.1
  197.2 5.8 %convolution_convert_fusion.1 = bf16[1200,2048]{1,0:T(8,128)(2,1)} fusion(pred[384,1200]{0,1:T(8,128)(4,1)S(1)} %fusion.1, bf16[384,2176]{1,0:T(8,128)(2,1)} %copy-done.26), kind=kOutput, calls=%fused_computation.7 | convolution fusion | flops 1889894400 | bytes 6948864 | tf_op jit(solution)/shard_map/dot_general | solution.py:361
  203.0 4.6 %reshape.250 = bf16[8,150,2048]{2,1,0:T(8,128)(2,1)} reshape(bf16[1200,2048]{1,0:T(8,128)(2,1)} %convolution_convert_fusion.1) | data formatting | bytes 9830400 | tf_op jit(solution)/shard_map/reshape | solution.py:364
  207.6 8.6 %all-to-all-start.2 = ((bf16[8,150,2048]{2,1,0:T(8,128)(2,1)}), bf16[8,150,2048]{2,1,0:T(8,128)(2,1)}, u32[]{:S(2)}, u32[]{:S(2)}) async-start(bf16[8,150,2048]{2,1,0:T(8,128)(2,1)} %reshape.250), calls=%async_computation.2 | async-start | bytes 9961472 | tf_op jit(solution)/shard_map/all_to_all | solution.py:365
  217.2 1.7 convolution_convert_fusion.3
  218.9 2.6 reshape.247
  221.6 50.7 %all-to-all-done.2 = bf16[8,150,2048]{2,1,0:T(8,128)(2,1)} async-done(((bf16[8,150,2048]{2,1,0:T(8,128)(2,1)}), bf16[8,150,2048]{2,1,0:T(8,128)(2,1)}, u32[]{:S(2)}, u32[]{:S(2)}) %all-to-all-start.2) | async-done | bytes 4915232 | tf_op jit(solution)/shard_map/all_to_all | solution.py:365
  272.3 6.0 %all-to-all-start = ((bf16[8,50,2048]{2,1,0:T(8,128)(2,1)}), bf16[8,50,2048]{2,1,0:T(8,128)(2,1)}, u32[]{:S(2)}, u32[]{:S(2)}) async-start(bf16[8,50,2048]{2,1,0:T(8,128)(2,1)} %reshape.247), calls=%async_computation | async-start | bytes 3670016 | tf_op jit(solution)/shard_map/all_to_all | solution.py:365
  278.3 4.6 %reshape_squeeze_reshape.7 = bf16[1200,2048]{1,0:T(8,128)(2,1)} reshape(bf16[8,150,2048]{2,1,0:T(8,128)(2,1)} %all-to-all-done.2) | data formatting | bytes 9830400 | tf_op jit(solution)/shard_map/reshape;squeeze;reshape | solution.py:370
  283.0 8.4 %fusion.5 = f32[1200,1024]{1,0:T(8,128)S(1)} fusion(bf16[1200,2048]{1,0:T(8,128)(2,1)} %reshape_squeeze_reshape.7, bf16[1,2048,1024]{2,1,0:T(8,128)(2,1)} %param.30), kind=kOutput, calls=%fused_computation.8 | convolution fusion | flops 5033164800 | bytes 14024704 | tf_op jit(solution)/shard_map/dot_general | solution.py:201
  291.3 4.5 %convolution_convert_fusion = bf16[1200,2048]{1,0:T(8,128)(2,1)} fusion(bf16[1,512,2048]{2,1,0:T(8,128)(2,1)S(1)} %copy-done, f32[1200,1024]{1,0:T(8,128)S(1)} %fusion.5), kind=kOutput, calls=%fused_computation.6 | convolution fusion | flops 2522726400 | bytes 11927552 | tf_op jit(solution)/shard_map/dot_general | solution.py:205
  295.9 4.6 %reshape_stack_reshape.7 = bf16[8,150,2048]{2,1,0:T(8,128)(2,1)} reshape(bf16[1200,2048]{1,0:T(8,128)(2,1)} %convolution_convert_fusion) | data formatting | bytes 9830400 | tf_op jit(solution)/shard_map/reshape;stack;reshape | solution.py:375
  300.6 6.1 %all-to-all-start.3 = ((bf16[8,150,2048]{2,1,0:T(8,128)(2,1)}), bf16[8,150,2048]{2,1,0:T(8,128)(2,1)}, u32[]{:S(2)}, u32[]{:S(2)}) async-start(bf16[8,150,2048]{2,1,0:T(8,128)(2,1)} %reshape_stack_reshape.7), calls=%async_computation.3 | async-start | bytes 9961472 | tf_op jit(solution)/shard_map/all_to_all | solution.py:376
  308.2 5.8 %fusion.3 = (bf16[384,1200]{0,1:T(8,128)(2,1)S(1)}, bf16[384,1200]{0,1:T(8,128)(2,1)}) fusion(s32[384,10]{0,1:T(8,128)} %copy-done.34, bf16[384,10]{0,1:T(8,128)(2,1)} %copy.168, bf16[384,10]{0,1:T(8,128)(2,1)} %copy.169), kind=kLoop, calls=%fused_computation.4 | loop fusion | flops 22118400 | bytes 1873920 | tf_op jit(solution)/shard_map/reduce_sum | solution.py:378
  314.0 2.6 reshape_squeeze_reshape.6
  316.7 4.5 %fusion.7 = f32[400,1024]{1,0:T(8,128)S(1)} fusion(bf16[400,2048]{1,0:T(8,128)(2,1)} %reshape_squeeze_reshape.6, bf16[1,2048,1024]{2,1,0:T(8,128)(2,1)} %param.30), kind=kOutput, calls=%fused_computation.10 | convolution fusion | flops 1677721600 | bytes 7471104 | tf_op jit(solution)/shard_map/dot_general | solution.py:201
  321.2 2.3 convolution_convert_fusion.2
  323.5 2.6 reshape_stack_reshape.6
  326.1 36.8 %all-to-all-done.3 = bf16[8,150,2048]{2,1,0:T(8,128)(2,1)} async-done(((bf16[8,150,2048]{2,1,0:T(8,128)(2,1)}), bf16[8,150,2048]{2,1,0:T(8,128)(2,1)}, u32[]{:S(2)}, u32[]{:S(2)}) %all-to-all-start.3) | async-done | bytes 4915232 | tf_op jit(solution)/shard_map/all_to_all | solution.py:376
  362.8 6.1 %all-to-all-start.1 = ((bf16[8,50,2048]{2,1,0:T(8,128)(2,1)}), bf16[8,50,2048]{2,1,0:T(8,128)(2,1)}, u32[]{:S(2)}, u32[]{:S(2)}) async-start(bf16[8,50,2048]{2,1,0:T(8,128)(2,1)} %reshape_stack_reshape.6), calls=%async_computation.1 | async-start | bytes 3670016 | tf_op jit(solution)/shard_map/all_to_all | solution.py:376
  368.9 4.6 %reshape.251 = bf16[1200,2048]{1,0:T(8,128)(2,1)} reshape(bf16[8,150,2048]{2,1,0:T(8,128)(2,1)} %all-to-all-done.3) | data formatting | bytes 9830400 | tf_op jit(solution)/shard_map/reshape | solution.py:377
  373.5 5.1 %fusion.207 = f32[384,2048]{1,0:T(8,128)S(1)} fusion(bf16[384,1200]{0,1:T(8,128)(2,1)} %get-tuple-element.8, bf16[1200,2048]{1,0:T(8,128)(2,1)} %reshape.251), kind=kOutput, calls=%fused_computation.428 | convolution fusion | flops 1887436800 | bytes 8982528 | tf_op jit(solution)/shard_map/dot_general | solution.py:384
  378.6 2.4 add_convert_fusion
  382.3 2.1 collective-permute-start.10
  386.0 5.3 %all-to-all-done.1 = bf16[8,50,2048]{2,1,0:T(8,128)(2,1)} async-done(((bf16[8,50,2048]{2,1,0:T(8,128)(2,1)}), bf16[8,50,2048]{2,1,0:T(8,128)(2,1)}, u32[]{:S(2)}, u32[]{:S(2)}) %all-to-all-start.1) | async-done | bytes 1638432 | tf_op jit(solution)/shard_map/all_to_all | solution.py:376
  391.2 2.6 reshape.248
  393.8 2.0 fusion.206
  396.0 33.3 %collective-permute-done.11 = bf16[128,2048]{1,0:T(8,128)(2,1)} collective-permute-done((bf16[128,2048]{1,0:T(8,128)(2,1)}, bf16[128,2048]{1,0:T(8,128)(2,1)}, u32[]{:S(2)}, u32[]{:S(2)}) %collective-permute-start.11) | collective-permute-done | bytes 524320 | tf_op jit(solution)/shard_map/ppermute | solution.py:392
  429.3 1.7 collective-permute-done.12
  431.0 2.7 fusion.57
  (230 shorter events, 52.0 us)
Async XLA Ops:
  0.0 291.3 %copy-start = (bf16[1,512,2048]{2,1,0:T(8,128)(2,1)S(1)}, bf16[1,512,2048]{2,1,0:T(8,128)(2,1)}, u32[]{:S(2)}) copy-start(bf16[1,512,2048]{2,1,0:T(8,128)(2,1)} %param.31) | copy-start | bytes 6291460
  0.0 12.5 %copy-start.25 = (bf16[256,1024]{1,0:T(8,128)(2,1)S(1)}, bf16[256,1024]{1,0:T(8,128)(2,1)}, u32[]{:S(2)}) copy-start(bf16[256,1024]{1,0:T(8,128)(2,1)} %param.17) | copy-start | bytes 1572868
  1.6 10.9 %collective-permute-start = (bf16[3,2048]{1,0:T(4,128)(2,1)S(1)}, bf16[3,2048]{1,0:T(4,128)(2,1)S(1)}, u32[]{:S(2)}, u32[]{:S(2)}) collective-permute-start(bf16[3,2048]{1,0:T(4,128)(2,1)S(1)} %pad_maximum_fusion.5), channel_id=1, source_target_pairs={{0,2},{2,4},{4,6},{6,8},{8,10},{10,12},{12,14},{14,16},{16,18},{18... | collective-permute-start | bytes 36872 | tf_op jit(solution)/shard_map/ppermute | solution.py:19
  34.6 1.2 copy-start.16
  38.8 3.5 copy-start.2
  46.7 0.8 copy-start.22
  48.2 1.4 copy-start.18
  48.9 1.5 copy-start.20
  49.6 0.8 copy-start.5
  51.2 1.4 copy-start.8
  51.9 1.4 copy-start.10
  52.5 0.8 copy-start.12
  53.2 1.0 copy-start.14
  54.2 14.7 %collective-permute-start.1 = (bf16[2,8,128,128]{3,2,1,0:T(8,128)(2,1)}, bf16[2,8,128,128]{3,2,1,0:T(8,128)(2,1)}, u32[]{:S(2)}, u32[]{:S(2)}) collective-permute-start(bf16[2,8,128,128]{3,2,1,0:T(8,128)(2,1)} %pad_maximum_fusion.2), channel_id=1, source_target_pairs={{0,2},{2,4},{4,6},{6,8},{8,10},{10,12},{12,14},{14,16},{16,18},{18... | collective-permute-start | bytes 1572872 | tf_op jit(solution)/shard_map/ppermute | solution.py:19
  57.3 13.3 %copy-start.6 = (f32[8,128,128]{2,1,0:T(8,128)S(1)}, f32[8,128,128]{2,1,0:T(8,128)}, u32[]{:S(2)}) copy-start(f32[8,128,128]{2,1,0:T(8,128)} %copy-done.5) | copy-start | bytes 1572868
  57.3 13.3 %copy-start.15 = (f32[8,128,128]{2,1,0:T(8,128)S(1)}, f32[8,128,128]{2,1,0:T(8,128)}, u32[]{:S(2)}) copy-start(f32[8,128,128]{2,1,0:T(8,128)} %copy-done.14) | copy-start | bytes 1572868
  70.5 4.8 %copy-start.42 = (f32[128]{0:T(128)S(1)}, f32[128]{0:T(128)}, u32[]{:S(2)}) copy-start(f32[128]{0:T(128)} %param.24) | copy-start | bytes 1540
  70.5 4.8 %copy-start.24 = (f32[256,4,128]{2,1,0:T(4,128)S(1)}, f32[256,4,128]{2,1,0:T(4,128)}, u32[]{:S(2)}) copy-start(f32[256,4,128]{2,1,0:T(4,128)} %get-tuple-element.26) | copy-start | bytes 1572868
  72.1 14.3 %collective-permute-start.2 = (bf16[2,8,128,128]{3,2,1,0:T(8,128)(2,1)S(1)}, bf16[2,8,128,128]{3,2,1,0:T(8,128)(2,1)S(1)}, u32[]{:S(2)}, u32[]{:S(2)}) collective-permute-start(bf16[2,8,128,128]{3,2,1,0:T(8,128)(2,1)S(1)} %pad_maximum_fusion.3), channel_id=1, source_target_pairs={{0,4},{2,6},{4,8},{6,10},{8,12},{10,14},{12,16},{14,18},{16,20},{1... | collective-permute-start | bytes 1572872 | tf_op jit(solution)/shard_map/ppermute | solution.py:19
  86.9 3.9 copy-start.3
  87.4 12.7 %collective-permute-start.3 = (bf16[2,8,128,128]{3,2,1,0:T(8,128)(2,1)S(1)}, bf16[2,8,128,128]{3,2,1,0:T(8,128)(2,1)S(1)}, u32[]{:S(2)}, u32[]{:S(2)}) collective-permute-start(bf16[2,8,128,128]{3,2,1,0:T(8,128)(2,1)S(1)} %pad_maximum_fusion.4), channel_id=1, source_target_pairs={{0,8},{2,10},{4,12},{6,14},{8,16},{10,18},{12,20},{14,22},{16,24},... | collective-permute-start | bytes 1572872 | tf_op jit(solution)/shard_map/ppermute | solution.py:19
  93.3 11.6 %copy-start.9 = (f32[8,128,128]{2,1,0:T(8,128)S(1)}, f32[8,128,128]{2,1,0:T(8,128)}, u32[]{:S(2)}) copy-start(f32[8,128,128]{2,1,0:T(8,128)} %copy-done.8) | copy-start | bytes 1572868
  93.3 11.6 %copy-start.11 = (f32[8,128,128]{2,1,0:T(8,128)S(1)}, f32[8,128,128]{2,1,0:T(8,128)}, u32[]{:S(2)}) copy-start(f32[8,128,128]{2,1,0:T(8,128)} %copy-done.10) | copy-start | bytes 1572868
  93.3 11.6 %copy-start.13 = (f32[8,128,128]{2,1,0:T(8,128)S(1)}, f32[8,128,128]{2,1,0:T(8,128)}, u32[]{:S(2)}) copy-start(f32[8,128,128]{2,1,0:T(8,128)} %copy-done.12) | copy-start | bytes 1572868
  100.5 14.3 %collective-permute-start.4 = (bf16[8,128,128]{2,1,0:T(8,128)(2,1)S(1)}, bf16[8,128,128]{2,1,0:T(8,128)(2,1)S(1)}, u32[]{:S(2)}, u32[]{:S(2)}) collective-permute-start(bf16[8,128,128]{2,1,0:T(8,128)(2,1)S(1)} %get-tuple-element.55), channel_id=1, source_target_pairs={{0,16},{2,18},{4,20},{6,22},{8,24},{10,26},{12,28},{14,30},{1,17},... | collective-permute-start | bytes 786440 | tf_op jit(solution)/shard_map/ppermute | solution.py:19
  106.9 11.5 %copy-start.19 = (f32[8,128,128]{2,1,0:T(8,128)S(1)}, f32[8,128,128]{2,1,0:T(8,128)}, u32[]{:S(2)}) copy-start(f32[8,128,128]{2,1,0:T(8,128)} %copy-done.18) | copy-start | bytes 1572868
  106.9 11.5 %copy-start.21 = (f32[8,128,128]{2,1,0:T(8,128)S(1)}, f32[8,128,128]{2,1,0:T(8,128)}, u32[]{:S(2)}) copy-start(f32[8,128,128]{2,1,0:T(8,128)} %copy-done.20) | copy-start | bytes 1572868
  106.9 11.5 %copy-start.23 = (f32[8,128,128]{2,1,0:T(8,128)S(1)}, f32[8,128,128]{2,1,0:T(8,128)}, u32[]{:S(2)}) copy-start(f32[8,128,128]{2,1,0:T(8,128)} %copy-done.22) | copy-start | bytes 1572868
  115.1 8.6 %collective-permute-start.5 = (bf16[8,128,128]{2,1,0:T(8,128)(2,1)S(1)}, bf16[8,128,128]{2,1,0:T(8,128)(2,1)S(1)}, u32[]{:S(2)}, u32[]{:S(2)}) collective-permute-start(bf16[8,128,128]{2,1,0:T(8,128)(2,1)S(1)} %fusion.49), channel_id=1, source_target_pairs={{0,2},{2,4},{4,6},{6,8},{8,10},{10,12},{12,14},{14,16},{16,18},{18... | collective-permute-start | bytes 786440 | tf_op jit(solution)/shard_map/ppermute | solution.py:19
  124.8 1.0 copy-start.28
  125.4 2.2 copy-start.17
  127.7 5.4 %copy-start.40 = (s32[128,10]{0,1:T(8,128)S(1)}, s32[128,10]{0,1:T(8,128)}, u32[]{:S(2)}) copy-start(s32[128,10]{0,1:T(8,128)} %param.28) | copy-start | bytes 15364
  127.7 5.5 %copy-start.41 = (f32[128,10]{0,1:T(8,128)S(1)}, f32[128,10]{0,1:T(8,128)}, u32[]{:S(2)}) copy-start(f32[128,10]{0,1:T(8,128)} %param.29) | copy-start | bytes 15364
  127.7 7.6 %copy-start.27 = (bf16[128,2048]{1,0:T(8,128)(2,1)S(1)}, bf16[128,2048]{1,0:T(8,128)(2,1)}, u32[]{:S(2)}) copy-start(bf16[128,2048]{1,0:T(8,128)(2,1)} %param.26) | copy-start | bytes 1572868
  128.9 1.4 copy-start.7
  130.3 6.7 %copy-start.39 = (f32[2048]{0:T(1024)S(1)}, f32[2048]{0:T(1024)}, u32[]{:S(2)}) copy-start(f32[2048]{0:T(1024)} %param.27) | copy-start | bytes 24580
  130.4 4.9 %collective-permute-start.6 = (bf16[128,2048]{1,0:T(8,128)(2,1)S(1)}, bf16[128,2048]{1,0:T(8,128)(2,1)}, u32[]{:S(2)}, u32[]{:S(2)}) collective-permute-start(bf16[128,2048]{1,0:T(8,128)(2,1)S(1)} %fusion.94), channel_id=1, source_target_pairs={{0,1},{1,0},{2,3},{3,2},{4,5},{5,4},{6,7},{7,6},{8,9},{9,8},{10,11... | collective-permute-start | bytes 1572872 | tf_op jit(solution)/shard_map/ppermute | solution.py:289
  133.1 2.1 copy-start.37
  135.3 2.0 copy-start.31
  135.3 2.0 copy-start.35
  135.3 2.0 copy-start.36
  138.3 14.5 %collective-permute-start.7 = (bf16[128,2176]{1,0:T(8,128)(2,1)}, bf16[128,2176]{1,0:T(8,128)(2,1)S(1)}, u32[]{:S(2)}, u32[]{:S(2)}) collective-permute-start(bf16[128,2176]{1,0:T(8,128)(2,1)} %concatenate.26), channel_id=1, source_target_pairs={{0,24},{8,0},{16,8},{24,16},{1,25},{9,1},{17,9},{25,17},{2,26},{10... | collective-permute-start | bytes 1671176 | tf_op jit(solution)/shard_map/ppermute | solution.py:328
  138.3 39.4 %collective-permute-start.8 = (bf16[128,2176]{1,0:T(8,128)(2,1)}, bf16[128,2176]{1,0:T(8,128)(2,1)S(1)}, u32[]{:S(2)}, u32[]{:S(2)}) collective-permute-start(bf16[128,2176]{1,0:T(8,128)(2,1)} %concatenate.26), channel_id=1, source_target_pairs={{0,16},{8,24},{16,0},{24,8},{1,17},{9,25},{17,1},{25,9},{2,18},{10... | collective-permute-start | bytes 1671176 | tf_op jit(solution)/shard_map/ppermute | solution.py:328
  141.4 48.2 %collective-permute-start.9 = (bf16[128,2176]{1,0:T(8,128)(2,1)}, bf16[128,2176]{1,0:T(8,128)(2,1)S(1)}, u32[]{:S(2)}, u32[]{:S(2)}) collective-permute-start(bf16[128,2176]{1,0:T(8,128)(2,1)} %concatenate.26), channel_id=1, source_target_pairs={{0,8},{8,16},{16,24},{24,0},{1,9},{9,17},{17,25},{25,1},{2,10},{10... | collective-permute-start | bytes 1671176 | tf_op jit(solution)/shard_map/ppermute | solution.py:328
  189.7 1.2 copy-start.26
  193.5 9.5 %copy-start.34 = (s32[384,10]{0,1:T(8,128)}, s32[384,10]{0,1:T(8,128)S(1)}, u32[]{:S(2)}) copy-start(s32[384,10]{0,1:T(8,128)S(1)} %copy.167) | copy-start | bytes 46084
  207.6 8.6 %copy-start.33 = (s32[128,10]{1,0:T(8,128)S(1)}, s32[128,10]{1,0:T(8,128)}, u32[]{:S(2)}) copy-start(s32[128,10]{1,0:T(8,128)} %get-tuple-element.11) | copy-start | bytes 15364
  207.6 9.1 %copy-start.32 = (bf16[128,10]{1,0:T(8,128)(2,1)S(1)}, bf16[128,10]{1,0:T(8,128)(2,1)}, u32[]{:S(2)}) copy-start(bf16[128,10]{1,0:T(8,128)(2,1)} %get-tuple-element.12) | copy-start | bytes 7684
  207.6 64.7 %all-to-all-start.2 = ((bf16[8,150,2048]{2,1,0:T(8,128)(2,1)}), bf16[8,150,2048]{2,1,0:T(8,128)(2,1)}, u32[]{:S(2)}, u32[]{:S(2)}) async-start(bf16[8,150,2048]{2,1,0:T(8,128)(2,1)} %reshape.250), calls=%async_computation.2 | async-start | bytes 9961472 | tf_op jit(solution)/shard_map/all_to_all | solution.py:365
  272.3 28.4 %all-to-all-start = ((bf16[8,50,2048]{2,1,0:T(8,128)(2,1)}), bf16[8,50,2048]{2,1,0:T(8,128)(2,1)}, u32[]{:S(2)}, u32[]{:S(2)}) async-start(bf16[8,50,2048]{2,1,0:T(8,128)(2,1)} %reshape.247), calls=%async_computation | async-start | bytes 3670016 | tf_op jit(solution)/shard_map/all_to_all | solution.py:365
  300.5 6.3 %copy-start.30 = (bf16[384,10]{1,0:T(8,128)(2,1)S(1)}, bf16[384,10]{1,0:T(8,128)(2,1)}, u32[]{:S(2)}) copy-start(bf16[384,10]{1,0:T(8,128)(2,1)} %get-tuple-element.18) | copy-start | bytes 23044
  300.5 7.0 %copy-start.29 = (bf16[384,10]{1,0:T(8,128)(2,1)S(1)}, bf16[384,10]{1,0:T(8,128)(2,1)}, u32[]{:S(2)}) copy-start(bf16[384,10]{1,0:T(8,128)(2,1)} %get-tuple-element.17) | copy-start | bytes 23044
  300.6 62.2 %all-to-all-start.3 = ((bf16[8,150,2048]{2,1,0:T(8,128)(2,1)}), bf16[8,150,2048]{2,1,0:T(8,128)(2,1)}, u32[]{:S(2)}, u32[]{:S(2)}) async-start(bf16[8,150,2048]{2,1,0:T(8,128)(2,1)} %reshape_stack_reshape.7), calls=%async_computation.3 | async-start | bytes 9961472 | tf_op jit(solution)/shard_map/all_to_all | solution.py:376
  362.8 28.4 %all-to-all-start.1 = ((bf16[8,50,2048]{2,1,0:T(8,128)(2,1)}), bf16[8,50,2048]{2,1,0:T(8,128)(2,1)}, u32[]{:S(2)}, u32[]{:S(2)}) async-start(bf16[8,50,2048]{2,1,0:T(8,128)(2,1)} %reshape_stack_reshape.6), calls=%async_computation.1 | async-start | bytes 3670016 | tf_op jit(solution)/shard_map/all_to_all | solution.py:376
  373.5 5.1 %copy-start.1 = (bf16[1200,2048]{1,0:T(8,128)(2,1)S(1)}, bf16[1200,2048]{1,0:T(8,128)(2,1)}, u32[]{:S(2)}) copy-start(bf16[1200,2048]{1,0:T(8,128)(2,1)} %reshape.251) | copy-start | bytes 14745604
  381.1 4.5 %copy-start.38 = (bf16[128,10]{0,1:T(8,128)(2,1)S(1)}, bf16[128,10]{0,1:T(8,128)(2,1)}, u32[]{:S(2)}) copy-start(bf16[128,10]{0,1:T(8,128)(2,1)} %copy-done.37) | copy-start | bytes 7684
  382.3 13.8 %collective-permute-start.10 = (bf16[128,2048]{1,0:T(8,128)(2,1)}, bf16[128,2048]{1,0:T(8,128)(2,1)S(1)}, u32[]{:S(2)}, u32[]{:S(2)}) collective-permute-start(bf16[128,2048]{1,0:T(8,128)(2,1)} %get-tuple-element.20), channel_id=1, source_target_pairs={{0,8},{8,16},{16,24},{24,0},{1,9},{9,17},{17,25},{25,1},{2,10},{10... | collective-permute-start | bytes 1572872 | tf_op jit(solution)/shard_map/ppermute | solution.py:392
  384.4 45.0 %collective-permute-start.11 = (bf16[128,2048]{1,0:T(8,128)(2,1)}, bf16[128,2048]{1,0:T(8,128)(2,1)}, u32[]{:S(2)}, u32[]{:S(2)}) collective-permute-start(bf16[128,2048]{1,0:T(8,128)(2,1)} %get-tuple-element.22), channel_id=1, source_target_pairs={{0,16},{8,24},{16,0},{24,8},{1,17},{9,25},{17,1},{25,9},{2,18},{10... | collective-permute-start | bytes 1572872 | tf_op jit(solution)/shard_map/ppermute | solution.py:392
  384.6 46.4 %collective-permute-start.12 = (bf16[128,2048]{1,0:T(8,128)(2,1)}, bf16[128,2048]{1,0:T(8,128)(2,1)}, u32[]{:S(2)}, u32[]{:S(2)}) collective-permute-start(bf16[128,2048]{1,0:T(8,128)(2,1)} %get-tuple-element.21), channel_id=1, source_target_pairs={{0,24},{8,0},{16,8},{24,16},{1,25},{9,1},{17,9},{25,17},{2,26},{10... | collective-permute-start | bytes 1572872 | tf_op jit(solution)/shard_map/ppermute | solution.py:392
  393.8 37.2 %copy-start.4 = (bf16[400,2048]{1,0:T(8,128)(2,1)S(1)}, bf16[400,2048]{1,0:T(8,128)(2,1)}, u32[]{:S(2)}) copy-start(bf16[400,2048]{1,0:T(8,128)(2,1)} %reshape.248) | copy-start | bytes 4915204

commit v2 on v0

--- a/solution.py
+++ b/solution.py
@@ -10,7 +10,7 @@
 CTX = ("ctx_hi", "ctx_lo")
 
 
-HIGHEST = lax.Precision.HIGHEST
+HIGHEST = lax.Precision.HIGH
 
 
 def passed_along(block, axis, distance):

time: 400 us -> 386 us (0.965)
  matrix products: 97.6 us -> 79.1 us
    dot_general x17, matrix products: 27 us -> 14.7 us  [precise_dot(): jnp.dot(left, right, precision=HIGHEST, preferred_element_type=jnp.float32)]
where the time goes in v2:
time: 386 us; the launch traced here: 380 us
  waiting for transfers between devices  133 us (34%)
  starting transfers between devices  86.4 us (22%)
  matrix products  79.1 us (20%)
  local copies, waits for them, and re-layouts  59.9 us (16%)
  other arithmetic  19.4 us (5%)
    all_to_all x4, waiting for transfers between devices, per_device(): lax.all_to_all(outgoing, level_axes, split_axis=0, concat_axis=0, tiled=T...  51 us
    all_to_all x4, waiting for transfers between devices, per_device(): lax.all_to_all(answered, level_axes, split_axis=0, concat_axis=0, tiled=T...  33 us
    ppermute x6, waiting for transfers between devices, passed_along(): return lax.ppermute(block, axis, route)  31.6 us
    ppermute x6, starting transfers between devices, passed_along(): return lax.ppermute(block, axis, route)  28 us
    dot_general x4, matrix products, expert_apply_rows(): gate_up = jnp.dot(rows_in, up_matrix, preferred_element_type=jnp.float32)  18.1 us
    all_to_all x4, starting transfers between devices, per_device(): lax.all_to_all(answered, level_axes, split_axis=0, concat_axis=0, tiled=T...  17.6 us
    all_to_all x4, starting transfers between devices, per_device(): lax.all_to_all(outgoing, level_axes, split_axis=0, concat_axis=0, tiled=T...  17.3 us
    ppermute x3, starting transfers between devices, per_device(): lax.ppermute(packed, 'ctx_hi', [(i, (i - turn) % levels) for i in range(l...  17.2 us
  transfers between devices with their start and end apart: 21, of which 16 were waited for; matrix products, arithmetic and copies ran while one was open for 30% of the time, Pallas kernels for 0%

profile of v2, /device:TPU:0, one launch (start us, length us, event | category | flops | bytes accessed | tf_op | source)
XLA Modules:
  0.0 380.3 jit_solution(9592379382474532730)
XLA Ops:
  1.6 4.8 %collective-permute-start = (bf16[3,2048]{1,0:T(4,128)(2,1)S(1)}, bf16[3,2048]{1,0:T(4,128)(2,1)S(1)}, u32[]{:S(2)}, u32[]{:S(2)}) collective-permute-start(bf16[3,2048]{1,0:T(4,128)(2,1)S(1)} %pad_maximum_fusion.5), channel_id=1, source_target_pairs={{0,2},{2,4},{4,6},{6,8},{8,10},{10,12},{12,14},{14,16},{16,18},{18... | collective-permute-start | bytes 36872 | tf_op jit(solution)/shard_map/ppermute | solution.py:19
  14.5 2.9 multiply_bitcast_fusion
  35.3 2.1 multiply_subtract_fusion
  42.3 4.2 %collective-permute-start.1 = (bf16[2,8,128,128]{3,2,1,0:T(8,128)(2,1)}, bf16[2,8,128,128]{3,2,1,0:T(8,128)(2,1)}, u32[]{:S(2)}, u32[]{:S(2)}) collective-permute-start(bf16[2,8,128,128]{3,2,1,0:T(8,128)(2,1)} %pad_maximum_fusion.2), channel_id=1, source_target_pairs={{0,2},{2,4},{4,6},{6,8},{8,10},{10,12},{12,14},{14,16},{16,18},{18... | collective-permute-start | bytes 1572872 | tf_op jit(solution)/shard_map/ppermute | solution.py:19
  46.7 10.2 %collective-permute-done.1 = bf16[2,8,128,128]{3,2,1,0:T(8,128)(2,1)} collective-permute-done((bf16[2,8,128,128]{3,2,1,0:T(8,128)(2,1)}, bf16[2,8,128,128]{3,2,1,0:T(8,128)(2,1)}, u32[]{:S(2)}, u32[]{:S(2)}) %collective-permute-start.1) | collective-permute-done | bytes 524320 | tf_op jit(solution)/shard_map/ppermute | solution.py:19
  60.0 5.3 %collective-permute-start.2 = (bf16[2,8,128,128]{3,2,1,0:T(8,128)(2,1)S(1)}, bf16[2,8,128,128]{3,2,1,0:T(8,128)(2,1)S(1)}, u32[]{:S(2)}, u32[]{:S(2)}) collective-permute-start(bf16[2,8,128,128]{3,2,1,0:T(8,128)(2,1)S(1)} %pad_maximum_fusion.3), channel_id=1, source_target_pairs={{0,4},{2,6},{4,8},{6,10},{8,12},{10,14},{12,16},{14,18},{16,20},{1... | collective-permute-start | bytes 1572872 | tf_op jit(solution)/shard_map/ppermute | solution.py:19
  66.5 8.7 %collective-permute-done.2 = bf16[2,8,128,128]{3,2,1,0:T(8,128)(2,1)S(1)} collective-permute-done((bf16[2,8,128,128]{3,2,1,0:T(8,128)(2,1)S(1)}, bf16[2,8,128,128]{3,2,1,0:T(8,128)(2,1)S(1)}, u32[]{:S(2)}, u32[]{:S(2)}) %collective-permute-start.2) | collective-permute-done | bytes 524320 | tf_op jit(solution)/shard_map/ppermute | solution.py:19
  76.0 6.6 %collective-permute-start.3 = (bf16[2,8,128,128]{3,2,1,0:T(8,128)(2,1)S(1)}, bf16[2,8,128,128]{3,2,1,0:T(8,128)(2,1)S(1)}, u32[]{:S(2)}, u32[]{:S(2)}) collective-permute-start(bf16[2,8,128,128]{3,2,1,0:T(8,128)(2,1)S(1)} %pad_maximum_fusion.4), channel_id=1, source_target_pairs={{0,8},{2,10},{4,12},{6,14},{8,16},{10,18},{12,20},{14,22},{16,24},... | collective-permute-start | bytes 1572872 | tf_op jit(solution)/shard_map/ppermute | solution.py:19
  84.1 7.4 %collective-permute-done.3 = bf16[2,8,128,128]{3,2,1,0:T(8,128)(2,1)S(1)} collective-permute-done((bf16[2,8,128,128]{3,2,1,0:T(8,128)(2,1)S(1)}, bf16[2,8,128,128]{3,2,1,0:T(8,128)(2,1)S(1)}, u32[]{:S(2)}, u32[]{:S(2)}) %collective-permute-start.3) | collective-permute-done | bytes 524320 | tf_op jit(solution)/shard_map/ppermute | solution.py:19
  91.8 5.4 %collective-permute-start.4 = (bf16[8,128,128]{2,1,0:T(8,128)(2,1)S(1)}, bf16[8,128,128]{2,1,0:T(8,128)(2,1)S(1)}, u32[]{:S(2)}, u32[]{:S(2)}) collective-permute-start(bf16[8,128,128]{2,1,0:T(8,128)(2,1)S(1)} %get-tuple-element.62), channel_id=1, source_target_pairs={{0,16},{2,18},{4,20},{6,22},{8,24},{10,26},{12,28},{14,30},{1,17},... | collective-permute-start | bytes 786440 | tf_op jit(solution)/shard_map/ppermute | solution.py:19
  98.6 2.5 collective-permute-done.4
  104.2 2.7 collective-permute-done.5
  118.3 10.7 %collective-permute-start.11 = (bf16[128,2176]{1,0:T(8,128)(2,1)}, bf16[128,2176]{1,0:T(8,128)(2,1)}, u32[]{:S(2)}, u32[]{:S(2)}) collective-permute-start(bf16[128,2176]{1,0:T(8,128)(2,1)} %concatenate.23), channel_id=1, source_target_pairs={{0,8},{8,16},{16,24},{24,0},{1,9},{9,17},{17,25},{25,1},{2,10},{10... | collective-permute-start | bytes 1671176 | tf_op jit(solution)/shard_map/ppermute | solution.py:332
  131.2 2.6 reshape.262
  133.8 4.3 %all-to-all-start = ((bf16[8,50,2048]{2,1,0:T(8,128)(2,1)}), bf16[8,50,2048]{2,1,0:T(8,128)(2,1)}, u32[]{:S(2)}, u32[]{:S(2)}) async-start(bf16[8,50,2048]{2,1,0:T(8,128)(2,1)} %reshape.262), calls=%async_computation | async-start | bytes 3670016 | tf_op jit(solution)/shard_map/all_to_all | solution.py:356
  138.1 3.4 collective-permute-start.9
  141.6 4.1 %collective-permute-done.11 = bf16[128,2176]{1,0:T(8,128)(2,1)} collective-permute-done((bf16[128,2176]{1,0:T(8,128)(2,1)}, bf16[128,2176]{1,0:T(8,128)(2,1)}, u32[]{:S(2)}, u32[]{:S(2)}) %collective-permute-start.11) | collective-permute-done | bytes 557088 | tf_op jit(solution)/shard_map/ppermute | solution.py:332
  148.2 2.8 convolution_convert_fusion.4
  151.0 2.6 reshape.268
  153.7 8.3 %all-to-all-done = bf16[8,50,2048]{2,1,0:T(8,128)(2,1)} async-done(((bf16[8,50,2048]{2,1,0:T(8,128)(2,1)}), bf16[8,50,2048]{2,1,0:T(8,128)(2,1)}, u32[]{:S(2)}, u32[]{:S(2)}) %all-to-all-start) | async-done | bytes 1638432 | tf_op jit(solution)/shard_map/all_to_all | solution.py:356
  162.0 4.3 %all-to-all-start.6 = ((bf16[8,50,2048]{2,1,0:T(8,128)(2,1)}), bf16[8,50,2048]{2,1,0:T(8,128)(2,1)}, u32[]{:S(2)}, u32[]{:S(2)}) async-start(bf16[8,50,2048]{2,1,0:T(8,128)(2,1)} %reshape.268), calls=%async_computation.6 | async-start | bytes 3670016 | tf_op jit(solution)/shard_map/all_to_all | solution.py:356
  166.3 3.1 collective-permute-start.7
  172.2 2.6 reshape.266
  174.8 15.3 %all-to-all-done.6 = bf16[8,50,2048]{2,1,0:T(8,128)(2,1)} async-done(((bf16[8,50,2048]{2,1,0:T(8,128)(2,1)}), bf16[8,50,2048]{2,1,0:T(8,128)(2,1)}, u32[]{:S(2)}, u32[]{:S(2)}) %all-to-all-start.6) | async-done | bytes 1638432 | tf_op jit(solution)/shard_map/all_to_all | solution.py:356
  190.1 4.3 %all-to-all-start.4 = ((bf16[8,50,2048]{2,1,0:T(8,128)(2,1)}), bf16[8,50,2048]{2,1,0:T(8,128)(2,1)}, u32[]{:S(2)}, u32[]{:S(2)}) async-start(bf16[8,50,2048]{2,1,0:T(8,128)(2,1)} %reshape.266), calls=%async_computation.4 | async-start | bytes 3670016 | tf_op jit(solution)/shard_map/all_to_all | solution.py:356
  197.2 2.9 convolution_convert_fusion.6
  200.1 2.6 reshape.264
  202.6 15.7 %all-to-all-done.4 = bf16[8,50,2048]{2,1,0:T(8,128)(2,1)} async-done(((bf16[8,50,2048]{2,1,0:T(8,128)(2,1)}), bf16[8,50,2048]{2,1,0:T(8,128)(2,1)}, u32[]{:S(2)}, u32[]{:S(2)}) %all-to-all-start.4) | async-done | bytes 1638432 | tf_op jit(solution)/shard_map/all_to_all | solution.py:356
  218.3 4.3 %all-to-all-start.2 = ((bf16[8,50,2048]{2,1,0:T(8,128)(2,1)}), bf16[8,50,2048]{2,1,0:T(8,128)(2,1)}, u32[]{:S(2)}, u32[]{:S(2)}) async-start(bf16[8,50,2048]{2,1,0:T(8,128)(2,1)} %reshape.264), calls=%async_computation.2 | async-start | bytes 3670016 | tf_op jit(solution)/shard_map/all_to_all | solution.py:356
  222.7 2.7 reshape_squeeze_reshape.15
  225.3 4.5 %fusion = f32[400,1024]{1,0:T(8,128)S(1)} fusion(bf16[400,2048]{1,0:T(8,128)(2,1)} %reshape_squeeze_reshape.15, bf16[1,2048,1024]{2,1,0:T(8,128)(2,1)} %param.30), kind=kOutput, calls=%fused_computation | convolution fusion | flops 1677721600 | bytes 7471104 | tf_op jit(solution)/shard_map/dot_general | solution.py:201
  229.9 2.2 convolution_convert_fusion
  232.1 2.7 reshape_stack_reshape.15
  234.8 11.7 %all-to-all-done.2 = bf16[8,50,2048]{2,1,0:T(8,128)(2,1)} async-done(((bf16[8,50,2048]{2,1,0:T(8,128)(2,1)}), bf16[8,50,2048]{2,1,0:T(8,128)(2,1)}, u32[]{:S(2)}, u32[]{:S(2)}) %all-to-all-start.2) | async-done | bytes 1638432 | tf_op jit(solution)/shard_map/all_to_all | solution.py:356
  246.5 4.3 %all-to-all-start.7 = ((bf16[8,50,2048]{2,1,0:T(8,128)(2,1)}), bf16[8,50,2048]{2,1,0:T(8,128)(2,1)}, u32[]{:S(2)}, u32[]{:S(2)}) async-start(bf16[8,50,2048]{2,1,0:T(8,128)(2,1)} %reshape_stack_reshape.15), calls=%async_computation.7 | async-start | bytes 3670016 | tf_op jit(solution)/shard_map/all_to_all | solution.py:367
  251.0 2.7 reshape_squeeze_reshape.14
  253.7 4.5 %fusion.2 = f32[400,1024]{1,0:T(8,128)S(1)} fusion(bf16[400,2048]{1,0:T(8,128)(2,1)} %reshape_squeeze_reshape.14, bf16[1,2048,1024]{2,1,0:T(8,128)(2,1)} %param.30), kind=kOutput, calls=%fused_computation.2 | convolution fusion | flops 1677721600 | bytes 7471104 | tf_op jit(solution)/shard_map/dot_general | solution.py:201
  258.2 2.3 convolution_convert_fusion.1
  260.5 2.6 reshape_stack_reshape.14
  263.0 11.6 %all-to-all-done.7 = bf16[8,50,2048]{2,1,0:T(8,128)(2,1)} async-done(((bf16[8,50,2048]{2,1,0:T(8,128)(2,1)}), bf16[8,50,2048]{2,1,0:T(8,128)(2,1)}, u32[]{:S(2)}, u32[]{:S(2)}) %all-to-all-start.7) | async-done | bytes 1638432 | tf_op jit(solution)/shard_map/all_to_all | solution.py:367
  274.7 4.6 %all-to-all-start.5 = ((bf16[8,50,2048]{2,1,0:T(8,128)(2,1)}), bf16[8,50,2048]{2,1,0:T(8,128)(2,1)}, u32[]{:S(2)}, u32[]{:S(2)}) async-start(bf16[8,50,2048]{2,1,0:T(8,128)(2,1)} %reshape_stack_reshape.14), calls=%async_computation.5 | async-start | bytes 3670016 | tf_op jit(solution)/shard_map/all_to_all | solution.py:367
  280.9 2.6 reshape_squeeze_reshape.12
  283.5 2.6 reshape_squeeze_reshape.13
  286.1 4.5 %fusion.4 = f32[400,1024]{1,0:T(8,128)S(1)} fusion(bf16[400,2048]{1,0:T(8,128)(2,1)} %reshape_squeeze_reshape.13, bf16[1,2048,1024]{2,1,0:T(8,128)(2,1)} %param.30), kind=kOutput, calls=%fused_computation.4 | convolution fusion | flops 1677721600 | bytes 7471104 | tf_op jit(solution)/shard_map/dot_general | solution.py:201
  290.7 2.2 convolution_convert_fusion.2
  292.9 2.7 reshape_stack_reshape.13
  295.6 7.6 %all-to-all-done.5 = bf16[8,50,2048]{2,1,0:T(8,128)(2,1)} async-done(((bf16[8,50,2048]{2,1,0:T(8,128)(2,1)}), bf16[8,50,2048]{2,1,0:T(8,128)(2,1)}, u32[]{:S(2)}, u32[]{:S(2)}) %all-to-all-start.5) | async-done | bytes 1638432 | tf_op jit(solution)/shard_map/all_to_all | solution.py:367
  303.1 4.3 %all-to-all-start.3 = ((bf16[8,50,2048]{2,1,0:T(8,128)(2,1)}), bf16[8,50,2048]{2,1,0:T(8,128)(2,1)}, u32[]{:S(2)}, u32[]{:S(2)}) async-start(bf16[8,50,2048]{2,1,0:T(8,128)(2,1)} %reshape_stack_reshape.13), calls=%async_computation.3 | async-start | bytes 3670016 | tf_op jit(solution)/shard_map/all_to_all | solution.py:367
  307.5 4.5 %fusion.6 = f32[400,1024]{1,0:T(8,128)S(1)} fusion(bf16[400,2048]{1,0:T(8,128)(2,1)} %reshape_squeeze_reshape.12, bf16[1,2048,1024]{2,1,0:T(8,128)(2,1)} %param.30), kind=kOutput, calls=%fused_computation.6 | convolution fusion | flops 1677721600 | bytes 7471104 | tf_op jit(solution)/shard_map/dot_general | solution.py:201
  312.0 2.2 convolution_convert_fusion.3
  314.3 2.6 reshape_stack_reshape.12
  316.9 2.6 reshape.269
  322.8 2.8 collective-permute-start.12
  325.6 2.6 reshape.267
  328.3 3.1 all-to-all-done.3
  331.3 4.3 %all-to-all-start.1 = ((bf16[8,50,2048]{2,1,0:T(8,128)(2,1)}), bf16[8,50,2048]{2,1,0:T(8,128)(2,1)}, u32[]{:S(2)}, u32[]{:S(2)}) async-start(bf16[8,50,2048]{2,1,0:T(8,128)(2,1)} %reshape_stack_reshape.12), calls=%async_computation.1 | async-start | bytes 3670016 | tf_op jit(solution)/shard_map/all_to_all | solution.py:367
  335.7 2.0 fusion.247
  339.0 3.4 collective-permute-start.10
  342.4 2.6 reshape.265
  345.0 2.0 fusion.246
  348.8 10.7 %all-to-all-done.1 = bf16[8,50,2048]{2,1,0:T(8,128)(2,1)} async-done(((bf16[8,50,2048]{2,1,0:T(8,128)(2,1)}), bf16[8,50,2048]{2,1,0:T(8,128)(2,1)}, u32[]{:S(2)}, u32[]{:S(2)}) %all-to-all-start.1) | async-done | bytes 1638432 | tf_op jit(solution)/shard_map/all_to_all | solution.py:367
  359.5 2.6 reshape.263
  364.2 13.0 %collective-permute-done.10 = bf16[128,2048]{1,0:T(8,128)(2,1)} collective-permute-done((bf16[128,2048]{1,0:T(8,128)(2,1)}, bf16[128,2048]{1,0:T(8,128)(2,1)}, u32[]{:S(2)}, u32[]{:S(2)}) %collective-permute-start.10) | collective-permute-done | bytes 524320 | tf_op jit(solution)/shard_map/ppermute | solution.py:381
  377.1 2.7 fusion.66
  (265 shorter events, 74.5 us)
Async XLA Ops:
  0.0 229.9 %copy-start = (bf16[1,512,2048]{2,1,0:T(8,128)(2,1)S(1)}, bf16[1,512,2048]{2,1,0:T(8,128)(2,1)}, u32[]{:S(2)}) copy-start(bf16[1,512,2048]{2,1,0:T(8,128)(2,1)} %param.31) | copy-start | bytes 6291460
  0.0 14.2 %copy-start.26 = (bf16[256,1024]{1,0:T(8,128)(2,1)S(1)}, bf16[256,1024]{1,0:T(8,128)(2,1)}, u32[]{:S(2)}) copy-start(bf16[256,1024]{1,0:T(8,128)(2,1)} %param.17) | copy-start | bytes 1572868
  1.6 12.6 %collective-permute-start = (bf16[3,2048]{1,0:T(4,128)(2,1)S(1)}, bf16[3,2048]{1,0:T(4,128)(2,1)S(1)}, u32[]{:S(2)}, u32[]{:S(2)}) collective-permute-start(bf16[3,2048]{1,0:T(4,128)(2,1)S(1)} %pad_maximum_fusion.5), channel_id=1, source_target_pairs={{0,2},{2,4},{4,6},{6,8},{8,10},{10,12},{12,14},{14,16},{16,18},{18... | collective-permute-start | bytes 36872 | tf_op jit(solution)/shard_map/ppermute | solution.py:19
  29.6 1.2 copy-start.17
  33.5 1.9 copy-start.1
  37.7 1.2 copy-start.23
  38.1 0.8 copy-start.10
  38.5 1.2 copy-start.12
  38.9 1.2 copy-start.14
  39.3 1.2 copy-start.19
  39.8 0.9 copy-start.21
  40.2 2.1 copy-start.16
  40.2 6.3 %copy-start.36 = (s32[128,10]{0,1:T(8,128)S(1)}, s32[128,10]{0,1:T(8,128)}, u32[]{:S(2)}) copy-start(s32[128,10]{0,1:T(8,128)} %param.28) | copy-start | bytes 15364
  40.6 0.8 copy-start.7
  42.3 14.6 %collective-permute-start.1 = (bf16[2,8,128,128]{3,2,1,0:T(8,128)(2,1)}, bf16[2,8,128,128]{3,2,1,0:T(8,128)(2,1)}, u32[]{:S(2)}, u32[]{:S(2)}) collective-permute-start(bf16[2,8,128,128]{3,2,1,0:T(8,128)(2,1)} %pad_maximum_fusion.2), channel_id=1, source_target_pairs={{0,2},{2,4},{4,6},{6,8},{8,10},{10,12},{12,14},{14,16},{16,18},{18... | collective-permute-start | bytes 1572872 | tf_op jit(solution)/shard_map/ppermute | solution.py:19
  46.6 11.9 %copy-start.8 = (f32[8,128,128]{2,1,0:T(8,128)S(1)}, f32[8,128,128]{2,1,0:T(8,128)}, u32[]{:S(2)}) copy-start(f32[8,128,128]{2,1,0:T(8,128)} %copy-done.7) | copy-start | bytes 1572868
  58.5 6.8 %copy-start.38 = (f32[128]{0:T(128)S(1)}, f32[128]{0:T(128)}, u32[]{:S(2)}) copy-start(f32[128]{0:T(128)} %param.24) | copy-start | bytes 1540
  58.5 6.9 %copy-start.25 = (f32[256,4,128]{2,1,0:T(4,128)S(1)}, f32[256,4,128]{2,1,0:T(4,128)}, u32[]{:S(2)}) copy-start(f32[256,4,128]{2,1,0:T(4,128)} %get-tuple-element.24) | copy-start | bytes 1572868
  60.0 15.3 %collective-permute-start.2 = (bf16[2,8,128,128]{3,2,1,0:T(8,128)(2,1)S(1)}, bf16[2,8,128,128]{3,2,1,0:T(8,128)(2,1)S(1)}, u32[]{:S(2)}, u32[]{:S(2)}) collective-permute-start(bf16[2,8,128,128]{3,2,1,0:T(8,128)(2,1)S(1)} %pad_maximum_fusion.3), channel_id=1, source_target_pairs={{0,4},{2,6},{4,8},{6,10},{8,12},{10,14},{12,16},{14,18},{16,20},{1... | collective-permute-start | bytes 1572872 | tf_op jit(solution)/shard_map/ppermute | solution.py:19
  75.6 7.0 %copy-start.2 = (f32[8,4,64,256]{3,2,1,0:T(8,128)S(1)}, f32[8,4,64,256]{3,2,1,0:T(8,128)}, u32[]{:S(2)}) copy-start(f32[8,4,64,256]{3,2,1,0:T(8,128)} %copy-done.1) | copy-start | bytes 6291460
  76.0 15.4 %collective-permute-start.3 = (bf16[2,8,128,128]{3,2,1,0:T(8,128)(2,1)S(1)}, bf16[2,8,128,128]{3,2,1,0:T(8,128)(2,1)S(1)}, u32[]{:S(2)}, u32[]{:S(2)}) collective-permute-start(bf16[2,8,128,128]{3,2,1,0:T(8,128)(2,1)S(1)} %pad_maximum_fusion.4), channel_id=1, source_target_pairs={{0,8},{2,10},{4,12},{6,14},{8,16},{10,18},{12,20},{14,22},{16,24},... | collective-permute-start | bytes 1572872 | tf_op jit(solution)/shard_map/ppermute | solution.py:19
  84.0 13.2 %copy-start.11 = (f32[8,128,128]{2,1,0:T(8,128)S(1)}, f32[8,128,128]{2,1,0:T(8,128)}, u32[]{:S(2)}) copy-start(f32[8,128,128]{2,1,0:T(8,128)} %copy-done.10) | copy-start | bytes 1572868
  84.0 13.2 %copy-start.13 = (f32[8,128,128]{2,1,0:T(8,128)S(1)}, f32[8,128,128]{2,1,0:T(8,128)}, u32[]{:S(2)}) copy-start(f32[8,128,128]{2,1,0:T(8,128)} %copy-done.12) | copy-start | bytes 1572868
  84.1 13.2 %copy-start.15 = (f32[8,128,128]{2,1,0:T(8,128)S(1)}, f32[8,128,128]{2,1,0:T(8,128)}, u32[]{:S(2)}) copy-start(f32[8,128,128]{2,1,0:T(8,128)} %copy-done.14) | copy-start | bytes 1572868
  91.8 9.3 %collective-permute-start.4 = (bf16[8,128,128]{2,1,0:T(8,128)(2,1)S(1)}, bf16[8,128,128]{2,1,0:T(8,128)(2,1)S(1)}, u32[]{:S(2)}, u32[]{:S(2)}) collective-permute-start(bf16[8,128,128]{2,1,0:T(8,128)(2,1)S(1)} %get-tuple-element.62), channel_id=1, source_target_pairs={{0,16},{2,18},{4,20},{6,22},{8,24},{10,26},{12,28},{14,30},{1,17},... | collective-permute-start | bytes 786440 | tf_op jit(solution)/shard_map/ppermute | solution.py:19
  98.3 4.8 %copy-start.20 = (f32[8,128,128]{2,1,0:T(8,128)S(1)}, f32[8,128,128]{2,1,0:T(8,128)}, u32[]{:S(2)}) copy-start(f32[8,128,128]{2,1,0:T(8,128)} %copy-done.19) | copy-start | bytes 1572868
  98.3 4.8 %copy-start.22 = (f32[8,128,128]{2,1,0:T(8,128)S(1)}, f32[8,128,128]{2,1,0:T(8,128)}, u32[]{:S(2)}) copy-start(f32[8,128,128]{2,1,0:T(8,128)} %copy-done.21) | copy-start | bytes 1572868
  98.3 4.8 %copy-start.24 = (f32[8,128,128]{2,1,0:T(8,128)S(1)}, f32[8,128,128]{2,1,0:T(8,128)}, u32[]{:S(2)}) copy-start(f32[8,128,128]{2,1,0:T(8,128)} %copy-done.23) | copy-start | bytes 1572868
  101.4 5.5 %collective-permute-start.5 = (bf16[8,128,128]{2,1,0:T(8,128)(2,1)S(1)}, bf16[8,128,128]{2,1,0:T(8,128)(2,1)S(1)}, u32[]{:S(2)}, u32[]{:S(2)}) collective-permute-start(bf16[8,128,128]{2,1,0:T(8,128)(2,1)S(1)} %fusion.58), channel_id=1, source_target_pairs={{0,2},{2,4},{4,6},{6,8},{8,10},{10,12},{12,14},{14,16},{16,18},{18... | collective-permute-start | bytes 786440 | tf_op jit(solution)/shard_map/ppermute | solution.py:19
  107.7 1.0 copy-start.28
  108.4 2.2 copy-start.18
  110.6 2.8 copy-start.37
  110.6 4.8 %copy-start.27 = (bf16[128,2048]{1,0:T(8,128)(2,1)S(1)}, bf16[128,2048]{1,0:T(8,128)(2,1)}, u32[]{:S(2)}) copy-start(bf16[128,2048]{1,0:T(8,128)(2,1)} %param.26) | copy-start | bytes 1572868
  111.9 1.3 copy-start.9
  113.2 3.9 %copy-start.35 = (f32[2048]{0:T(1024)S(1)}, f32[2048]{0:T(1024)}, u32[]{:S(2)}) copy-start(f32[2048]{0:T(1024)} %param.27) | copy-start | bytes 24580
  113.3 2.1 collective-permute-start.6
  113.4 0.6 copy-start.33
  113.4 0.7 copy-start.31
  118.3 27.3 %collective-permute-start.11 = (bf16[128,2176]{1,0:T(8,128)(2,1)}, bf16[128,2176]{1,0:T(8,128)(2,1)}, u32[]{:S(2)}, u32[]{:S(2)}) collective-permute-start(bf16[128,2176]{1,0:T(8,128)(2,1)} %concatenate.23), channel_id=1, source_target_pairs={{0,8},{8,16},{16,24},{24,0},{1,9},{9,17},{17,25},{25,1},{2,10},{10... | collective-permute-start | bytes 1671176 | tf_op jit(solution)/shard_map/ppermute | solution.py:332
  129.1 4.7 %copy-start.29 = (s32[128,10]{0,1:T(8,128)}, s32[128,10]{0,1:T(8,128)S(1)}, u32[]{:S(2)}) copy-start(s32[128,10]{0,1:T(8,128)S(1)} %copy.171) | copy-start | bytes 15364
  133.8 28.2 %all-to-all-start = ((bf16[8,50,2048]{2,1,0:T(8,128)(2,1)}), bf16[8,50,2048]{2,1,0:T(8,128)(2,1)}, u32[]{:S(2)}, u32[]{:S(2)}) async-start(bf16[8,50,2048]{2,1,0:T(8,128)(2,1)} %reshape.262), calls=%async_computation | async-start | bytes 3670016 | tf_op jit(solution)/shard_map/all_to_all | solution.py:356
  138.1 31.3 %collective-permute-start.9 = (bf16[128,2176]{1,0:T(8,128)(2,1)}, bf16[128,2176]{1,0:T(8,128)(2,1)S(1)}, u32[]{:S(2)}, u32[]{:S(2)}) collective-permute-start(bf16[128,2176]{1,0:T(8,128)(2,1)} %concatenate.23), channel_id=1, source_target_pairs={{0,16},{8,24},{16,0},{24,8},{1,17},{9,25},{17,1},{25,9},{2,18},{10... | collective-permute-start | bytes 1671176 | tf_op jit(solution)/shard_map/ppermute | solution.py:332
  162.0 28.2 %all-to-all-start.6 = ((bf16[8,50,2048]{2,1,0:T(8,128)(2,1)}), bf16[8,50,2048]{2,1,0:T(8,128)(2,1)}, u32[]{:S(2)}, u32[]{:S(2)}) async-start(bf16[8,50,2048]{2,1,0:T(8,128)(2,1)} %reshape.268), calls=%async_computation.6 | async-start | bytes 3670016 | tf_op jit(solution)/shard_map/all_to_all | solution.py:356
  166.3 28.2 %collective-permute-start.7 = (bf16[128,2176]{1,0:T(8,128)(2,1)}, bf16[128,2176]{1,0:T(8,128)(2,1)}, u32[]{:S(2)}, u32[]{:S(2)}) collective-permute-start(bf16[128,2176]{1,0:T(8,128)(2,1)} %concatenate.23), channel_id=1, source_target_pairs={{0,24},{8,0},{16,8},{24,16},{1,25},{9,1},{17,9},{25,17},{2,26},{10... | collective-permute-start | bytes 1671176 | tf_op jit(solution)/shard_map/ppermute | solution.py:332
  190.1 28.2 %all-to-all-start.4 = ((bf16[8,50,2048]{2,1,0:T(8,128)(2,1)}), bf16[8,50,2048]{2,1,0:T(8,128)(2,1)}, u32[]{:S(2)}, u32[]{:S(2)}) async-start(bf16[8,50,2048]{2,1,0:T(8,128)(2,1)} %reshape.266), calls=%async_computation.4 | async-start | bytes 3670016 | tf_op jit(solution)/shard_map/all_to_all | solution.py:356
  218.3 28.2 %all-to-all-start.2 = ((bf16[8,50,2048]{2,1,0:T(8,128)(2,1)}), bf16[8,50,2048]{2,1,0:T(8,128)(2,1)}, u32[]{:S(2)}, u32[]{:S(2)}) async-start(bf16[8,50,2048]{2,1,0:T(8,128)(2,1)} %reshape.264), calls=%async_computation.2 | async-start | bytes 3670016 | tf_op jit(solution)/shard_map/all_to_all | solution.py:356
  246.5 28.2 %all-to-all-start.7 = ((bf16[8,50,2048]{2,1,0:T(8,128)(2,1)}), bf16[8,50,2048]{2,1,0:T(8,128)(2,1)}, u32[]{:S(2)}, u32[]{:S(2)}) async-start(bf16[8,50,2048]{2,1,0:T(8,128)(2,1)} %reshape_stack_reshape.15), calls=%async_computation.7 | async-start | bytes 3670016 | tf_op jit(solution)/shard_map/all_to_all | solution.py:367
  274.7 28.5 %all-to-all-start.5 = ((bf16[8,50,2048]{2,1,0:T(8,128)(2,1)}), bf16[8,50,2048]{2,1,0:T(8,128)(2,1)}, u32[]{:S(2)}, u32[]{:S(2)}) async-start(bf16[8,50,2048]{2,1,0:T(8,128)(2,1)} %reshape_stack_reshape.14), calls=%async_computation.5 | async-start | bytes 3670016 | tf_op jit(solution)/shard_map/all_to_all | solution.py:367
  303.1 28.2 %all-to-all-start.3 = ((bf16[8,50,2048]{2,1,0:T(8,128)(2,1)}), bf16[8,50,2048]{2,1,0:T(8,128)(2,1)}, u32[]{:S(2)}, u32[]{:S(2)}) async-start(bf16[8,50,2048]{2,1,0:T(8,128)(2,1)} %reshape_stack_reshape.13), calls=%async_computation.3 | async-start | bytes 3670016 | tf_op jit(solution)/shard_map/all_to_all | solution.py:367
  319.5 2.0 copy-start.5
  322.8 41.3 %collective-permute-start.12 = (bf16[128,2048]{1,0:T(8,128)(2,1)}, bf16[128,2048]{1,0:T(8,128)(2,1)S(1)}, u32[]{:S(2)}, u32[]{:S(2)}) collective-permute-start(bf16[128,2048]{1,0:T(8,128)(2,1)} %fusion.12), channel_id=1, source_target_pairs={{0,24},{8,0},{16,8},{24,16},{1,25},{9,1},{17,9},{25,17},{2,26},{10... | collective-permute-start | bytes 1572872 | tf_op jit(solution)/shard_map/ppermute | solution.py:381
  331.3 28.2 %all-to-all-start.1 = ((bf16[8,50,2048]{2,1,0:T(8,128)(2,1)}), bf16[8,50,2048]{2,1,0:T(8,128)(2,1)}, u32[]{:S(2)}, u32[]{:S(2)}) async-start(bf16[8,50,2048]{2,1,0:T(8,128)(2,1)} %reshape_stack_reshape.12), calls=%async_computation.1 | async-start | bytes 3670016 | tf_op jit(solution)/shard_map/all_to_all | solution.py:367
  335.7 2.0 copy-start.4
  339.0 38.1 %collective-permute-start.10 = (bf16[128,2048]{1,0:T(8,128)(2,1)}, bf16[128,2048]{1,0:T(8,128)(2,1)}, u32[]{:S(2)}, u32[]{:S(2)}) collective-permute-start(bf16[128,2048]{1,0:T(8,128)(2,1)} %fusion.11), channel_id=1, source_target_pairs={{0,16},{8,24},{16,0},{24,8},{1,17},{9,25},{17,1},{25,9},{2,18},{10... | collective-permute-start | bytes 1572872 | tf_op jit(solution)/shard_map/ppermute | solution.py:381
  345.0 2.1 copy-start.6
  347.1 1.3 copy-start.30
  347.1 1.3 copy-start.32
  347.1 1.3 copy-start.34
  348.4 28.7 %collective-permute-start.8 = (bf16[128,2048]{1,0:T(8,128)(2,1)}, bf16[128,2048]{1,0:T(8,128)(2,1)}, u32[]{:S(2)}, u32[]{:S(2)}) collective-permute-start(bf16[128,2048]{1,0:T(8,128)(2,1)} %fusion.10), channel_id=1, source_target_pairs={{0,8},{8,16},{16,24},{24,0},{1,9},{9,17},{17,25},{25,1},{2,10},{10... | collective-permute-start | bytes 1572872 | tf_op jit(solution)/shard_map/ppermute | solution.py:381
  362.1 15.0 %copy-start.3 = (bf16[400,2048]{1,0:T(8,128)(2,1)S(1)}, bf16[400,2048]{1,0:T(8,128)(2,1)}, u32[]{:S(2)}) copy-start(bf16[400,2048]{1,0:T(8,128)(2,1)} %reshape.263) | copy-start | bytes 4915204

commit v3 on v2

--- a/solution.py
+++ b/solution.py
@@ -325,7 +325,7 @@
     slot_ids = jnp.arange(slots_total, dtype=jnp.int32)
     level_axes = ("ctx_lo", "head")
     routed = None
-    for turn in range(levels):
+    for turn in list(range(1, levels)) + [0]:
         if turn == 0:
             chunk = packed
         else:
@@ -376,13 +376,14 @@
             weight_low, result_rows, preferred_element_type=jnp.float32
         )
         if turn == 0:
-            routed = partial
+            routed = partial if routed is None else routed + partial
         else:
-            routed = routed + lax.ppermute(
+            carried = lax.ppermute(
                 partial.astype(jnp.bfloat16),
                 "ctx_hi",
                 [(i, (i + turn) % levels) for i in range(levels)],
             ).astype(jnp.float32)
+            routed = carried if routed is None else routed + carried
     combined = hidden.astype(jnp.float32) + routed
     return combined.astype(jnp.bfloat16)
 

time: 386 us -> 386 us (level)
  no operation moved by 1% of the time
where the time goes in v3:
time: 386 us; the launch traced here: 380 us
  waiting for transfers between devices  133 us (34%)
  starting transfers between devices  86.4 us (22%)
  matrix products  79 us (20%)
  local copies, waits for them, and re-layouts  59.9 us (16%)
  other arithmetic  19.4 us (5%)
    all_to_all x4, waiting for transfers between devices, per_device(): lax.all_to_all(outgoing, level_axes, split_axis=0, concat_axis=0, tiled=T...  51 us
    all_to_all x4, waiting for transfers between devices, per_device(): lax.all_to_all(answered, level_axes, split_axis=0, concat_axis=0, tiled=T...  33 us
    ppermute x6, waiting for transfers between devices, passed_along(): return lax.ppermute(block, axis, route)  31.6 us
    ppermute x6, starting transfers between devices, passed_along(): return lax.ppermute(block, axis, route)  28 us
    dot_general x4, matrix products, expert_apply_rows(): gate_up = jnp.dot(rows_in, up_matrix, preferred_element_type=jnp.float32)  18.1 us
    all_to_all x4, starting transfers between devices, per_device(): lax.all_to_all(answered, level_axes, split_axis=0, concat_axis=0, tiled=T...  17.6 us
    all_to_all x4, starting transfers between devices, per_device(): lax.all_to_all(outgoing, level_axes, split_axis=0, concat_axis=0, tiled=T...  17.3 us
    ppermute x3, starting transfers between devices, per_device(): lax.ppermute(packed, 'ctx_hi', [(i, (i - turn) % levels) for i in range(l...  17.2 us
  transfers between devices with their start and end apart: 21, of which 16 were waited for; matrix products, arithmetic and copies ran while one was open for 30% of the time, Pallas kernels for 0%

profile of v3, /device:TPU:0, one launch (start us, length us, event | category | flops | bytes accessed | tf_op | source)
XLA Modules:
  0.0 380.2 jit_solution(12658165972427394986)
XLA Ops:
  1.6 4.8 %collective-permute-start = (bf16[3,2048]{1,0:T(4,128)(2,1)S(1)}, bf16[3,2048]{1,0:T(4,128)(2,1)S(1)}, u32[]{:S(2)}, u32[]{:S(2)}) collective-permute-start(bf16[3,2048]{1,0:T(4,128)(2,1)S(1)} %pad_maximum_fusion.5), channel_id=1, source_target_pairs={{0,2},{2,4},{4,6},{6,8},{8,10},{10,12},{12,14},{14,16},{16,18},{18... | collective-permute-start | bytes 36872 | tf_op jit(solution)/shard_map/ppermute | solution.py:19
  14.5 2.9 multiply_bitcast_fusion
  35.3 2.1 multiply_subtract_fusion
  42.3 4.2 %collective-permute-start.1 = (bf16[2,8,128,128]{3,2,1,0:T(8,128)(2,1)}, bf16[2,8,128,128]{3,2,1,0:T(8,128)(2,1)}, u32[]{:S(2)}, u32[]{:S(2)}) collective-permute-start(bf16[2,8,128,128]{3,2,1,0:T(8,128)(2,1)} %pad_maximum_fusion.2), channel_id=1, source_target_pairs={{0,2},{2,4},{4,6},{6,8},{8,10},{10,12},{12,14},{14,16},{16,18},{18... | collective-permute-start | bytes 1572872 | tf_op jit(solution)/shard_map/ppermute | solution.py:19
  46.7 10.2 %collective-permute-done.1 = bf16[2,8,128,128]{3,2,1,0:T(8,128)(2,1)} collective-permute-done((bf16[2,8,128,128]{3,2,1,0:T(8,128)(2,1)}, bf16[2,8,128,128]{3,2,1,0:T(8,128)(2,1)}, u32[]{:S(2)}, u32[]{:S(2)}) %collective-permute-start.1) | collective-permute-done | bytes 524320 | tf_op jit(solution)/shard_map/ppermute | solution.py:19
  60.0 5.3 %collective-permute-start.2 = (bf16[2,8,128,128]{3,2,1,0:T(8,128)(2,1)S(1)}, bf16[2,8,128,128]{3,2,1,0:T(8,128)(2,1)S(1)}, u32[]{:S(2)}, u32[]{:S(2)}) collective-permute-start(bf16[2,8,128,128]{3,2,1,0:T(8,128)(2,1)S(1)} %pad_maximum_fusion.3), channel_id=1, source_target_pairs={{0,4},{2,6},{4,8},{6,10},{8,12},{10,14},{12,16},{14,18},{16,20},{1... | collective-permute-start | bytes 1572872 | tf_op jit(solution)/shard_map/ppermute | solution.py:19
  66.5 8.7 %collective-permute-done.2 = bf16[2,8,128,128]{3,2,1,0:T(8,128)(2,1)S(1)} collective-permute-done((bf16[2,8,128,128]{3,2,1,0:T(8,128)(2,1)S(1)}, bf16[2,8,128,128]{3,2,1,0:T(8,128)(2,1)S(1)}, u32[]{:S(2)}, u32[]{:S(2)}) %collective-permute-start.2) | collective-permute-done | bytes 524320 | tf_op jit(solution)/shard_map/ppermute | solution.py:19
  76.0 6.6 %collective-permute-start.3 = (bf16[2,8,128,128]{3,2,1,0:T(8,128)(2,1)S(1)}, bf16[2,8,128,128]{3,2,1,0:T(8,128)(2,1)S(1)}, u32[]{:S(2)}, u32[]{:S(2)}) collective-permute-start(bf16[2,8,128,128]{3,2,1,0:T(8,128)(2,1)S(1)} %pad_maximum_fusion.4), channel_id=1, source_target_pairs={{0,8},{2,10},{4,12},{6,14},{8,16},{10,18},{12,20},{14,22},{16,24},... | collective-permute-start | bytes 1572872 | tf_op jit(solution)/shard_map/ppermute | solution.py:19
  84.1 7.4 %collective-permute-done.3 = bf16[2,8,128,128]{3,2,1,0:T(8,128)(2,1)S(1)} collective-permute-done((bf16[2,8,128,128]{3,2,1,0:T(8,128)(2,1)S(1)}, bf16[2,8,128,128]{3,2,1,0:T(8,128)(2,1)S(1)}, u32[]{:S(2)}, u32[]{:S(2)}) %collective-permute-start.3) | collective-permute-done | bytes 524320 | tf_op jit(solution)/shard_map/ppermute | solution.py:19
  91.8 5.4 %collective-permute-start.4 = (bf16[8,128,128]{2,1,0:T(8,128)(2,1)S(1)}, bf16[8,128,128]{2,1,0:T(8,128)(2,1)S(1)}, u32[]{:S(2)}, u32[]{:S(2)}) collective-permute-start(bf16[8,128,128]{2,1,0:T(8,128)(2,1)S(1)} %get-tuple-element.62), channel_id=1, source_target_pairs={{0,16},{2,18},{4,20},{6,22},{8,24},{10,26},{12,28},{14,30},{1,17},... | collective-permute-start | bytes 786440 | tf_op jit(solution)/shard_map/ppermute | solution.py:19
  98.6 2.5 collective-permute-done.4
  104.2 2.7 collective-permute-done.5
  118.3 10.7 %collective-permute-start.11 = (bf16[128,2176]{1,0:T(8,128)(2,1)}, bf16[128,2176]{1,0:T(8,128)(2,1)}, u32[]{:S(2)}, u32[]{:S(2)}) collective-permute-start(bf16[128,2176]{1,0:T(8,128)(2,1)} %concatenate.23), channel_id=1, source_target_pairs={{0,8},{8,16},{16,24},{24,0},{1,9},{9,17},{17,25},{25,1},{2,10},{10... | collective-permute-start | bytes 1671176 | tf_op jit(solution)/shard_map/ppermute | solution.py:332
  131.2 2.6 reshape.268
  133.8 4.3 %all-to-all-start.6 = ((bf16[8,50,2048]{2,1,0:T(8,128)(2,1)}), bf16[8,50,2048]{2,1,0:T(8,128)(2,1)}, u32[]{:S(2)}, u32[]{:S(2)}) async-start(bf16[8,50,2048]{2,1,0:T(8,128)(2,1)} %reshape.268), calls=%async_computation.6 | async-start | bytes 3670016 | tf_op jit(solution)/shard_map/all_to_all | solution.py:356
  138.1 3.4 collective-permute-start.9
  141.6 4.1 %collective-permute-done.11 = bf16[128,2176]{1,0:T(8,128)(2,1)} collective-permute-done((bf16[128,2176]{1,0:T(8,128)(2,1)}, bf16[128,2176]{1,0:T(8,128)(2,1)}, u32[]{:S(2)}, u32[]{:S(2)}) %collective-permute-start.11) | collective-permute-done | bytes 557088 | tf_op jit(solution)/shard_map/ppermute | solution.py:332
  148.2 2.8 convolution_convert_fusion.5
  151.0 2.6 reshape.266
  153.7 8.3 %all-to-all-done.6 = bf16[8,50,2048]{2,1,0:T(8,128)(2,1)} async-done(((bf16[8,50,2048]{2,1,0:T(8,128)(2,1)}), bf16[8,50,2048]{2,1,0:T(8,128)(2,1)}, u32[]{:S(2)}, u32[]{:S(2)}) %all-to-all-start.6) | async-done | bytes 1638432 | tf_op jit(solution)/shard_map/all_to_all | solution.py:356
  162.0 4.3 %all-to-all-start.4 = ((bf16[8,50,2048]{2,1,0:T(8,128)(2,1)}), bf16[8,50,2048]{2,1,0:T(8,128)(2,1)}, u32[]{:S(2)}, u32[]{:S(2)}) async-start(bf16[8,50,2048]{2,1,0:T(8,128)(2,1)} %reshape.266), calls=%async_computation.4 | async-start | bytes 3670016 | tf_op jit(solution)/shard_map/all_to_all | solution.py:356
  166.3 3.1 collective-permute-start.7
  172.2 2.6 reshape.264
  174.8 15.3 %all-to-all-done.4 = bf16[8,50,2048]{2,1,0:T(8,128)(2,1)} async-done(((bf16[8,50,2048]{2,1,0:T(8,128)(2,1)}), bf16[8,50,2048]{2,1,0:T(8,128)(2,1)}, u32[]{:S(2)}, u32[]{:S(2)}) %all-to-all-start.4) | async-done | bytes 1638432 | tf_op jit(solution)/shard_map/all_to_all | solution.py:356
  190.1 4.3 %all-to-all-start.2 = ((bf16[8,50,2048]{2,1,0:T(8,128)(2,1)}), bf16[8,50,2048]{2,1,0:T(8,128)(2,1)}, u32[]{:S(2)}, u32[]{:S(2)}) async-start(bf16[8,50,2048]{2,1,0:T(8,128)(2,1)} %reshape.264), calls=%async_computation.2 | async-start | bytes 3670016 | tf_op jit(solution)/shard_map/all_to_all | solution.py:356
  197.2 2.9 convolution_convert_fusion.7
  200.1 2.6 reshape.262
  202.6 15.7 %all-to-all-done.2 = bf16[8,50,2048]{2,1,0:T(8,128)(2,1)} async-done(((bf16[8,50,2048]{2,1,0:T(8,128)(2,1)}), bf16[8,50,2048]{2,1,0:T(8,128)(2,1)}, u32[]{:S(2)}, u32[]{:S(2)}) %all-to-all-start.2) | async-done | bytes 1638432 | tf_op jit(solution)/shard_map/all_to_all | solution.py:356
  218.3 4.3 %all-to-all-start = ((bf16[8,50,2048]{2,1,0:T(8,128)(2,1)}), bf16[8,50,2048]{2,1,0:T(8,128)(2,1)}, u32[]{:S(2)}, u32[]{:S(2)}) async-start(bf16[8,50,2048]{2,1,0:T(8,128)(2,1)} %reshape.262), calls=%async_computation | async-start | bytes 3670016 | tf_op jit(solution)/shard_map/all_to_all | solution.py:356
  222.7 2.7 reshape_squeeze_reshape.14
  225.3 4.5 %fusion.2 = f32[400,1024]{1,0:T(8,128)S(1)} fusion(bf16[400,2048]{1,0:T(8,128)(2,1)} %reshape_squeeze_reshape.14, bf16[1,2048,1024]{2,1,0:T(8,128)(2,1)} %param.30), kind=kOutput, calls=%fused_computation.2 | convolution fusion | flops 1677721600 | bytes 7471104 | tf_op jit(solution)/shard_map/dot_general | solution.py:201
  229.9 2.2 convolution_convert_fusion.1
  232.1 2.7 reshape_stack_reshape.14
  234.8 11.7 %all-to-all-done = bf16[8,50,2048]{2,1,0:T(8,128)(2,1)} async-done(((bf16[8,50,2048]{2,1,0:T(8,128)(2,1)}), bf16[8,50,2048]{2,1,0:T(8,128)(2,1)}, u32[]{:S(2)}, u32[]{:S(2)}) %all-to-all-start) | async-done | bytes 1638432 | tf_op jit(solution)/shard_map/all_to_all | solution.py:356
  246.5 4.3 %all-to-all-start.5 = ((bf16[8,50,2048]{2,1,0:T(8,128)(2,1)}), bf16[8,50,2048]{2,1,0:T(8,128)(2,1)}, u32[]{:S(2)}, u32[]{:S(2)}) async-start(bf16[8,50,2048]{2,1,0:T(8,128)(2,1)} %reshape_stack_reshape.14), calls=%async_computation.5 | async-start | bytes 3670016 | tf_op jit(solution)/shard_map/all_to_all | solution.py:367
  251.0 2.7 reshape_squeeze_reshape.13
  253.7 4.5 %fusion.4 = f32[400,1024]{1,0:T(8,128)S(1)} fusion(bf16[400,2048]{1,0:T(8,128)(2,1)} %reshape_squeeze_reshape.13, bf16[1,2048,1024]{2,1,0:T(8,128)(2,1)} %param.30), kind=kOutput, calls=%fused_computation.4 | convolution fusion | flops 1677721600 | bytes 7471104 | tf_op jit(solution)/shard_map/dot_general | solution.py:201
  258.2 2.3 convolution_convert_fusion.2
  260.5 2.6 reshape_stack_reshape.13
  263.0 11.6 %all-to-all-done.5 = bf16[8,50,2048]{2,1,0:T(8,128)(2,1)} async-done(((bf16[8,50,2048]{2,1,0:T(8,128)(2,1)}), bf16[8,50,2048]{2,1,0:T(8,128)(2,1)}, u32[]{:S(2)}, u32[]{:S(2)}) %all-to-all-start.5) | async-done | bytes 1638432 | tf_op jit(solution)/shard_map/all_to_all | solution.py:367
  274.7 4.6 %all-to-all-start.3 = ((bf16[8,50,2048]{2,1,0:T(8,128)(2,1)}), bf16[8,50,2048]{2,1,0:T(8,128)(2,1)}, u32[]{:S(2)}, u32[]{:S(2)}) async-start(bf16[8,50,2048]{2,1,0:T(8,128)(2,1)} %reshape_stack_reshape.13), calls=%async_computation.3 | async-start | bytes 3670016 | tf_op jit(solution)/shard_map/all_to_all | solution.py:367
  280.9 2.6 reshape_squeeze_reshape.15
  283.5 2.6 reshape_squeeze_reshape.12
  286.1 4.5 %fusion.6 = f32[400,1024]{1,0:T(8,128)S(1)} fusion(bf16[400,2048]{1,0:T(8,128)(2,1)} %reshape_squeeze_reshape.12, bf16[1,2048,1024]{2,1,0:T(8,128)(2,1)} %param.30), kind=kOutput, calls=%fused_computation.6 | convolution fusion | flops 1677721600 | bytes 7471104 | tf_op jit(solution)/shard_map/dot_general | solution.py:201
  290.7 2.2 convolution_convert_fusion.3
  292.9 2.7 reshape_stack_reshape.12
  295.6 7.6 %all-to-all-done.3 = bf16[8,50,2048]{2,1,0:T(8,128)(2,1)} async-done(((bf16[8,50,2048]{2,1,0:T(8,128)(2,1)}), bf16[8,50,2048]{2,1,0:T(8,128)(2,1)}, u32[]{:S(2)}, u32[]{:S(2)}) %all-to-all-start.3) | async-done | bytes 1638432 | tf_op jit(solution)/shard_map/all_to_all | solution.py:367
  303.1 4.3 %all-to-all-start.1 = ((bf16[8,50,2048]{2,1,0:T(8,128)(2,1)}), bf16[8,50,2048]{2,1,0:T(8,128)(2,1)}, u32[]{:S(2)}, u32[]{:S(2)}) async-start(bf16[8,50,2048]{2,1,0:T(8,128)(2,1)} %reshape_stack_reshape.12), calls=%async_computation.1 | async-start | bytes 3670016 | tf_op jit(solution)/shard_map/all_to_all | solution.py:367
  307.5 4.5 %fusion = f32[400,1024]{1,0:T(8,128)S(1)} fusion(bf16[400,2048]{1,0:T(8,128)(2,1)} %reshape_squeeze_reshape.15, bf16[1,2048,1024]{2,1,0:T(8,128)(2,1)} %param.30), kind=kOutput, calls=%fused_computation | convolution fusion | flops 1677721600 | bytes 7471104 | tf_op jit(solution)/shard_map/dot_general | solution.py:201
  312.0 2.2 convolution_convert_fusion
  314.3 2.6 reshape_stack_reshape.15
  316.9 2.6 reshape.267
  322.8 2.8 collective-permute-start.12
  325.6 2.6 reshape.265
  328.3 3.1 all-to-all-done.1
  331.3 4.3 %all-to-all-start.7 = ((bf16[8,50,2048]{2,1,0:T(8,128)(2,1)}), bf16[8,50,2048]{2,1,0:T(8,128)(2,1)}, u32[]{:S(2)}, u32[]{:S(2)}) async-start(bf16[8,50,2048]{2,1,0:T(8,128)(2,1)} %reshape_stack_reshape.15), calls=%async_computation.7 | async-start | bytes 3670016 | tf_op jit(solution)/shard_map/all_to_all | solution.py:367
  335.7 2.0 fusion.246
  339.0 3.4 collective-permute-start.10
  342.4 2.6 reshape.263
  345.0 2.0 fusion.245
  348.8 10.7 %all-to-all-done.7 = bf16[8,50,2048]{2,1,0:T(8,128)(2,1)} async-done(((bf16[8,50,2048]{2,1,0:T(8,128)(2,1)}), bf16[8,50,2048]{2,1,0:T(8,128)(2,1)}, u32[]{:S(2)}, u32[]{:S(2)}) %all-to-all-start.7) | async-done | bytes 1638432 | tf_op jit(solution)/shard_map/all_to_all | solution.py:367
  359.5 2.6 reshape.269
  364.2 13.0 %collective-permute-done.10 = bf16[128,2048]{1,0:T(8,128)(2,1)} collective-permute-done((bf16[128,2048]{1,0:T(8,128)(2,1)}, bf16[128,2048]{1,0:T(8,128)(2,1)}, u32[]{:S(2)}, u32[]{:S(2)}) %collective-permute-start.10) | collective-permute-done | bytes 524320 | tf_op jit(solution)/shard_map/ppermute | solution.py:381
  377.1 2.6 fusion.66
  (265 shorter events, 74.5 us)
Async XLA Ops:
  0.0 229.9 %copy-start = (bf16[1,512,2048]{2,1,0:T(8,128)(2,1)S(1)}, bf16[1,512,2048]{2,1,0:T(8,128)(2,1)}, u32[]{:S(2)}) copy-start(bf16[1,512,2048]{2,1,0:T(8,128)(2,1)} %param.31) | copy-start | bytes 6291460
  0.0 14.2 %copy-start.26 = (bf16[256,1024]{1,0:T(8,128)(2,1)S(1)}, bf16[256,1024]{1,0:T(8,128)(2,1)}, u32[]{:S(2)}) copy-start(bf16[256,1024]{1,0:T(8,128)(2,1)} %param.17) | copy-start | bytes 1572868
  1.6 12.6 %collective-permute-start = (bf16[3,2048]{1,0:T(4,128)(2,1)S(1)}, bf16[3,2048]{1,0:T(4,128)(2,1)S(1)}, u32[]{:S(2)}, u32[]{:S(2)}) collective-permute-start(bf16[3,2048]{1,0:T(4,128)(2,1)S(1)} %pad_maximum_fusion.5), channel_id=1, source_target_pairs={{0,2},{2,4},{4,6},{6,8},{8,10},{10,12},{12,14},{14,16},{16,18},{18... | collective-permute-start | bytes 36872 | tf_op jit(solution)/shard_map/ppermute | solution.py:19
  29.6 1.2 copy-start.17
  33.5 1.9 copy-start.1
  37.7 1.2 copy-start.23
  38.1 0.8 copy-start.10
  38.5 1.2 copy-start.12
  38.9 1.2 copy-start.14
  39.3 1.2 copy-start.19
  39.8 0.9 copy-start.21
  40.2 2.1 copy-start.16
  40.2 6.3 %copy-start.36 = (s32[128,10]{0,1:T(8,128)S(1)}, s32[128,10]{0,1:T(8,128)}, u32[]{:S(2)}) copy-start(s32[128,10]{0,1:T(8,128)} %param.28) | copy-start | bytes 15364
  40.6 0.8 copy-start.7
  42.3 14.6 %collective-permute-start.1 = (bf16[2,8,128,128]{3,2,1,0:T(8,128)(2,1)}, bf16[2,8,128,128]{3,2,1,0:T(8,128)(2,1)}, u32[]{:S(2)}, u32[]{:S(2)}) collective-permute-start(bf16[2,8,128,128]{3,2,1,0:T(8,128)(2,1)} %pad_maximum_fusion.2), channel_id=1, source_target_pairs={{0,2},{2,4},{4,6},{6,8},{8,10},{10,12},{12,14},{14,16},{16,18},{18... | collective-permute-start | bytes 1572872 | tf_op jit(solution)/shard_map/ppermute | solution.py:19
  46.6 11.9 %copy-start.8 = (f32[8,128,128]{2,1,0:T(8,128)S(1)}, f32[8,128,128]{2,1,0:T(8,128)}, u32[]{:S(2)}) copy-start(f32[8,128,128]{2,1,0:T(8,128)} %copy-done.7) | copy-start | bytes 1572868
  58.5 6.8 %copy-start.38 = (f32[128]{0:T(128)S(1)}, f32[128]{0:T(128)}, u32[]{:S(2)}) copy-start(f32[128]{0:T(128)} %param.24) | copy-start | bytes 1540
  58.5 6.9 %copy-start.25 = (f32[256,4,128]{2,1,0:T(4,128)S(1)}, f32[256,4,128]{2,1,0:T(4,128)}, u32[]{:S(2)}) copy-start(f32[256,4,128]{2,1,0:T(4,128)} %get-tuple-element.24) | copy-start | bytes 1572868
  60.0 15.3 %collective-permute-start.2 = (bf16[2,8,128,128]{3,2,1,0:T(8,128)(2,1)S(1)}, bf16[2,8,128,128]{3,2,1,0:T(8,128)(2,1)S(1)}, u32[]{:S(2)}, u32[]{:S(2)}) collective-permute-start(bf16[2,8,128,128]{3,2,1,0:T(8,128)(2,1)S(1)} %pad_maximum_fusion.3), channel_id=1, source_target_pairs={{0,4},{2,6},{4,8},{6,10},{8,12},{10,14},{12,16},{14,18},{16,20},{1... | collective-permute-start | bytes 1572872 | tf_op jit(solution)/shard_map/ppermute | solution.py:19
  75.6 7.0 %copy-start.2 = (f32[8,4,64,256]{3,2,1,0:T(8,128)S(1)}, f32[8,4,64,256]{3,2,1,0:T(8,128)}, u32[]{:S(2)}) copy-start(f32[8,4,64,256]{3,2,1,0:T(8,128)} %copy-done.1) | copy-start | bytes 6291460
  76.0 15.4 %collective-permute-start.3 = (bf16[2,8,128,128]{3,2,1,0:T(8,128)(2,1)S(1)}, bf16[2,8,128,128]{3,2,1,0:T(8,128)(2,1)S(1)}, u32[]{:S(2)}, u32[]{:S(2)}) collective-permute-start(bf16[2,8,128,128]{3,2,1,0:T(8,128)(2,1)S(1)} %pad_maximum_fusion.4), channel_id=1, source_target_pairs={{0,8},{2,10},{4,12},{6,14},{8,16},{10,18},{12,20},{14,22},{16,24},... | collective-permute-start | bytes 1572872 | tf_op jit(solution)/shard_map/ppermute | solution.py:19
  84.0 13.2 %copy-start.11 = (f32[8,128,128]{2,1,0:T(8,128)S(1)}, f32[8,128,128]{2,1,0:T(8,128)}, u32[]{:S(2)}) copy-start(f32[8,128,128]{2,1,0:T(8,128)} %copy-done.10) | copy-start | bytes 1572868
  84.0 13.2 %copy-start.13 = (f32[8,128,128]{2,1,0:T(8,128)S(1)}, f32[8,128,128]{2,1,0:T(8,128)}, u32[]{:S(2)}) copy-start(f32[8,128,128]{2,1,0:T(8,128)} %copy-done.12) | copy-start | bytes 1572868
  84.1 13.2 %copy-start.15 = (f32[8,128,128]{2,1,0:T(8,128)S(1)}, f32[8,128,128]{2,1,0:T(8,128)}, u32[]{:S(2)}) copy-start(f32[8,128,128]{2,1,0:T(8,128)} %copy-done.14) | copy-start | bytes 1572868
  91.8 9.3 %collective-permute-start.4 = (bf16[8,128,128]{2,1,0:T(8,128)(2,1)S(1)}, bf16[8,128,128]{2,1,0:T(8,128)(2,1)S(1)}, u32[]{:S(2)}, u32[]{:S(2)}) collective-permute-start(bf16[8,128,128]{2,1,0:T(8,128)(2,1)S(1)} %get-tuple-element.62), channel_id=1, source_target_pairs={{0,16},{2,18},{4,20},{6,22},{8,24},{10,26},{12,28},{14,30},{1,17},... | collective-permute-start | bytes 786440 | tf_op jit(solution)/shard_map/ppermute | solution.py:19
  98.3 4.8 %copy-start.20 = (f32[8,128,128]{2,1,0:T(8,128)S(1)}, f32[8,128,128]{2,1,0:T(8,128)}, u32[]{:S(2)}) copy-start(f32[8,128,128]{2,1,0:T(8,128)} %copy-done.19) | copy-start | bytes 1572868
  98.3 4.8 %copy-start.22 = (f32[8,128,128]{2,1,0:T(8,128)S(1)}, f32[8,128,128]{2,1,0:T(8,128)}, u32[]{:S(2)}) copy-start(f32[8,128,128]{2,1,0:T(8,128)} %copy-done.21) | copy-start | bytes 1572868
  98.3 4.8 %copy-start.24 = (f32[8,128,128]{2,1,0:T(8,128)S(1)}, f32[8,128,128]{2,1,0:T(8,128)}, u32[]{:S(2)}) copy-start(f32[8,128,128]{2,1,0:T(8,128)} %copy-done.23) | copy-start | bytes 1572868
  101.4 5.5 %collective-permute-start.5 = (bf16[8,128,128]{2,1,0:T(8,128)(2,1)S(1)}, bf16[8,128,128]{2,1,0:T(8,128)(2,1)S(1)}, u32[]{:S(2)}, u32[]{:S(2)}) collective-permute-start(bf16[8,128,128]{2,1,0:T(8,128)(2,1)S(1)} %fusion.58), channel_id=1, source_target_pairs={{0,2},{2,4},{4,6},{6,8},{8,10},{10,12},{12,14},{14,16},{16,18},{18... | collective-permute-start | bytes 786440 | tf_op jit(solution)/shard_map/ppermute | solution.py:19
  107.7 1.0 copy-start.28
  108.4 2.2 copy-start.18
  110.6 2.8 copy-start.37
  110.6 4.8 %copy-start.27 = (bf16[128,2048]{1,0:T(8,128)(2,1)S(1)}, bf16[128,2048]{1,0:T(8,128)(2,1)}, u32[]{:S(2)}) copy-start(bf16[128,2048]{1,0:T(8,128)(2,1)} %param.26) | copy-start | bytes 1572868
  111.9 1.3 copy-start.9
  113.2 3.9 %copy-start.35 = (f32[2048]{0:T(1024)S(1)}, f32[2048]{0:T(1024)}, u32[]{:S(2)}) copy-start(f32[2048]{0:T(1024)} %param.27) | copy-start | bytes 24580
  113.3 2.1 collective-permute-start.6
  113.4 0.6 copy-start.33
  113.4 0.7 copy-start.31
  118.3 27.3 %collective-permute-start.11 = (bf16[128,2176]{1,0:T(8,128)(2,1)}, bf16[128,2176]{1,0:T(8,128)(2,1)}, u32[]{:S(2)}, u32[]{:S(2)}) collective-permute-start(bf16[128,2176]{1,0:T(8,128)(2,1)} %concatenate.23), channel_id=1, source_target_pairs={{0,8},{8,16},{16,24},{24,0},{1,9},{9,17},{17,25},{25,1},{2,10},{10... | collective-permute-start | bytes 1671176 | tf_op jit(solution)/shard_map/ppermute | solution.py:332
  129.1 4.7 %copy-start.29 = (s32[128,10]{0,1:T(8,128)}, s32[128,10]{0,1:T(8,128)S(1)}, u32[]{:S(2)}) copy-start(s32[128,10]{0,1:T(8,128)S(1)} %copy.188) | copy-start | bytes 15364
  133.8 28.2 %all-to-all-start.6 = ((bf16[8,50,2048]{2,1,0:T(8,128)(2,1)}), bf16[8,50,2048]{2,1,0:T(8,128)(2,1)}, u32[]{:S(2)}, u32[]{:S(2)}) async-start(bf16[8,50,2048]{2,1,0:T(8,128)(2,1)} %reshape.268), calls=%async_computation.6 | async-start | bytes 3670016 | tf_op jit(solution)/shard_map/all_to_all | solution.py:356
  138.1 31.3 %collective-permute-start.9 = (bf16[128,2176]{1,0:T(8,128)(2,1)}, bf16[128,2176]{1,0:T(8,128)(2,1)S(1)}, u32[]{:S(2)}, u32[]{:S(2)}) collective-permute-start(bf16[128,2176]{1,0:T(8,128)(2,1)} %concatenate.23), channel_id=1, source_target_pairs={{0,16},{8,24},{16,0},{24,8},{1,17},{9,25},{17,1},{25,9},{2,18},{10... | collective-permute-start | bytes 1671176 | tf_op jit(solution)/shard_map/ppermute | solution.py:332
  162.0 28.2 %all-to-all-start.4 = ((bf16[8,50,2048]{2,1,0:T(8,128)(2,1)}), bf16[8,50,2048]{2,1,0:T(8,128)(2,1)}, u32[]{:S(2)}, u32[]{:S(2)}) async-start(bf16[8,50,2048]{2,1,0:T(8,128)(2,1)} %reshape.266), calls=%async_computation.4 | async-start | bytes 3670016 | tf_op jit(solution)/shard_map/all_to_all | solution.py:356
  166.3 28.2 %collective-permute-start.7 = (bf16[128,2176]{1,0:T(8,128)(2,1)}, bf16[128,2176]{1,0:T(8,128)(2,1)}, u32[]{:S(2)}, u32[]{:S(2)}) collective-permute-start(bf16[128,2176]{1,0:T(8,128)(2,1)} %concatenate.23), channel_id=1, source_target_pairs={{0,24},{8,0},{16,8},{24,16},{1,25},{9,1},{17,9},{25,17},{2,26},{10... | collective-permute-start | bytes 1671176 | tf_op jit(solution)/shard_map/ppermute | solution.py:332
  190.1 28.2 %all-to-all-start.2 = ((bf16[8,50,2048]{2,1,0:T(8,128)(2,1)}), bf16[8,50,2048]{2,1,0:T(8,128)(2,1)}, u32[]{:S(2)}, u32[]{:S(2)}) async-start(bf16[8,50,2048]{2,1,0:T(8,128)(2,1)} %reshape.264), calls=%async_computation.2 | async-start | bytes 3670016 | tf_op jit(solution)/shard_map/all_to_all | solution.py:356
  218.3 28.2 %all-to-all-start = ((bf16[8,50,2048]{2,1,0:T(8,128)(2,1)}), bf16[8,50,2048]{2,1,0:T(8,128)(2,1)}, u32[]{:S(2)}, u32[]{:S(2)}) async-start(bf16[8,50,2048]{2,1,0:T(8,128)(2,1)} %reshape.262), calls=%async_computation | async-start | bytes 3670016 | tf_op jit(solution)/shard_map/all_to_all | solution.py:356
  246.5 28.2 %all-to-all-start.5 = ((bf16[8,50,2048]{2,1,0:T(8,128)(2,1)}), bf16[8,50,2048]{2,1,0:T(8,128)(2,1)}, u32[]{:S(2)}, u32[]{:S(2)}) async-start(bf16[8,50,2048]{2,1,0:T(8,128)(2,1)} %reshape_stack_reshape.14), calls=%async_computation.5 | async-start | bytes 3670016 | tf_op jit(solution)/shard_map/all_to_all | solution.py:367
  274.7 28.5 %all-to-all-start.3 = ((bf16[8,50,2048]{2,1,0:T(8,128)(2,1)}), bf16[8,50,2048]{2,1,0:T(8,128)(2,1)}, u32[]{:S(2)}, u32[]{:S(2)}) async-start(bf16[8,50,2048]{2,1,0:T(8,128)(2,1)} %reshape_stack_reshape.13), calls=%async_computation.3 | async-start | bytes 3670016 | tf_op jit(solution)/shard_map/all_to_all | solution.py:367
  303.1 28.2 %all-to-all-start.1 = ((bf16[8,50,2048]{2,1,0:T(8,128)(2,1)}), bf16[8,50,2048]{2,1,0:T(8,128)(2,1)}, u32[]{:S(2)}, u32[]{:S(2)}) async-start(bf16[8,50,2048]{2,1,0:T(8,128)(2,1)} %reshape_stack_reshape.12), calls=%async_computation.1 | async-start | bytes 3670016 | tf_op jit(solution)/shard_map/all_to_all | solution.py:367
  319.5 2.0 copy-start.5
  322.8 41.3 %collective-permute-start.12 = (bf16[128,2048]{1,0:T(8,128)(2,1)}, bf16[128,2048]{1,0:T(8,128)(2,1)S(1)}, u32[]{:S(2)}, u32[]{:S(2)}) collective-permute-start(bf16[128,2048]{1,0:T(8,128)(2,1)} %fusion.12), channel_id=1, source_target_pairs={{0,24},{8,0},{16,8},{24,16},{1,25},{9,1},{17,9},{25,17},{2,26},{10... | collective-permute-start | bytes 1572872 | tf_op jit(solution)/shard_map/ppermute | solution.py:381
  331.3 28.2 %all-to-all-start.7 = ((bf16[8,50,2048]{2,1,0:T(8,128)(2,1)}), bf16[8,50,2048]{2,1,0:T(8,128)(2,1)}, u32[]{:S(2)}, u32[]{:S(2)}) async-start(bf16[8,50,2048]{2,1,0:T(8,128)(2,1)} %reshape_stack_reshape.15), calls=%async_computation.7 | async-start | bytes 3670016 | tf_op jit(solution)/shard_map/all_to_all | solution.py:367
  335.7 2.0 copy-start.4
  339.0 38.1 %collective-permute-start.10 = (bf16[128,2048]{1,0:T(8,128)(2,1)}, bf16[128,2048]{1,0:T(8,128)(2,1)}, u32[]{:S(2)}, u32[]{:S(2)}) collective-permute-start(bf16[128,2048]{1,0:T(8,128)(2,1)} %fusion.11), channel_id=1, source_target_pairs={{0,16},{8,24},{16,0},{24,8},{1,17},{9,25},{17,1},{25,9},{2,18},{10... | collective-permute-start | bytes 1572872 | tf_op jit(solution)/shard_map/ppermute | solution.py:381
  345.0 2.1 copy-start.6
  347.1 1.3 copy-start.30
  347.1 1.3 copy-start.32
  347.1 1.3 copy-start.34
  348.4 28.7 %collective-permute-start.8 = (bf16[128,2048]{1,0:T(8,128)(2,1)}, bf16[128,2048]{1,0:T(8,128)(2,1)}, u32[]{:S(2)}, u32[]{:S(2)}) collective-permute-start(bf16[128,2048]{1,0:T(8,128)(2,1)} %fusion.10), channel_id=1, source_target_pairs={{0,8},{8,16},{16,24},{24,0},{1,9},{9,17},{17,25},{25,1},{2,10},{10... | collective-permute-start | bytes 1572872 | tf_op jit(solution)/shard_map/ppermute | solution.py:381
  362.1 15.0 %copy-start.3 = (bf16[400,2048]{1,0:T(8,128)(2,1)S(1)}, bf16[400,2048]{1,0:T(8,128)(2,1)}, u32[]{:S(2)}) copy-start(bf16[400,2048]{1,0:T(8,128)(2,1)} %reshape.269) | copy-start | bytes 4915204

commit v4 on v2

--- a/solution.py
+++ b/solution.py
@@ -11,6 +11,7 @@
 
 
 HIGHEST = lax.Precision.HIGH
+LEAF = lax.Precision.DEFAULT
 
 
 def passed_along(block, axis, distance):
@@ -119,7 +120,7 @@
     solved = precise_dot(unit_lower_inverse(system), stacked)
     targets = solved[:, :DV]
     corrector = solved[:, DV:]
-    within = jnp.where(causal, precise_dot(queries, key_rows.T) * decay_matrix, 0.0)
+    within = jnp.where(causal, jnp.dot(queries, key_rows.T, preferred_element_type=jnp.float32) * decay_matrix, 0.0)
     query_decayed = queries * (jnp.exp(cumulative) * carried_in)[:, None]
     final_log = cumulative[BLOCK - 1]
     weighting = (segment_here == segment_here[BLOCK - 1]).astype(jnp.float32) * jnp.exp(
@@ -156,8 +157,8 @@
     )
 
 
-def blockwise(left, right):
-    return jnp.einsum("hbij,hbjk->hbik", left, right, precision=HIGHEST)
+def blockwise(left, right, precision=HIGHEST):
+    return jnp.einsum("hbij,hbjk->hbik", left, right, precision=precision)
 
 
 def batched(left, right):
@@ -270,12 +271,12 @@
         prefix_shift = batched(transition[:, block], prefix_shift) + increment[:, block]
     stacked_maps = jnp.stack(prefix_maps, axis=1)
     stacked_shifts = jnp.stack(prefix_shifts, axis=1)
-    query_effective = query_decayed - blockwise(within, corrector)
-    through_entry = blockwise(query_effective, stacked_maps)
-    fixed_part = blockwise(query_effective, stacked_shifts) + blockwise(within, targets)
+    query_effective = query_decayed - blockwise(within, corrector, LEAF)
+    through_entry = blockwise(query_effective, stacked_maps, LEAF)
+    fixed_part = blockwise(query_effective, stacked_shifts, LEAF) + blockwise(within, targets, LEAF)
     entering = scanned_entry(prefix_map, prefix_shift, CTX)
     emitted = (
-        jnp.einsum("hbtk,hkv->hbtv", through_entry, entering, precision=HIGHEST) + fixed_part
+        jnp.einsum("hbtk,hkv->hbtv", through_entry, entering, precision=LEAF) + fixed_part
     )
     mixed_heads = jnp.transpose(emitted, (1, 2, 0, 3)).reshape(-1, heads_here, DV)
     gated_out = gate_output(mixed_heads, gate_raw, norm_gain)

time: 386 us -> 392 us (1.016)
    dot_general x17 -> x16, matrix products: 14.7 us -> 13.7 us  [precise_dot(): jnp.dot(left, right, precision=HIGHEST, preferred_element_type=jnp.float32)]
    unnamed x87 -> x93, local copies, waits for them, and re-layouts: 7.14 us -> 8.11 us
  transfers between devices with their start and end apart: 21 -> 21, of which waited for: 16 -> 16; matrix products, arithmetic and copies ran while one was open for 30% -> 29% of each run, Pallas kernels for 0% -> 0%
where the time goes in v4:
time: 392 us; the launch traced here: 386 us
  waiting for transfers between devices  133 us (34%)
  starting transfers between devices  87.2 us (22%)
  matrix products  81.8 us (21%)
  local copies, waits for them, and re-layouts  61.5 us (16%)
  other arithmetic  20.9 us (5%)
    all_to_all x4, waiting for transfers between devices, per_device(): lax.all_to_all(outgoing, level_axes, split_axis=0, concat_axis=0, tiled=T...  51.2 us
    all_to_all x4, waiting for transfers between devices, per_device(): lax.all_to_all(answered, level_axes, split_axis=0, concat_axis=0, tiled=T...  33 us
    ppermute x6, waiting for transfers between devices, passed_along(): return lax.ppermute(block, axis, route)  31.4 us
    ppermute x6, starting transfers between devices, passed_along(): return lax.ppermute(block, axis, route)  28.8 us
    dot_general x4, matrix products, expert_apply_rows(): gate_up = jnp.dot(rows_in, up_matrix, preferred_element_type=jnp.float32)  18.1 us
    all_to_all x4, starting transfers between devices, per_device(): lax.all_to_all(outgoing, level_axes, split_axis=0, concat_axis=0, tiled=T...  17.7 us
    all_to_all x4, starting transfers between devices, per_device(): lax.all_to_all(answered, level_axes, split_axis=0, concat_axis=0, tiled=T...  17.4 us
    ppermute x3, starting transfers between devices, per_device(): lax.ppermute(packed, 'ctx_hi', [(i, (i - turn) % levels) for i in range(l...  17 us
  transfers between devices with their start and end apart: 21, of which 16 were waited for; matrix products, arithmetic and copies ran while one was open for 29% of the time, Pallas kernels for 0%

profile of v4, /device:TPU:0, one launch (start us, length us, event | category | flops | bytes accessed | tf_op | source)
XLA Modules:
  0.0 386.4 jit_solution(346023343036662645)
XLA Ops:
  1.6 4.8 %collective-permute-start = (bf16[3,2048]{1,0:T(4,128)(2,1)S(1)}, bf16[3,2048]{1,0:T(4,128)(2,1)S(1)}, u32[]{:S(2)}, u32[]{:S(2)}) collective-permute-start(bf16[3,2048]{1,0:T(4,128)(2,1)S(1)} %pad_maximum_fusion.5), channel_id=1, source_target_pairs={{0,2},{2,4},{4,6},{6,8},{8,10},{10,12},{12,14},{14,16},{16,18},{18... | collective-permute-start | bytes 36872 | tf_op jit(solution)/shard_map/ppermute | solution.py:20
  13.8 2.8 multiply_bitcast_fusion
  34.8 2.1 multiply_subtract_fusion
  41.0 4.2 %collective-permute-start.1 = (bf16[2,8,128,128]{3,2,1,0:T(8,128)(2,1)}, bf16[2,8,128,128]{3,2,1,0:T(8,128)(2,1)}, u32[]{:S(2)}, u32[]{:S(2)}) collective-permute-start(bf16[2,8,128,128]{3,2,1,0:T(8,128)(2,1)} %pad_maximum_fusion.2), channel_id=1, source_target_pairs={{0,2},{2,4},{4,6},{6,8},{8,10},{10,12},{12,14},{14,16},{16,18},{18... | collective-permute-start | bytes 1572872 | tf_op jit(solution)/shard_map/ppermute | solution.py:20
  45.2 10.4 %collective-permute-done.1 = bf16[2,8,128,128]{3,2,1,0:T(8,128)(2,1)} collective-permute-done((bf16[2,8,128,128]{3,2,1,0:T(8,128)(2,1)}, bf16[2,8,128,128]{3,2,1,0:T(8,128)(2,1)}, u32[]{:S(2)}, u32[]{:S(2)}) %collective-permute-start.1) | collective-permute-done | bytes 524320 | tf_op jit(solution)/shard_map/ppermute | solution.py:20
  59.2 6.1 %collective-permute-start.2 = (bf16[2,8,128,128]{3,2,1,0:T(8,128)(2,1)}, bf16[2,8,128,128]{3,2,1,0:T(8,128)(2,1)}, u32[]{:S(2)}, u32[]{:S(2)}) collective-permute-start(bf16[2,8,128,128]{3,2,1,0:T(8,128)(2,1)} %pad_maximum_fusion.3), channel_id=1, source_target_pairs={{0,4},{2,6},{4,8},{6,10},{8,12},{10,14},{12,16},{14,18},{16,20},{1... | collective-permute-start | bytes 1572872 | tf_op jit(solution)/shard_map/ppermute | solution.py:20
  66.2 8.7 %collective-permute-done.2 = bf16[2,8,128,128]{3,2,1,0:T(8,128)(2,1)} collective-permute-done((bf16[2,8,128,128]{3,2,1,0:T(8,128)(2,1)}, bf16[2,8,128,128]{3,2,1,0:T(8,128)(2,1)}, u32[]{:S(2)}, u32[]{:S(2)}) %collective-permute-start.2) | collective-permute-done | bytes 524320 | tf_op jit(solution)/shard_map/ppermute | solution.py:20
  77.7 6.4 %collective-permute-start.3 = (bf16[2,8,128,128]{3,2,1,0:T(8,128)(2,1)S(1)}, bf16[2,8,128,128]{3,2,1,0:T(8,128)(2,1)S(1)}, u32[]{:S(2)}, u32[]{:S(2)}) collective-permute-start(bf16[2,8,128,128]{3,2,1,0:T(8,128)(2,1)S(1)} %pad_maximum_fusion.4), channel_id=1, source_target_pairs={{0,8},{2,10},{4,12},{6,14},{8,16},{10,18},{12,20},{14,22},{16,24},... | collective-permute-start | bytes 1572872 | tf_op jit(solution)/shard_map/ppermute | solution.py:20
  86.2 7.0 %collective-permute-done.3 = bf16[2,8,128,128]{3,2,1,0:T(8,128)(2,1)S(1)} collective-permute-done((bf16[2,8,128,128]{3,2,1,0:T(8,128)(2,1)S(1)}, bf16[2,8,128,128]{3,2,1,0:T(8,128)(2,1)S(1)}, u32[]{:S(2)}, u32[]{:S(2)}) %collective-permute-start.3) | collective-permute-done | bytes 524320 | tf_op jit(solution)/shard_map/ppermute | solution.py:20
  93.5 5.6 %collective-permute-start.4 = (bf16[8,128,128]{2,1,0:T(8,128)(2,1)S(1)}, bf16[8,128,128]{2,1,0:T(8,128)(2,1)S(1)}, u32[]{:S(2)}, u32[]{:S(2)}) collective-permute-start(bf16[8,128,128]{2,1,0:T(8,128)(2,1)S(1)} %get-tuple-element.62), channel_id=1, source_target_pairs={{0,16},{2,18},{4,20},{6,22},{8,24},{10,26},{12,28},{14,30},{1,17},... | collective-permute-start | bytes 786440 | tf_op jit(solution)/shard_map/ppermute | solution.py:20
  99.7 3.1 collective-permute-done.4
  106.3 2.3 collective-permute-done.5
  109.3 3.2 multiply_reduce_fusion
  124.4 10.7 %collective-permute-start.11 = (bf16[128,2176]{1,0:T(8,128)(2,1)}, bf16[128,2176]{1,0:T(8,128)(2,1)}, u32[]{:S(2)}, u32[]{:S(2)}) collective-permute-start(bf16[128,2176]{1,0:T(8,128)(2,1)} %concatenate.23), channel_id=1, source_target_pairs={{0,8},{8,16},{16,24},{24,0},{1,9},{9,17},{17,25},{25,1},{2,10},{10... | collective-permute-start | bytes 1671176 | tf_op jit(solution)/shard_map/ppermute | solution.py:333
  137.4 2.6 reshape.262
  140.0 4.3 %all-to-all-start = ((bf16[8,50,2048]{2,1,0:T(8,128)(2,1)}), bf16[8,50,2048]{2,1,0:T(8,128)(2,1)}, u32[]{:S(2)}, u32[]{:S(2)}) async-start(bf16[8,50,2048]{2,1,0:T(8,128)(2,1)} %reshape.262), calls=%async_computation | async-start | bytes 3670016 | tf_op jit(solution)/shard_map/all_to_all | solution.py:357
  144.3 3.4 collective-permute-start.9
  147.8 4.0 %collective-permute-done.11 = bf16[128,2176]{1,0:T(8,128)(2,1)} collective-permute-done((bf16[128,2176]{1,0:T(8,128)(2,1)}, bf16[128,2176]{1,0:T(8,128)(2,1)}, u32[]{:S(2)}, u32[]{:S(2)}) %collective-permute-start.11) | collective-permute-done | bytes 557088 | tf_op jit(solution)/shard_map/ppermute | solution.py:333
  154.4 2.8 convolution_convert_fusion.4
  157.3 2.6 reshape.268
  159.9 8.3 %all-to-all-done = bf16[8,50,2048]{2,1,0:T(8,128)(2,1)} async-done(((bf16[8,50,2048]{2,1,0:T(8,128)(2,1)}), bf16[8,50,2048]{2,1,0:T(8,128)(2,1)}, u32[]{:S(2)}, u32[]{:S(2)}) %all-to-all-start) | async-done | bytes 1638432 | tf_op jit(solution)/shard_map/all_to_all | solution.py:357
  168.2 4.3 %all-to-all-start.6 = ((bf16[8,50,2048]{2,1,0:T(8,128)(2,1)}), bf16[8,50,2048]{2,1,0:T(8,128)(2,1)}, u32[]{:S(2)}, u32[]{:S(2)}) async-start(bf16[8,50,2048]{2,1,0:T(8,128)(2,1)} %reshape.268), calls=%async_computation.6 | async-start | bytes 3670016 | tf_op jit(solution)/shard_map/all_to_all | solution.py:357
  172.5 2.9 collective-permute-start.7
  178.1 2.6 reshape.266
  180.8 15.6 %all-to-all-done.6 = bf16[8,50,2048]{2,1,0:T(8,128)(2,1)} async-done(((bf16[8,50,2048]{2,1,0:T(8,128)(2,1)}), bf16[8,50,2048]{2,1,0:T(8,128)(2,1)}, u32[]{:S(2)}, u32[]{:S(2)}) %all-to-all-start.6) | async-done | bytes 1638432 | tf_op jit(solution)/shard_map/all_to_all | solution.py:357
  196.3 4.3 %all-to-all-start.4 = ((bf16[8,50,2048]{2,1,0:T(8,128)(2,1)}), bf16[8,50,2048]{2,1,0:T(8,128)(2,1)}, u32[]{:S(2)}, u32[]{:S(2)}) async-start(bf16[8,50,2048]{2,1,0:T(8,128)(2,1)} %reshape.266), calls=%async_computation.4 | async-start | bytes 3670016 | tf_op jit(solution)/shard_map/all_to_all | solution.py:357
  203.4 2.9 convolution_convert_fusion.6
  206.2 2.6 reshape.264
  208.8 15.7 %all-to-all-done.4 = bf16[8,50,2048]{2,1,0:T(8,128)(2,1)} async-done(((bf16[8,50,2048]{2,1,0:T(8,128)(2,1)}), bf16[8,50,2048]{2,1,0:T(8,128)(2,1)}, u32[]{:S(2)}, u32[]{:S(2)}) %all-to-all-start.4) | async-done | bytes 1638432 | tf_op jit(solution)/shard_map/all_to_all | solution.py:357
  224.5 4.7 %all-to-all-start.2 = ((bf16[8,50,2048]{2,1,0:T(8,128)(2,1)}), bf16[8,50,2048]{2,1,0:T(8,128)(2,1)}, u32[]{:S(2)}, u32[]{:S(2)}) async-start(bf16[8,50,2048]{2,1,0:T(8,128)(2,1)} %reshape.264), calls=%async_computation.2 | async-start | bytes 3670016 | tf_op jit(solution)/shard_map/all_to_all | solution.py:357
  229.2 2.6 reshape_squeeze_reshape.15
  231.9 4.5 %fusion = f32[400,1024]{1,0:T(8,128)S(1)} fusion(bf16[400,2048]{1,0:T(8,128)(2,1)} %reshape_squeeze_reshape.15, bf16[1,2048,1024]{2,1,0:T(8,128)(2,1)} %param.30), kind=kOutput, calls=%fused_computation | convolution fusion | flops 1677721600 | bytes 7471104 | tf_op jit(solution)/shard_map/dot_general | solution.py:202
  236.4 2.2 convolution_convert_fusion
  238.7 2.7 reshape_stack_reshape.15
  241.4 11.7 %all-to-all-done.2 = bf16[8,50,2048]{2,1,0:T(8,128)(2,1)} async-done(((bf16[8,50,2048]{2,1,0:T(8,128)(2,1)}), bf16[8,50,2048]{2,1,0:T(8,128)(2,1)}, u32[]{:S(2)}, u32[]{:S(2)}) %all-to-all-start.2) | async-done | bytes 1638432 | tf_op jit(solution)/shard_map/all_to_all | solution.py:357
  253.1 4.3 %all-to-all-start.7 = ((bf16[8,50,2048]{2,1,0:T(8,128)(2,1)}), bf16[8,50,2048]{2,1,0:T(8,128)(2,1)}, u32[]{:S(2)}, u32[]{:S(2)}) async-start(bf16[8,50,2048]{2,1,0:T(8,128)(2,1)} %reshape_stack_reshape.15), calls=%async_computation.7 | async-start | bytes 3670016 | tf_op jit(solution)/shard_map/all_to_all | solution.py:368
  257.6 2.6 reshape_squeeze_reshape.14
  260.2 4.5 %fusion.2 = f32[400,1024]{1,0:T(8,128)S(1)} fusion(bf16[400,2048]{1,0:T(8,128)(2,1)} %reshape_squeeze_reshape.14, bf16[1,2048,1024]{2,1,0:T(8,128)(2,1)} %param.30), kind=kOutput, calls=%fused_computation.2 | convolution fusion | flops 1677721600 | bytes 7471104 | tf_op jit(solution)/shard_map/dot_general | solution.py:202
  264.7 2.2 convolution_convert_fusion.1
  267.0 2.6 reshape_stack_reshape.14
  269.6 11.7 %all-to-all-done.7 = bf16[8,50,2048]{2,1,0:T(8,128)(2,1)} async-done(((bf16[8,50,2048]{2,1,0:T(8,128)(2,1)}), bf16[8,50,2048]{2,1,0:T(8,128)(2,1)}, u32[]{:S(2)}, u32[]{:S(2)}) %all-to-all-start.7) | async-done | bytes 1638432 | tf_op jit(solution)/shard_map/all_to_all | solution.py:368
  281.2 4.3 %all-to-all-start.5 = ((bf16[8,50,2048]{2,1,0:T(8,128)(2,1)}), bf16[8,50,2048]{2,1,0:T(8,128)(2,1)}, u32[]{:S(2)}, u32[]{:S(2)}) async-start(bf16[8,50,2048]{2,1,0:T(8,128)(2,1)} %reshape_stack_reshape.14), calls=%async_computation.5 | async-start | bytes 3670016 | tf_op jit(solution)/shard_map/all_to_all | solution.py:368
  287.2 2.6 reshape_squeeze_reshape.12
  289.8 2.6 reshape_squeeze_reshape.13
  292.4 4.5 %fusion.4 = f32[400,1024]{1,0:T(8,128)S(1)} fusion(bf16[400,2048]{1,0:T(8,128)(2,1)} %reshape_squeeze_reshape.13, bf16[1,2048,1024]{2,1,0:T(8,128)(2,1)} %param.30), kind=kOutput, calls=%fused_computation.4 | convolution fusion | flops 1677721600 | bytes 7471104 | tf_op jit(solution)/shard_map/dot_general | solution.py:202
  297.0 2.3 convolution_convert_fusion.2
  299.2 2.7 reshape_stack_reshape.13
  301.9 7.5 %all-to-all-done.5 = bf16[8,50,2048]{2,1,0:T(8,128)(2,1)} async-done(((bf16[8,50,2048]{2,1,0:T(8,128)(2,1)}), bf16[8,50,2048]{2,1,0:T(8,128)(2,1)}, u32[]{:S(2)}, u32[]{:S(2)}) %all-to-all-start.5) | async-done | bytes 1638432 | tf_op jit(solution)/shard_map/all_to_all | solution.py:368
  309.4 4.5 %all-to-all-start.3 = ((bf16[8,50,2048]{2,1,0:T(8,128)(2,1)}), bf16[8,50,2048]{2,1,0:T(8,128)(2,1)}, u32[]{:S(2)}, u32[]{:S(2)}) async-start(bf16[8,50,2048]{2,1,0:T(8,128)(2,1)} %reshape_stack_reshape.13), calls=%async_computation.3 | async-start | bytes 3670016 | tf_op jit(solution)/shard_map/all_to_all | solution.py:368
  313.9 4.5 %fusion.6 = f32[400,1024]{1,0:T(8,128)S(1)} fusion(bf16[400,2048]{1,0:T(8,128)(2,1)} %reshape_squeeze_reshape.12, bf16[1,2048,1024]{2,1,0:T(8,128)(2,1)} %param.30), kind=kOutput, calls=%fused_computation.6 | convolution fusion | flops 1677721600 | bytes 7471104 | tf_op jit(solution)/shard_map/dot_general | solution.py:202
  318.5 2.2 convolution_convert_fusion.3
  320.7 2.6 reshape_stack_reshape.12
  323.3 2.6 reshape.269
  325.9 2.0 fusion.258
  329.2 2.8 collective-permute-start.12
  332.1 2.6 reshape.267
  334.7 3.1 all-to-all-done.3
  337.8 4.3 %all-to-all-start.1 = ((bf16[8,50,2048]{2,1,0:T(8,128)(2,1)}), bf16[8,50,2048]{2,1,0:T(8,128)(2,1)}, u32[]{:S(2)}, u32[]{:S(2)}) async-start(bf16[8,50,2048]{2,1,0:T(8,128)(2,1)} %reshape_stack_reshape.12), calls=%async_computation.1 | async-start | bytes 3670016 | tf_op jit(solution)/shard_map/all_to_all | solution.py:368
  345.5 3.4 collective-permute-start.10
  348.9 2.6 reshape.265
  355.3 10.7 %all-to-all-done.1 = bf16[8,50,2048]{2,1,0:T(8,128)(2,1)} async-done(((bf16[8,50,2048]{2,1,0:T(8,128)(2,1)}), bf16[8,50,2048]{2,1,0:T(8,128)(2,1)}, u32[]{:S(2)}, u32[]{:S(2)}) %all-to-all-start.1) | async-done | bytes 1638432 | tf_op jit(solution)/shard_map/all_to_all | solution.py:368
  365.9 2.6 reshape.263
  370.6 12.9 %collective-permute-done.10 = bf16[128,2048]{1,0:T(8,128)(2,1)} collective-permute-done((bf16[128,2048]{1,0:T(8,128)(2,1)}, bf16[128,2048]{1,0:T(8,128)(2,1)}, u32[]{:S(2)}, u32[]{:S(2)}) %collective-permute-start.10) | collective-permute-done | bytes 524320 | tf_op jit(solution)/shard_map/ppermute | solution.py:382
  383.5 2.7 fusion.74
  (270 shorter events, 79.0 us)
Async XLA Ops:
  0.0 236.4 %copy-start = (bf16[1,512,2048]{2,1,0:T(8,128)(2,1)S(1)}, bf16[1,512,2048]{2,1,0:T(8,128)(2,1)}, u32[]{:S(2)}) copy-start(bf16[1,512,2048]{2,1,0:T(8,128)(2,1)} %param.31) | copy-start | bytes 6291460
  0.0 13.5 %copy-start.25 = (bf16[256,1024]{1,0:T(8,128)(2,1)S(1)}, bf16[256,1024]{1,0:T(8,128)(2,1)}, u32[]{:S(2)}) copy-start(bf16[256,1024]{1,0:T(8,128)(2,1)} %param.17) | copy-start | bytes 1572868
  0.0 13.3 %copy-start.37 = (f32[256,8]{0,1:T(8,128)S(1)}, f32[256,8]{0,1:T(8,128)}, u32[]{:S(2)}) copy-start(f32[256,8]{0,1:T(8,128)} %param.19) | copy-start | bytes 24580
  1.6 11.9 %collective-permute-start = (bf16[3,2048]{1,0:T(4,128)(2,1)S(1)}, bf16[3,2048]{1,0:T(4,128)(2,1)S(1)}, u32[]{:S(2)}, u32[]{:S(2)}) collective-permute-start(bf16[3,2048]{1,0:T(4,128)(2,1)S(1)} %pad_maximum_fusion.5), channel_id=1, source_target_pairs={{0,2},{2,4},{4,6},{6,8},{8,10},{10,12},{12,14},{14,16},{16,18},{18... | collective-permute-start | bytes 36872 | tf_op jit(solution)/shard_map/ppermute | solution.py:20
  21.1 9.5 %copy-start.9 = (f32[256,4,2,128]{3,0,2,1:T(8,128)}, f32[256,4,2,128]{3,0,2,1:T(8,128)S(1)}, u32[]{:S(2)}) copy-start(f32[256,4,2,128]{3,0,2,1:T(8,128)S(1)} %broadcast_in_dim.205) | copy-start | bytes 3145732
  29.3 1.2 copy-start.11
  32.9 1.9 copy-start.1
  37.2 1.6 copy-start.17
  37.6 0.8 copy-start.18
  38.0 0.8 copy-start.21
  38.4 0.8 copy-start.23
  39.2 0.9 copy-start.13
  39.6 1.4 copy-start.15
  41.0 14.6 %collective-permute-start.1 = (bf16[2,8,128,128]{3,2,1,0:T(8,128)(2,1)}, bf16[2,8,128,128]{3,2,1,0:T(8,128)(2,1)}, u32[]{:S(2)}, u32[]{:S(2)}) collective-permute-start(bf16[2,8,128,128]{3,2,1,0:T(8,128)(2,1)} %pad_maximum_fusion.2), channel_id=1, source_target_pairs={{0,2},{2,4},{4,6},{6,8},{8,10},{10,12},{12,14},{14,16},{16,18},{18... | collective-permute-start | bytes 1572872 | tf_op jit(solution)/shard_map/ppermute | solution.py:20
  56.9 2.4 copy-start.8
  56.9 8.5 %copy-start.38 = (s32[128,10]{0,1:T(8,128)S(1)}, s32[128,10]{0,1:T(8,128)}, u32[]{:S(2)}) copy-start(s32[128,10]{0,1:T(8,128)} %param.28) | copy-start | bytes 15364
  56.9 8.6 %copy-start.40 = (f32[128]{0:T(128)S(1)}, f32[128]{0:T(128)}, u32[]{:S(2)}) copy-start(f32[128]{0:T(128)} %param.24) | copy-start | bytes 1540
  58.3 7.8 %copy-start.20 = (f32[256,4,128]{2,1,0:T(4,128)S(1)}, f32[256,4,128]{2,1,0:T(4,128)}, u32[]{:S(2)}) copy-start(f32[256,4,128]{2,1,0:T(4,128)} %get-tuple-element.24) | copy-start | bytes 1572868
  59.2 15.6 %collective-permute-start.2 = (bf16[2,8,128,128]{3,2,1,0:T(8,128)(2,1)}, bf16[2,8,128,128]{3,2,1,0:T(8,128)(2,1)}, u32[]{:S(2)}, u32[]{:S(2)}) collective-permute-start(bf16[2,8,128,128]{3,2,1,0:T(8,128)(2,1)} %pad_maximum_fusion.3), channel_id=1, source_target_pairs={{0,4},{2,6},{4,8},{6,10},{8,12},{10,14},{12,16},{14,18},{16,20},{1... | collective-permute-start | bytes 1572872 | tf_op jit(solution)/shard_map/ppermute | solution.py:20
  77.6 6.6 %copy-start.10 = (f32[256,4,2,128]{3,0,2,1:T(8,128)S(1)}, f32[256,4,2,128]{3,0,2,1:T(8,128)}, u32[]{:S(2)}) copy-start(f32[256,4,2,128]{3,0,2,1:T(8,128)} %copy-done.9) | copy-start | bytes 3145732
  77.7 15.4 %collective-permute-start.3 = (bf16[2,8,128,128]{3,2,1,0:T(8,128)(2,1)S(1)}, bf16[2,8,128,128]{3,2,1,0:T(8,128)(2,1)S(1)}, u32[]{:S(2)}, u32[]{:S(2)}) collective-permute-start(bf16[2,8,128,128]{3,2,1,0:T(8,128)(2,1)S(1)} %pad_maximum_fusion.4), channel_id=1, source_target_pairs={{0,8},{2,10},{4,12},{6,14},{8,16},{10,18},{12,20},{14,22},{16,24},... | collective-permute-start | bytes 1572872 | tf_op jit(solution)/shard_map/ppermute | solution.py:20
  84.2 1.6 copy-start.2
  86.2 18.5 %copy-start.28 = (bf16[8,4,64,128]{3,2,1,0:T(8,128)(2,1)}, bf16[8,4,64,128]{3,2,1,0:T(8,128)(2,1)S(1)}, u32[]{:S(2)}) copy-start(bf16[8,4,64,128]{3,2,1,0:T(8,128)(2,1)S(1)} %convolution_subtract_fusion.5) | copy-start | bytes 1572868
  93.5 9.3 %collective-permute-start.4 = (bf16[8,128,128]{2,1,0:T(8,128)(2,1)S(1)}, bf16[8,128,128]{2,1,0:T(8,128)(2,1)S(1)}, u32[]{:S(2)}, u32[]{:S(2)}) collective-permute-start(bf16[8,128,128]{2,1,0:T(8,128)(2,1)S(1)} %get-tuple-element.62), channel_id=1, source_target_pairs={{0,16},{2,18},{4,20},{6,22},{8,24},{10,26},{12,28},{14,30},{1,17},... | collective-permute-start | bytes 786440 | tf_op jit(solution)/shard_map/ppermute | solution.py:20
  99.4 5.3 %copy-start.19 = (f32[8,128,128]{2,1,0:T(8,128)S(1)}, f32[8,128,128]{2,1,0:T(8,128)}, u32[]{:S(2)}) copy-start(f32[8,128,128]{2,1,0:T(8,128)} %copy-done.18) | copy-start | bytes 1572868
  99.4 5.3 %copy-start.22 = (f32[8,128,128]{2,1,0:T(8,128)S(1)}, f32[8,128,128]{2,1,0:T(8,128)}, u32[]{:S(2)}) copy-start(f32[8,128,128]{2,1,0:T(8,128)} %copy-done.21) | copy-start | bytes 1572868
  99.4 5.3 %copy-start.24 = (f32[8,128,128]{2,1,0:T(8,128)S(1)}, f32[8,128,128]{2,1,0:T(8,128)}, u32[]{:S(2)}) copy-start(f32[8,128,128]{2,1,0:T(8,128)} %copy-done.23) | copy-start | bytes 1572868
  103.1 5.4 %collective-permute-start.5 = (bf16[8,128,128]{2,1,0:T(8,128)(2,1)S(1)}, bf16[8,128,128]{2,1,0:T(8,128)(2,1)S(1)}, u32[]{:S(2)}, u32[]{:S(2)}) collective-permute-start(bf16[8,128,128]{2,1,0:T(8,128)(2,1)S(1)} %fusion.66), channel_id=1, source_target_pairs={{0,2},{2,4},{4,6},{6,8},{8,10},{10,12},{12,14},{14,16},{16,18},{18... | collective-permute-start | bytes 786440 | tf_op jit(solution)/shard_map/ppermute | solution.py:20
  104.7 4.6 %copy-start.14 = (f32[8,128,128]{2,1,0:T(8,128)S(1)}, f32[8,128,128]{2,1,0:T(8,128)}, u32[]{:S(2)}) copy-start(f32[8,128,128]{2,1,0:T(8,128)} %copy-done.13) | copy-start | bytes 1572868
  104.7 4.6 %copy-start.16 = (f32[8,128,128]{2,1,0:T(8,128)S(1)}, f32[8,128,128]{2,1,0:T(8,128)}, u32[]{:S(2)}) copy-start(f32[8,128,128]{2,1,0:T(8,128)} %copy-done.15) | copy-start | bytes 1572868
  108.6 0.7 copy-start.41
  112.5 2.3 copy-start.27
  114.5 2.2 copy-start.12
  116.7 2.8 copy-start.39
  116.7 3.5 copy-start.29
  116.7 4.8 %copy-start.26 = (bf16[128,2048]{1,0:T(8,128)(2,1)S(1)}, bf16[128,2048]{1,0:T(8,128)(2,1)}, u32[]{:S(2)}) copy-start(bf16[128,2048]{1,0:T(8,128)(2,1)} %param.26) | copy-start | bytes 1572868
  118.0 1.3 copy-start.7
  119.3 3.9 %copy-start.36 = (f32[2048]{0:T(1024)S(1)}, f32[2048]{0:T(1024)}, u32[]{:S(2)}) copy-start(f32[2048]{0:T(1024)} %param.27) | copy-start | bytes 24580
  119.4 2.1 collective-permute-start.6
  119.5 0.6 copy-start.34
  119.5 0.7 copy-start.32
  124.4 27.4 %collective-permute-start.11 = (bf16[128,2176]{1,0:T(8,128)(2,1)}, bf16[128,2176]{1,0:T(8,128)(2,1)}, u32[]{:S(2)}, u32[]{:S(2)}) collective-permute-start(bf16[128,2176]{1,0:T(8,128)(2,1)} %concatenate.23), channel_id=1, source_target_pairs={{0,8},{8,16},{16,24},{24,0},{1,9},{9,17},{17,25},{25,1},{2,10},{10... | collective-permute-start | bytes 1671176 | tf_op jit(solution)/shard_map/ppermute | solution.py:333
  135.3 4.7 %copy-start.30 = (s32[128,10]{0,1:T(8,128)}, s32[128,10]{0,1:T(8,128)S(1)}, u32[]{:S(2)}) copy-start(s32[128,10]{0,1:T(8,128)S(1)} %copy.171) | copy-start | bytes 15364
  140.0 28.2 %all-to-all-start = ((bf16[8,50,2048]{2,1,0:T(8,128)(2,1)}), bf16[8,50,2048]{2,1,0:T(8,128)(2,1)}, u32[]{:S(2)}, u32[]{:S(2)}) async-start(bf16[8,50,2048]{2,1,0:T(8,128)(2,1)} %reshape.262), calls=%async_computation | async-start | bytes 3670016 | tf_op jit(solution)/shard_map/all_to_all | solution.py:357
  144.3 31.0 %collective-permute-start.9 = (bf16[128,2176]{1,0:T(8,128)(2,1)}, bf16[128,2176]{1,0:T(8,128)(2,1)S(1)}, u32[]{:S(2)}, u32[]{:S(2)}) collective-permute-start(bf16[128,2176]{1,0:T(8,128)(2,1)} %concatenate.23), channel_id=1, source_target_pairs={{0,16},{8,24},{16,0},{24,8},{1,17},{9,25},{17,1},{25,9},{2,18},{10... | collective-permute-start | bytes 1671176 | tf_op jit(solution)/shard_map/ppermute | solution.py:333
  168.2 28.2 %all-to-all-start.6 = ((bf16[8,50,2048]{2,1,0:T(8,128)(2,1)}), bf16[8,50,2048]{2,1,0:T(8,128)(2,1)}, u32[]{:S(2)}, u32[]{:S(2)}) async-start(bf16[8,50,2048]{2,1,0:T(8,128)(2,1)} %reshape.268), calls=%async_computation.6 | async-start | bytes 3670016 | tf_op jit(solution)/shard_map/all_to_all | solution.py:357
  172.5 28.2 %collective-permute-start.7 = (bf16[128,2176]{1,0:T(8,128)(2,1)}, bf16[128,2176]{1,0:T(8,128)(2,1)}, u32[]{:S(2)}, u32[]{:S(2)}) collective-permute-start(bf16[128,2176]{1,0:T(8,128)(2,1)} %concatenate.23), channel_id=1, source_target_pairs={{0,24},{8,0},{16,8},{24,16},{1,25},{9,1},{17,9},{25,17},{2,26},{10... | collective-permute-start | bytes 1671176 | tf_op jit(solution)/shard_map/ppermute | solution.py:333
  196.3 28.2 %all-to-all-start.4 = ((bf16[8,50,2048]{2,1,0:T(8,128)(2,1)}), bf16[8,50,2048]{2,1,0:T(8,128)(2,1)}, u32[]{:S(2)}, u32[]{:S(2)}) async-start(bf16[8,50,2048]{2,1,0:T(8,128)(2,1)} %reshape.266), calls=%async_computation.4 | async-start | bytes 3670016 | tf_op jit(solution)/shard_map/all_to_all | solution.py:357
  224.5 28.6 %all-to-all-start.2 = ((bf16[8,50,2048]{2,1,0:T(8,128)(2,1)}), bf16[8,50,2048]{2,1,0:T(8,128)(2,1)}, u32[]{:S(2)}, u32[]{:S(2)}) async-start(bf16[8,50,2048]{2,1,0:T(8,128)(2,1)} %reshape.264), calls=%async_computation.2 | async-start | bytes 3670016 | tf_op jit(solution)/shard_map/all_to_all | solution.py:357
  253.1 28.2 %all-to-all-start.7 = ((bf16[8,50,2048]{2,1,0:T(8,128)(2,1)}), bf16[8,50,2048]{2,1,0:T(8,128)(2,1)}, u32[]{:S(2)}, u32[]{:S(2)}) async-start(bf16[8,50,2048]{2,1,0:T(8,128)(2,1)} %reshape_stack_reshape.15), calls=%async_computation.7 | async-start | bytes 3670016 | tf_op jit(solution)/shard_map/all_to_all | solution.py:368
  281.2 28.2 %all-to-all-start.5 = ((bf16[8,50,2048]{2,1,0:T(8,128)(2,1)}), bf16[8,50,2048]{2,1,0:T(8,128)(2,1)}, u32[]{:S(2)}, u32[]{:S(2)}) async-start(bf16[8,50,2048]{2,1,0:T(8,128)(2,1)} %reshape_stack_reshape.14), calls=%async_computation.5 | async-start | bytes 3670016 | tf_op jit(solution)/shard_map/all_to_all | solution.py:368
  309.4 28.3 %all-to-all-start.3 = ((bf16[8,50,2048]{2,1,0:T(8,128)(2,1)}), bf16[8,50,2048]{2,1,0:T(8,128)(2,1)}, u32[]{:S(2)}, u32[]{:S(2)}) async-start(bf16[8,50,2048]{2,1,0:T(8,128)(2,1)} %reshape_stack_reshape.13), calls=%async_computation.3 | async-start | bytes 3670016 | tf_op jit(solution)/shard_map/all_to_all | solution.py:368
  325.9 2.0 copy-start.5
  329.2 41.4 %collective-permute-start.12 = (bf16[128,2048]{1,0:T(8,128)(2,1)}, bf16[128,2048]{1,0:T(8,128)(2,1)S(1)}, u32[]{:S(2)}, u32[]{:S(2)}) collective-permute-start(bf16[128,2048]{1,0:T(8,128)(2,1)} %fusion.12), channel_id=1, source_target_pairs={{0,24},{8,0},{16,8},{24,16},{1,25},{9,1},{17,9},{25,17},{2,26},{10... | collective-permute-start | bytes 1572872 | tf_op jit(solution)/shard_map/ppermute | solution.py:382
  337.8 28.2 %all-to-all-start.1 = ((bf16[8,50,2048]{2,1,0:T(8,128)(2,1)}), bf16[8,50,2048]{2,1,0:T(8,128)(2,1)}, u32[]{:S(2)}, u32[]{:S(2)}) async-start(bf16[8,50,2048]{2,1,0:T(8,128)(2,1)} %reshape_stack_reshape.12), calls=%async_computation.1 | async-start | bytes 3670016 | tf_op jit(solution)/shard_map/all_to_all | solution.py:368
  342.1 2.0 copy-start.4
  345.5 38.1 %collective-permute-start.10 = (bf16[128,2048]{1,0:T(8,128)(2,1)}, bf16[128,2048]{1,0:T(8,128)(2,1)}, u32[]{:S(2)}, u32[]{:S(2)}) collective-permute-start(bf16[128,2048]{1,0:T(8,128)(2,1)} %fusion.11), channel_id=1, source_target_pairs={{0,16},{8,24},{16,0},{24,8},{1,17},{9,25},{17,1},{25,9},{2,18},{10... | collective-permute-start | bytes 1572872 | tf_op jit(solution)/shard_map/ppermute | solution.py:382
  351.5 2.1 copy-start.6
  353.5 1.3 copy-start.31
  353.5 1.3 copy-start.33
  353.5 1.3 copy-start.35
  354.8 28.7 %collective-permute-start.8 = (bf16[128,2048]{1,0:T(8,128)(2,1)}, bf16[128,2048]{1,0:T(8,128)(2,1)}, u32[]{:S(2)}, u32[]{:S(2)}) collective-permute-start(bf16[128,2048]{1,0:T(8,128)(2,1)} %fusion.10), channel_id=1, source_target_pairs={{0,8},{8,16},{16,24},{24,0},{1,9},{9,17},{17,25},{25,1},{2,10},{10... | collective-permute-start | bytes 1572872 | tf_op jit(solution)/shard_map/ppermute | solution.py:382
  368.6 15.0 %copy-start.3 = (bf16[400,2048]{1,0:T(8,128)(2,1)S(1)}, bf16[400,2048]{1,0:T(8,128)(2,1)}, u32[]{:S(2)}) copy-start(bf16[400,2048]{1,0:T(8,128)(2,1)} %reshape.263) | copy-start | bytes 4915204

commit v5 on v2

--- a/solution.py
+++ b/solution.py
@@ -260,19 +260,26 @@
     )
     within, query_decayed, targets, corrector, transition, increment = block_terms
     heads_here, block_count = transition.shape[:2]
-    prefix_map = jnp.broadcast_to(jnp.eye(DK, dtype=jnp.float32), (heads_here, DK, DK))
-    prefix_shift = jnp.zeros((heads_here, DK, DV), jnp.float32)
+    prefix_map, prefix_shift = (transition[:, 0], increment[:, 0])
     prefix_maps, prefix_shifts = ([], [])
-    for block in range(block_count):
+    for block in range(1, block_count):
         prefix_maps.append(prefix_map)
         prefix_shifts.append(prefix_shift)
         prefix_map = batched(transition[:, block], prefix_map)
         prefix_shift = batched(transition[:, block], prefix_shift) + increment[:, block]
-    stacked_maps = jnp.stack(prefix_maps, axis=1)
-    stacked_shifts = jnp.stack(prefix_shifts, axis=1)
     query_effective = query_decayed - blockwise(within, corrector)
-    through_entry = blockwise(query_effective, stacked_maps)
-    fixed_part = blockwise(query_effective, stacked_shifts) + blockwise(within, targets)
+    through_entry = query_effective
+    fixed_part = blockwise(within, targets)
+    if block_count > 1:
+        stacked_maps = jnp.stack(prefix_maps, axis=1)
+        stacked_shifts = jnp.stack(prefix_shifts, axis=1)
+        later = query_effective[:, 1:]
+        through_entry = jnp.concatenate(
+            [query_effective[:, :1], blockwise(later, stacked_maps)], axis=1
+        )
+        fixed_part = fixed_part + jnp.concatenate(
+            [jnp.zeros_like(later[:, :1]), blockwise(later, stacked_shifts)], axis=1
+        )
     entering = scanned_entry(prefix_map, prefix_shift, CTX)
     emitted = (
         jnp.einsum("hbtk,hkv->hbtv", through_entry, entering, precision=HIGHEST) + fixed_part

time: 386 us -> 385 us (level)
    unnamed x87 -> x86, local copies, waits for them, and re-layouts: 7.14 us -> 8.26 us
where the time goes in v5:
time: 385 us; the launch traced here: 379 us
  waiting for transfers between devices  133 us (35%)
  starting transfers between devices  86.4 us (22%)
  matrix products  78.8 us (20%)
  local copies, waits for them, and re-layouts  60.3 us (16%)
  other arithmetic  19 us (5%)
    all_to_all x4, waiting for transfers between devices, per_device(): lax.all_to_all(outgoing, level_axes, split_axis=0, concat_axis=0, tiled=T...  51.2 us
    all_to_all x4, waiting for transfers between devices, per_device(): lax.all_to_all(answered, level_axes, split_axis=0, concat_axis=0, tiled=T...  33 us
    ppermute x6, waiting for transfers between devices, passed_along(): return lax.ppermute(block, axis, route)  31.1 us
    ppermute x6, starting transfers between devices, passed_along(): return lax.ppermute(block, axis, route)  28 us
    dot_general x4, matrix products, expert_apply_rows(): gate_up = jnp.dot(rows_in, up_matrix, preferred_element_type=jnp.float32)  18.1 us
    all_to_all x4, starting transfers between devices, per_device(): lax.all_to_all(outgoing, level_axes, split_axis=0, concat_axis=0, tiled=T...  17.7 us
    all_to_all x4, starting transfers between devices, per_device(): lax.all_to_all(answered, level_axes, split_axis=0, concat_axis=0, tiled=T...  17.5 us
    ppermute x3, starting transfers between devices, per_device(): lax.ppermute(packed, 'ctx_hi', [(i, (i - turn) % levels) for i in range(l...  17 us
  transfers between devices with their start and end apart: 21, of which 16 were waited for; matrix products, arithmetic and copies ran while one was open for 30% of the time, Pallas kernels for 0%

profile of v5, /device:TPU:0, one launch (start us, length us, event | category | flops | bytes accessed | tf_op | source)
XLA Modules:
  0.0 379.3 jit_solution(15535940363338359600)
XLA Ops:
  1.6 4.8 %collective-permute-start = (bf16[3,2048]{1,0:T(4,128)(2,1)S(1)}, bf16[3,2048]{1,0:T(4,128)(2,1)S(1)}, u32[]{:S(2)}, u32[]{:S(2)}) collective-permute-start(bf16[3,2048]{1,0:T(4,128)(2,1)S(1)} %pad_maximum_fusion.4), channel_id=1, source_target_pairs={{0,2},{2,4},{4,6},{6,8},{8,10},{10,12},{12,14},{14,16},{16,18},{18... | collective-permute-start | bytes 36872 | tf_op jit(solution)/shard_map/ppermute | solution.py:19
  13.8 2.9 multiply_bitcast_fusion
  32.3 2.3 fusion.108
  34.7 2.3 multiply_subtract_fusion
  41.3 4.2 %collective-permute-start.1 = (bf16[2,8,128,128]{3,2,1,0:T(8,128)(2,1)}, bf16[2,8,128,128]{3,2,1,0:T(8,128)(2,1)}, u32[]{:S(2)}, u32[]{:S(2)}) collective-permute-start(bf16[2,8,128,128]{3,2,1,0:T(8,128)(2,1)} %pad_maximum_fusion.1), channel_id=1, source_target_pairs={{0,2},{2,4},{4,6},{6,8},{8,10},{10,12},{12,14},{14,16},{16,18},{18... | collective-permute-start | bytes 1572872 | tf_op jit(solution)/shard_map/ppermute | solution.py:19
  45.6 10.3 %collective-permute-done.1 = bf16[2,8,128,128]{3,2,1,0:T(8,128)(2,1)} collective-permute-done((bf16[2,8,128,128]{3,2,1,0:T(8,128)(2,1)}, bf16[2,8,128,128]{3,2,1,0:T(8,128)(2,1)}, u32[]{:S(2)}, u32[]{:S(2)}) %collective-permute-start.1) | collective-permute-done | bytes 524320 | tf_op jit(solution)/shard_map/ppermute | solution.py:19
  59.0 5.3 %collective-permute-start.2 = (bf16[2,8,128,128]{3,2,1,0:T(8,128)(2,1)S(1)}, bf16[2,8,128,128]{3,2,1,0:T(8,128)(2,1)S(1)}, u32[]{:S(2)}, u32[]{:S(2)}) collective-permute-start(bf16[2,8,128,128]{3,2,1,0:T(8,128)(2,1)S(1)} %pad_maximum_fusion.2), channel_id=1, source_target_pairs={{0,4},{2,6},{4,8},{6,10},{8,12},{10,14},{12,16},{14,18},{16,20},{1... | collective-permute-start | bytes 1572872 | tf_op jit(solution)/shard_map/ppermute | solution.py:19
  65.5 8.7 %collective-permute-done.2 = bf16[2,8,128,128]{3,2,1,0:T(8,128)(2,1)S(1)} collective-permute-done((bf16[2,8,128,128]{3,2,1,0:T(8,128)(2,1)S(1)}, bf16[2,8,128,128]{3,2,1,0:T(8,128)(2,1)S(1)}, u32[]{:S(2)}, u32[]{:S(2)}) %collective-permute-start.2) | collective-permute-done | bytes 524320 | tf_op jit(solution)/shard_map/ppermute | solution.py:19
  75.0 6.4 %collective-permute-start.3 = (bf16[2,8,128,128]{3,2,1,0:T(8,128)(2,1)S(1)}, bf16[2,8,128,128]{3,2,1,0:T(8,128)(2,1)S(1)}, u32[]{:S(2)}, u32[]{:S(2)}) collective-permute-start(bf16[2,8,128,128]{3,2,1,0:T(8,128)(2,1)S(1)} %pad_maximum_fusion.3), channel_id=1, source_target_pairs={{0,8},{2,10},{4,12},{6,14},{8,16},{10,18},{12,20},{14,22},{16,24},... | collective-permute-start | bytes 1572872 | tf_op jit(solution)/shard_map/ppermute | solution.py:19
  84.1 6.3 %collective-permute-done.3 = bf16[2,8,128,128]{3,2,1,0:T(8,128)(2,1)S(1)} collective-permute-done((bf16[2,8,128,128]{3,2,1,0:T(8,128)(2,1)S(1)}, bf16[2,8,128,128]{3,2,1,0:T(8,128)(2,1)S(1)}, u32[]{:S(2)}, u32[]{:S(2)}) %collective-permute-start.3) | collective-permute-done | bytes 524320 | tf_op jit(solution)/shard_map/ppermute | solution.py:19
  90.8 5.4 %collective-permute-start.4 = (bf16[8,128,128]{2,1,0:T(8,128)(2,1)S(1)}, bf16[8,128,128]{2,1,0:T(8,128)(2,1)S(1)}, u32[]{:S(2)}, u32[]{:S(2)}) collective-permute-start(bf16[8,128,128]{2,1,0:T(8,128)(2,1)S(1)} %get-tuple-element.61), channel_id=1, source_target_pairs={{0,16},{2,18},{4,20},{6,22},{8,24},{10,26},{12,28},{14,30},{1,17},... | collective-permute-start | bytes 786440 | tf_op jit(solution)/shard_map/ppermute | solution.py:19
  97.2 2.9 collective-permute-done.4
  103.0 2.8 collective-permute-done.5
  117.3 10.7 %collective-permute-start.11 = (bf16[128,2176]{1,0:T(8,128)(2,1)}, bf16[128,2176]{1,0:T(8,128)(2,1)}, u32[]{:S(2)}, u32[]{:S(2)}) collective-permute-start(bf16[128,2176]{1,0:T(8,128)(2,1)} %concatenate.31), channel_id=1, source_target_pairs={{0,8},{8,16},{16,24},{24,0},{1,9},{9,17},{17,25},{25,1},{2,10},{10... | collective-permute-start | bytes 1671176 | tf_op jit(solution)/shard_map/ppermute | solution.py:339
  130.2 2.6 reshape.262
  132.8 4.3 %all-to-all-start = ((bf16[8,50,2048]{2,1,0:T(8,128)(2,1)}), bf16[8,50,2048]{2,1,0:T(8,128)(2,1)}, u32[]{:S(2)}, u32[]{:S(2)}) async-start(bf16[8,50,2048]{2,1,0:T(8,128)(2,1)} %reshape.262), calls=%async_computation | async-start | bytes 3670016 | tf_op jit(solution)/shard_map/all_to_all | solution.py:363
  137.1 3.4 collective-permute-start.9
  140.5 4.1 %collective-permute-done.11 = bf16[128,2176]{1,0:T(8,128)(2,1)} collective-permute-done((bf16[128,2176]{1,0:T(8,128)(2,1)}, bf16[128,2176]{1,0:T(8,128)(2,1)}, u32[]{:S(2)}, u32[]{:S(2)}) %collective-permute-start.11) | collective-permute-done | bytes 557088 | tf_op jit(solution)/shard_map/ppermute | solution.py:339
  147.3 2.8 convolution_convert_fusion.4
  150.1 2.6 reshape.268
  152.8 8.2 %all-to-all-done = bf16[8,50,2048]{2,1,0:T(8,128)(2,1)} async-done(((bf16[8,50,2048]{2,1,0:T(8,128)(2,1)}), bf16[8,50,2048]{2,1,0:T(8,128)(2,1)}, u32[]{:S(2)}, u32[]{:S(2)}) %all-to-all-start) | async-done | bytes 1638432 | tf_op jit(solution)/shard_map/all_to_all | solution.py:363
  160.9 4.3 %all-to-all-start.6 = ((bf16[8,50,2048]{2,1,0:T(8,128)(2,1)}), bf16[8,50,2048]{2,1,0:T(8,128)(2,1)}, u32[]{:S(2)}, u32[]{:S(2)}) async-start(bf16[8,50,2048]{2,1,0:T(8,128)(2,1)} %reshape.268), calls=%async_computation.6 | async-start | bytes 3670016 | tf_op jit(solution)/shard_map/all_to_all | solution.py:363
  165.3 2.9 collective-permute-start.7
  170.9 2.6 reshape.266
  173.6 15.5 %all-to-all-done.6 = bf16[8,50,2048]{2,1,0:T(8,128)(2,1)} async-done(((bf16[8,50,2048]{2,1,0:T(8,128)(2,1)}), bf16[8,50,2048]{2,1,0:T(8,128)(2,1)}, u32[]{:S(2)}, u32[]{:S(2)}) %all-to-all-start.6) | async-done | bytes 1638432 | tf_op jit(solution)/shard_map/all_to_all | solution.py:363
  189.1 4.3 %all-to-all-start.4 = ((bf16[8,50,2048]{2,1,0:T(8,128)(2,1)}), bf16[8,50,2048]{2,1,0:T(8,128)(2,1)}, u32[]{:S(2)}, u32[]{:S(2)}) async-start(bf16[8,50,2048]{2,1,0:T(8,128)(2,1)} %reshape.266), calls=%async_computation.4 | async-start | bytes 3670016 | tf_op jit(solution)/shard_map/all_to_all | solution.py:363
  196.1 2.9 convolution_convert_fusion.6
  198.9 2.6 reshape.264
  201.5 15.8 %all-to-all-done.4 = bf16[8,50,2048]{2,1,0:T(8,128)(2,1)} async-done(((bf16[8,50,2048]{2,1,0:T(8,128)(2,1)}), bf16[8,50,2048]{2,1,0:T(8,128)(2,1)}, u32[]{:S(2)}, u32[]{:S(2)}) %all-to-all-start.4) | async-done | bytes 1638432 | tf_op jit(solution)/shard_map/all_to_all | solution.py:363
  217.3 4.7 %all-to-all-start.2 = ((bf16[8,50,2048]{2,1,0:T(8,128)(2,1)}), bf16[8,50,2048]{2,1,0:T(8,128)(2,1)}, u32[]{:S(2)}, u32[]{:S(2)}) async-start(bf16[8,50,2048]{2,1,0:T(8,128)(2,1)} %reshape.264), calls=%async_computation.2 | async-start | bytes 3670016 | tf_op jit(solution)/shard_map/all_to_all | solution.py:363
  222.0 2.7 reshape_squeeze_reshape.15
  224.7 4.5 %fusion = f32[400,1024]{1,0:T(8,128)S(1)} fusion(bf16[400,2048]{1,0:T(8,128)(2,1)} %reshape_squeeze_reshape.15, bf16[1,2048,1024]{2,1,0:T(8,128)(2,1)} %param.30), kind=kOutput, calls=%fused_computation | convolution fusion | flops 1677721600 | bytes 7471104 | tf_op jit(solution)/shard_map/dot_general | solution.py:201
  229.2 2.2 convolution_convert_fusion
  231.4 2.7 reshape_stack_reshape.15
  234.1 11.7 %all-to-all-done.2 = bf16[8,50,2048]{2,1,0:T(8,128)(2,1)} async-done(((bf16[8,50,2048]{2,1,0:T(8,128)(2,1)}), bf16[8,50,2048]{2,1,0:T(8,128)(2,1)}, u32[]{:S(2)}, u32[]{:S(2)}) %all-to-all-start.2) | async-done | bytes 1638432 | tf_op jit(solution)/shard_map/all_to_all | solution.py:363
  245.9 4.3 %all-to-all-start.7 = ((bf16[8,50,2048]{2,1,0:T(8,128)(2,1)}), bf16[8,50,2048]{2,1,0:T(8,128)(2,1)}, u32[]{:S(2)}, u32[]{:S(2)}) async-start(bf16[8,50,2048]{2,1,0:T(8,128)(2,1)} %reshape_stack_reshape.15), calls=%async_computation.7 | async-start | bytes 3670016 | tf_op jit(solution)/shard_map/all_to_all | solution.py:374
  250.4 2.6 reshape_squeeze_reshape.14
  253.0 4.5 %fusion.2 = f32[400,1024]{1,0:T(8,128)S(1)} fusion(bf16[400,2048]{1,0:T(8,128)(2,1)} %reshape_squeeze_reshape.14, bf16[1,2048,1024]{2,1,0:T(8,128)(2,1)} %param.30), kind=kOutput, calls=%fused_computation.2 | convolution fusion | flops 1677721600 | bytes 7471104 | tf_op jit(solution)/shard_map/dot_general | solution.py:201
  257.5 2.3 convolution_convert_fusion.1
  259.8 2.6 reshape_stack_reshape.14
  262.4 11.6 %all-to-all-done.7 = bf16[8,50,2048]{2,1,0:T(8,128)(2,1)} async-done(((bf16[8,50,2048]{2,1,0:T(8,128)(2,1)}), bf16[8,50,2048]{2,1,0:T(8,128)(2,1)}, u32[]{:S(2)}, u32[]{:S(2)}) %all-to-all-start.7) | async-done | bytes 1638432 | tf_op jit(solution)/shard_map/all_to_all | solution.py:374
  274.0 4.3 %all-to-all-start.5 = ((bf16[8,50,2048]{2,1,0:T(8,128)(2,1)}), bf16[8,50,2048]{2,1,0:T(8,128)(2,1)}, u32[]{:S(2)}, u32[]{:S(2)}) async-start(bf16[8,50,2048]{2,1,0:T(8,128)(2,1)} %reshape_stack_reshape.14), calls=%async_computation.5 | async-start | bytes 3670016 | tf_op jit(solution)/shard_map/all_to_all | solution.py:374
  280.0 2.6 reshape_squeeze_reshape.12
  282.6 2.6 reshape_squeeze_reshape.13
  285.2 4.5 %fusion.4 = f32[400,1024]{1,0:T(8,128)S(1)} fusion(bf16[400,2048]{1,0:T(8,128)(2,1)} %reshape_squeeze_reshape.13, bf16[1,2048,1024]{2,1,0:T(8,128)(2,1)} %param.30), kind=kOutput, calls=%fused_computation.4 | convolution fusion | flops 1677721600 | bytes 7471104 | tf_op jit(solution)/shard_map/dot_general | solution.py:201
  289.8 2.2 convolution_convert_fusion.2
  292.0 2.7 reshape_stack_reshape.13
  294.7 7.5 %all-to-all-done.5 = bf16[8,50,2048]{2,1,0:T(8,128)(2,1)} async-done(((bf16[8,50,2048]{2,1,0:T(8,128)(2,1)}), bf16[8,50,2048]{2,1,0:T(8,128)(2,1)}, u32[]{:S(2)}, u32[]{:S(2)}) %all-to-all-start.5) | async-done | bytes 1638432 | tf_op jit(solution)/shard_map/all_to_all | solution.py:374
  302.2 4.5 %all-to-all-start.3 = ((bf16[8,50,2048]{2,1,0:T(8,128)(2,1)}), bf16[8,50,2048]{2,1,0:T(8,128)(2,1)}, u32[]{:S(2)}, u32[]{:S(2)}) async-start(bf16[8,50,2048]{2,1,0:T(8,128)(2,1)} %reshape_stack_reshape.13), calls=%async_computation.3 | async-start | bytes 3670016 | tf_op jit(solution)/shard_map/all_to_all | solution.py:374
  306.7 4.5 %fusion.6 = f32[400,1024]{1,0:T(8,128)S(1)} fusion(bf16[400,2048]{1,0:T(8,128)(2,1)} %reshape_squeeze_reshape.12, bf16[1,2048,1024]{2,1,0:T(8,128)(2,1)} %param.30), kind=kOutput, calls=%fused_computation.6 | convolution fusion | flops 1677721600 | bytes 7471104 | tf_op jit(solution)/shard_map/dot_general | solution.py:201
  311.3 2.2 convolution_convert_fusion.3
  313.5 2.6 reshape_stack_reshape.12
  316.1 2.6 reshape.269
  322.0 2.8 collective-permute-start.12
  324.9 2.6 reshape.267
  327.5 3.1 all-to-all-done.3
  330.6 4.3 %all-to-all-start.1 = ((bf16[8,50,2048]{2,1,0:T(8,128)(2,1)}), bf16[8,50,2048]{2,1,0:T(8,128)(2,1)}, u32[]{:S(2)}, u32[]{:S(2)}) async-start(bf16[8,50,2048]{2,1,0:T(8,128)(2,1)} %reshape_stack_reshape.12), calls=%async_computation.1 | async-start | bytes 3670016 | tf_op jit(solution)/shard_map/all_to_all | solution.py:374
  338.3 3.4 collective-permute-start.10
  341.7 2.6 reshape.265
  344.3 2.0 fusion.254
  348.1 10.7 %all-to-all-done.1 = bf16[8,50,2048]{2,1,0:T(8,128)(2,1)} async-done(((bf16[8,50,2048]{2,1,0:T(8,128)(2,1)}), bf16[8,50,2048]{2,1,0:T(8,128)(2,1)}, u32[]{:S(2)}, u32[]{:S(2)}) %all-to-all-start.1) | async-done | bytes 1638432 | tf_op jit(solution)/shard_map/all_to_all | solution.py:374
  358.8 2.6 reshape.263
  363.4 13.0 %collective-permute-done.10 = bf16[128,2048]{1,0:T(8,128)(2,1)} collective-permute-done((bf16[128,2048]{1,0:T(8,128)(2,1)}, bf16[128,2048]{1,0:T(8,128)(2,1)}, u32[]{:S(2)}, u32[]{:S(2)}) %collective-permute-start.10) | collective-permute-done | bytes 524320 | tf_op jit(solution)/shard_map/ppermute | solution.py:388
  376.4 2.7 fusion.67
  (263 shorter events, 73.7 us)
Async XLA Ops:
  0.0 229.2 %copy-start = (bf16[1,512,2048]{2,1,0:T(8,128)(2,1)S(1)}, bf16[1,512,2048]{2,1,0:T(8,128)(2,1)}, u32[]{:S(2)}) copy-start(bf16[1,512,2048]{2,1,0:T(8,128)(2,1)} %param.31) | copy-start | bytes 6291460
  0.0 13.5 %copy-start.24 = (bf16[256,1024]{1,0:T(8,128)(2,1)S(1)}, bf16[256,1024]{1,0:T(8,128)(2,1)}, u32[]{:S(2)}) copy-start(bf16[256,1024]{1,0:T(8,128)(2,1)} %param.17) | copy-start | bytes 1572868
  0.0 13.3 %copy-start.34 = (f32[256,8]{0,1:T(8,128)S(1)}, f32[256,8]{0,1:T(8,128)}, u32[]{:S(2)}) copy-start(f32[256,8]{0,1:T(8,128)} %param.19) | copy-start | bytes 24580
  1.6 11.9 %collective-permute-start = (bf16[3,2048]{1,0:T(4,128)(2,1)S(1)}, bf16[3,2048]{1,0:T(4,128)(2,1)S(1)}, u32[]{:S(2)}, u32[]{:S(2)}) collective-permute-start(bf16[3,2048]{1,0:T(4,128)(2,1)S(1)} %pad_maximum_fusion.4), channel_id=1, source_target_pairs={{0,2},{2,4},{4,6},{6,8},{8,10},{10,12},{12,14},{14,16},{16,18},{18... | collective-permute-start | bytes 36872 | tf_op jit(solution)/shard_map/ppermute | solution.py:19
  29.3 1.2 copy-start.21
  32.3 2.4 copy-start.2
  34.7 3.6 copy-start.10
  37.0 2.1 copy-start.1
  37.4 1.2 copy-start.12
  37.8 0.9 copy-start.16
  38.3 0.8 copy-start.19
  38.7 0.9 copy-start.18
  39.1 2.2 copy-start.14
  39.1 6.4 %copy-start.35 = (s32[128,10]{0,1:T(8,128)S(1)}, s32[128,10]{0,1:T(8,128)}, u32[]{:S(2)}) copy-start(s32[128,10]{0,1:T(8,128)} %param.28) | copy-start | bytes 15364
  39.5 0.8 copy-start.8
  41.3 14.6 %collective-permute-start.1 = (bf16[2,8,128,128]{3,2,1,0:T(8,128)(2,1)}, bf16[2,8,128,128]{3,2,1,0:T(8,128)(2,1)}, u32[]{:S(2)}, u32[]{:S(2)}) collective-permute-start(bf16[2,8,128,128]{3,2,1,0:T(8,128)(2,1)} %pad_maximum_fusion.1), channel_id=1, source_target_pairs={{0,2},{2,4},{4,6},{6,8},{8,10},{10,12},{12,14},{14,16},{16,18},{18... | collective-permute-start | bytes 1572872 | tf_op jit(solution)/shard_map/ppermute | solution.py:19
  45.6 12.0 %copy-start.9 = (f32[8,128,128]{2,1,0:T(8,128)S(1)}, f32[8,128,128]{2,1,0:T(8,128)}, u32[]{:S(2)}) copy-start(f32[8,128,128]{2,1,0:T(8,128)} %copy-done.8) | copy-start | bytes 1572868
  57.5 6.8 %copy-start.37 = (f32[128]{0:T(128)S(1)}, f32[128]{0:T(128)}, u32[]{:S(2)}) copy-start(f32[128]{0:T(128)} %param.24) | copy-start | bytes 1540
  57.5 6.8 %copy-start.23 = (f32[256,4,128]{2,1,0:T(4,128)S(1)}, f32[256,4,128]{2,1,0:T(4,128)}, u32[]{:S(2)}) copy-start(f32[256,4,128]{2,1,0:T(4,128)} %get-tuple-element.22) | copy-start | bytes 1572868
  59.0 15.3 %collective-permute-start.2 = (bf16[2,8,128,128]{3,2,1,0:T(8,128)(2,1)S(1)}, bf16[2,8,128,128]{3,2,1,0:T(8,128)(2,1)S(1)}, u32[]{:S(2)}, u32[]{:S(2)}) collective-permute-start(bf16[2,8,128,128]{3,2,1,0:T(8,128)(2,1)S(1)} %pad_maximum_fusion.2), channel_id=1, source_target_pairs={{0,4},{2,6},{4,8},{6,10},{8,12},{10,14},{12,16},{14,18},{16,20},{1... | collective-permute-start | bytes 1572872 | tf_op jit(solution)/shard_map/ppermute | solution.py:19
  74.6 6.9 %copy-start.3 = (f32[8,4,64,256]{3,2,1,0:T(8,128)S(1)}, f32[8,4,64,256]{3,2,1,0:T(8,128)}, u32[]{:S(2)}) copy-start(f32[8,4,64,256]{3,2,1,0:T(8,128)} %copy-done.2) | copy-start | bytes 6291460
  75.0 8.3 %copy-start.17 = (f32[8,128,128]{2,1,0:T(8,128)S(1)}, f32[8,128,128]{2,1,0:T(8,128)}, u32[]{:S(2)}) copy-start(f32[8,128,128]{2,1,0:T(8,128)} %copy-done.16) | copy-start | bytes 1572868
  75.0 8.3 %copy-start.20 = (f32[8,128,128]{2,1,0:T(8,128)S(1)}, f32[8,128,128]{2,1,0:T(8,128)}, u32[]{:S(2)}) copy-start(f32[8,128,128]{2,1,0:T(8,128)} %copy-done.19) | copy-start | bytes 1572868
  75.0 15.4 %collective-permute-start.3 = (bf16[2,8,128,128]{3,2,1,0:T(8,128)(2,1)S(1)}, bf16[2,8,128,128]{3,2,1,0:T(8,128)(2,1)S(1)}, u32[]{:S(2)}, u32[]{:S(2)}) collective-permute-start(bf16[2,8,128,128]{3,2,1,0:T(8,128)(2,1)S(1)} %pad_maximum_fusion.3), channel_id=1, source_target_pairs={{0,8},{2,10},{4,12},{6,14},{8,16},{10,18},{12,20},{14,22},{16,24},... | collective-permute-start | bytes 1572872 | tf_op jit(solution)/shard_map/ppermute | solution.py:19
  90.8 9.3 %collective-permute-start.4 = (bf16[8,128,128]{2,1,0:T(8,128)(2,1)S(1)}, bf16[8,128,128]{2,1,0:T(8,128)(2,1)S(1)}, u32[]{:S(2)}, u32[]{:S(2)}) collective-permute-start(bf16[8,128,128]{2,1,0:T(8,128)(2,1)S(1)} %get-tuple-element.61), channel_id=1, source_target_pairs={{0,16},{2,18},{4,20},{6,22},{8,24},{10,26},{12,28},{14,30},{1,17},... | collective-permute-start | bytes 786440 | tf_op jit(solution)/shard_map/ppermute | solution.py:19
  96.9 5.3 %slice-start = ((f32[8,4,128,128]{3,2,1,0:T(8,128)}), f32[8,1,128,128]{3,2,1,0:T(8,128)S(1)}, s32[]{:S(2)}) async-start(f32[8,4,128,128]{3,2,1,0:T(8,128)} %copy-done.1), calls=%async_computation.8 | async-start | bytes 1048576 | tf_op jit(solution)/shard_map/slice | solution.py:263
  96.9 5.3 %copy-start.13 = (f32[8,128,128]{2,1,0:T(8,128)S(1)}, f32[8,128,128]{2,1,0:T(8,128)}, u32[]{:S(2)}) copy-start(f32[8,128,128]{2,1,0:T(8,128)} %copy-done.12) | copy-start | bytes 1572868
  96.9 5.3 %copy-start.15 = (f32[8,128,128]{2,1,0:T(8,128)S(1)}, f32[8,128,128]{2,1,0:T(8,128)}, u32[]{:S(2)}) copy-start(f32[8,128,128]{2,1,0:T(8,128)} %copy-done.14) | copy-start | bytes 1572868
  100.4 5.4 %collective-permute-start.5 = (bf16[8,128,128]{2,1,0:T(8,128)(2,1)S(1)}, bf16[8,128,128]{2,1,0:T(8,128)(2,1)S(1)}, u32[]{:S(2)}, u32[]{:S(2)}) collective-permute-start(bf16[8,128,128]{2,1,0:T(8,128)(2,1)S(1)} %fusion.59), channel_id=1, source_target_pairs={{0,2},{2,4},{4,6},{6,8},{8,10},{10,12},{12,14},{14,16},{16,18},{18... | collective-permute-start | bytes 786440 | tf_op jit(solution)/shard_map/ppermute | solution.py:19
  106.7 1.0 copy-start.26
  107.3 2.2 copy-start.22
  109.5 2.8 copy-start.36
  109.5 4.8 %copy-start.25 = (bf16[128,2048]{1,0:T(8,128)(2,1)S(1)}, bf16[128,2048]{1,0:T(8,128)(2,1)}, u32[]{:S(2)}) copy-start(bf16[128,2048]{1,0:T(8,128)(2,1)} %param.26) | copy-start | bytes 1572868
  110.8 1.3 copy-start.11
  112.2 3.9 %copy-start.33 = (f32[2048]{0:T(1024)S(1)}, f32[2048]{0:T(1024)}, u32[]{:S(2)}) copy-start(f32[2048]{0:T(1024)} %param.27) | copy-start | bytes 24580
  112.2 2.1 collective-permute-start.6
  112.3 0.6 copy-start.31
  112.3 0.7 copy-start.29
  117.3 27.3 %collective-permute-start.11 = (bf16[128,2176]{1,0:T(8,128)(2,1)}, bf16[128,2176]{1,0:T(8,128)(2,1)}, u32[]{:S(2)}, u32[]{:S(2)}) collective-permute-start(bf16[128,2176]{1,0:T(8,128)(2,1)} %concatenate.31), channel_id=1, source_target_pairs={{0,8},{8,16},{16,24},{24,0},{1,9},{9,17},{17,25},{25,1},{2,10},{10... | collective-permute-start | bytes 1671176 | tf_op jit(solution)/shard_map/ppermute | solution.py:339
  128.1 4.7 %copy-start.27 = (s32[128,10]{0,1:T(8,128)}, s32[128,10]{0,1:T(8,128)S(1)}, u32[]{:S(2)}) copy-start(s32[128,10]{0,1:T(8,128)S(1)} %copy.161) | copy-start | bytes 15364
  132.8 28.2 %all-to-all-start = ((bf16[8,50,2048]{2,1,0:T(8,128)(2,1)}), bf16[8,50,2048]{2,1,0:T(8,128)(2,1)}, u32[]{:S(2)}, u32[]{:S(2)}) async-start(bf16[8,50,2048]{2,1,0:T(8,128)(2,1)} %reshape.262), calls=%async_computation | async-start | bytes 3670016 | tf_op jit(solution)/shard_map/all_to_all | solution.py:363
  137.1 31.1 %collective-permute-start.9 = (bf16[128,2176]{1,0:T(8,128)(2,1)}, bf16[128,2176]{1,0:T(8,128)(2,1)S(1)}, u32[]{:S(2)}, u32[]{:S(2)}) collective-permute-start(bf16[128,2176]{1,0:T(8,128)(2,1)} %concatenate.31), channel_id=1, source_target_pairs={{0,16},{8,24},{16,0},{24,8},{1,17},{9,25},{17,1},{25,9},{2,18},{10... | collective-permute-start | bytes 1671176 | tf_op jit(solution)/shard_map/ppermute | solution.py:339
  160.9 28.2 %all-to-all-start.6 = ((bf16[8,50,2048]{2,1,0:T(8,128)(2,1)}), bf16[8,50,2048]{2,1,0:T(8,128)(2,1)}, u32[]{:S(2)}, u32[]{:S(2)}) async-start(bf16[8,50,2048]{2,1,0:T(8,128)(2,1)} %reshape.268), calls=%async_computation.6 | async-start | bytes 3670016 | tf_op jit(solution)/shard_map/all_to_all | solution.py:363
  165.3 28.2 %collective-permute-start.7 = (bf16[128,2176]{1,0:T(8,128)(2,1)}, bf16[128,2176]{1,0:T(8,128)(2,1)}, u32[]{:S(2)}, u32[]{:S(2)}) collective-permute-start(bf16[128,2176]{1,0:T(8,128)(2,1)} %concatenate.31), channel_id=1, source_target_pairs={{0,24},{8,0},{16,8},{24,16},{1,25},{9,1},{17,9},{25,17},{2,26},{10... | collective-permute-start | bytes 1671176 | tf_op jit(solution)/shard_map/ppermute | solution.py:339
  189.1 28.2 %all-to-all-start.4 = ((bf16[8,50,2048]{2,1,0:T(8,128)(2,1)}), bf16[8,50,2048]{2,1,0:T(8,128)(2,1)}, u32[]{:S(2)}, u32[]{:S(2)}) async-start(bf16[8,50,2048]{2,1,0:T(8,128)(2,1)} %reshape.266), calls=%async_computation.4 | async-start | bytes 3670016 | tf_op jit(solution)/shard_map/all_to_all | solution.py:363
  217.3 28.6 %all-to-all-start.2 = ((bf16[8,50,2048]{2,1,0:T(8,128)(2,1)}), bf16[8,50,2048]{2,1,0:T(8,128)(2,1)}, u32[]{:S(2)}, u32[]{:S(2)}) async-start(bf16[8,50,2048]{2,1,0:T(8,128)(2,1)} %reshape.264), calls=%async_computation.2 | async-start | bytes 3670016 | tf_op jit(solution)/shard_map/all_to_all | solution.py:363
  245.9 28.2 %all-to-all-start.7 = ((bf16[8,50,2048]{2,1,0:T(8,128)(2,1)}), bf16[8,50,2048]{2,1,0:T(8,128)(2,1)}, u32[]{:S(2)}, u32[]{:S(2)}) async-start(bf16[8,50,2048]{2,1,0:T(8,128)(2,1)} %reshape_stack_reshape.15), calls=%async_computation.7 | async-start | bytes 3670016 | tf_op jit(solution)/shard_map/all_to_all | solution.py:374
  274.0 28.2 %all-to-all-start.5 = ((bf16[8,50,2048]{2,1,0:T(8,128)(2,1)}), bf16[8,50,2048]{2,1,0:T(8,128)(2,1)}, u32[]{:S(2)}, u32[]{:S(2)}) async-start(bf16[8,50,2048]{2,1,0:T(8,128)(2,1)} %reshape_stack_reshape.14), calls=%async_computation.5 | async-start | bytes 3670016 | tf_op jit(solution)/shard_map/all_to_all | solution.py:374
  302.2 28.4 %all-to-all-start.3 = ((bf16[8,50,2048]{2,1,0:T(8,128)(2,1)}), bf16[8,50,2048]{2,1,0:T(8,128)(2,1)}, u32[]{:S(2)}, u32[]{:S(2)}) async-start(bf16[8,50,2048]{2,1,0:T(8,128)(2,1)} %reshape_stack_reshape.13), calls=%async_computation.3 | async-start | bytes 3670016 | tf_op jit(solution)/shard_map/all_to_all | solution.py:374
  318.7 2.0 copy-start.6
  322.0 41.4 %collective-permute-start.12 = (bf16[128,2048]{1,0:T(8,128)(2,1)}, bf16[128,2048]{1,0:T(8,128)(2,1)S(1)}, u32[]{:S(2)}, u32[]{:S(2)}) collective-permute-start(bf16[128,2048]{1,0:T(8,128)(2,1)} %fusion.12), channel_id=1, source_target_pairs={{0,24},{8,0},{16,8},{24,16},{1,25},{9,1},{17,9},{25,17},{2,26},{10... | collective-permute-start | bytes 1572872 | tf_op jit(solution)/shard_map/ppermute | solution.py:388
  330.6 28.2 %all-to-all-start.1 = ((bf16[8,50,2048]{2,1,0:T(8,128)(2,1)}), bf16[8,50,2048]{2,1,0:T(8,128)(2,1)}, u32[]{:S(2)}, u32[]{:S(2)}) async-start(bf16[8,50,2048]{2,1,0:T(8,128)(2,1)} %reshape_stack_reshape.12), calls=%async_computation.1 | async-start | bytes 3670016 | tf_op jit(solution)/shard_map/all_to_all | solution.py:374
  334.9 2.0 copy-start.5
  338.3 38.1 %collective-permute-start.10 = (bf16[128,2048]{1,0:T(8,128)(2,1)}, bf16[128,2048]{1,0:T(8,128)(2,1)}, u32[]{:S(2)}, u32[]{:S(2)}) collective-permute-start(bf16[128,2048]{1,0:T(8,128)(2,1)} %fusion.11), channel_id=1, source_target_pairs={{0,16},{8,24},{16,0},{24,8},{1,17},{9,25},{17,1},{25,9},{2,18},{10... | collective-permute-start | bytes 1572872 | tf_op jit(solution)/shard_map/ppermute | solution.py:388
  344.3 2.1 copy-start.7
  346.3 1.3 copy-start.28
  346.3 1.3 copy-start.30
  346.3 1.3 copy-start.32
  347.6 28.7 %collective-permute-start.8 = (bf16[128,2048]{1,0:T(8,128)(2,1)}, bf16[128,2048]{1,0:T(8,128)(2,1)}, u32[]{:S(2)}, u32[]{:S(2)}) collective-permute-start(bf16[128,2048]{1,0:T(8,128)(2,1)} %fusion.10), channel_id=1, source_target_pairs={{0,8},{8,16},{16,24},{24,0},{1,9},{9,17},{17,25},{25,1},{2,10},{10... | collective-permute-start | bytes 1572872 | tf_op jit(solution)/shard_map/ppermute | solution.py:388
  361.4 15.0 %copy-start.4 = (bf16[400,2048]{1,0:T(8,128)(2,1)S(1)}, bf16[400,2048]{1,0:T(8,128)(2,1)}, u32[]{:S(2)}) copy-start(bf16[400,2048]{1,0:T(8,128)(2,1)} %reshape.263) | copy-start | bytes 4915204
